TPU v7x, 512 devices: a whole 4x4x16 slice. The times are simulated.
512 devices in a mesh: seq: 32 (over z, core), chan: 16 (over y, x).
Axes of the slice: x: 4, y: 4, z: 16, core: 2. Of those that a mesh axis runs over, the one named last changes fastest.
Arguments:
- features: bfloat16 [3, 65536, 4096], P(None, ('seq', 'chan')), may hold values from -6 to 6
- short_weight: float32 [3, 3, 4096], replicated, may hold values from -3.5 to 3.5
- decay_rate: float32 [16, 4096], P(None, 'chan'), as said below
- residue: float32 [16, 4096], P(None, 'chan'), may hold values from -1.5 to 1.5
- skip_gain: float32 [4096], P('chan'), may hold values from 0.5 to 1.5
Outputs:
- mixed: bfloat16 [65536, 4096], P(('seq', 'chan'))
Inputs may be any that keep to these rules, and one draw needn't show every extreme that they name: `decay_rate`: every rate is positive and at most 1/30.
All inputs are finite; a program needn't handle non-finite values.
Results may differ from a plain program's by a relative error of at most 0.0075.
Values may be sent and summed in bfloat16 or wider, within the bound.
No kernel may reach another device: no remote copies, remote signals or barrier semaphores. Data moves between devices by JAX's collectives and lax.ppermute only.
A program may use at most 64 MiB of HBM per device.

v0:
```python
import math

import jax
import jax.numpy as jnp
from jax import lax
from jax.sharding import PartitionSpec as P

block_len = 64


def from_behind(block, axis, distance):
    devices = range(lax.axis_size(axis))
    route = [(i - distance, i) for i in devices if i - distance in devices]
    return lax.ppermute(block, axis, route)


def short_filter(padded, weights, taps):
    length = padded.shape[1] - taps + 1
    total = jnp.zeros((padded.shape[0], length, padded.shape[2]), jnp.float32)
    for offset in range(taps):
        window = lax.slice_in_dim(
            padded, taps - 1 - offset, taps - 1 - offset + length, axis=1
        ).astype(jnp.float32)
        total = total + weights[:, offset, :][:, None, :] * window
    return total


def modal_tables(decay_rate, scaled_residue, block):
    positions = jnp.arange(block).astype(jnp.float32)
    kernel = jnp.sum(
        scaled_residue[:, None, :] * jnp.exp(-decay_rate[:, None, :] * positions[None, :, None]),
        axis=0,
    )
    lag_index = jnp.arange(block)[:, None] - jnp.arange(block)[None, :]
    one_hot = (lag_index[:, :, None] == jnp.arange(block)[None, None, :]).astype(jnp.float32)
    toeplitz = jnp.dot(
        one_hot.reshape(block * block, block), kernel, precision=lax.Precision.HIGHEST
    ).reshape(block, block, kernel.shape[1])
    ending = jnp.exp(-decay_rate[:, None, :] * (block - 1.0 - positions)[None, :, None])
    reading = scaled_residue[:, None, :] * jnp.exp(
        -decay_rate[:, None, :] * (positions + 1.0)[None, :, None]
    )
    return (toeplitz, ending, reading)


def modal_conv(signal, decay_rate, tables, start_state, block):
    toeplitz, ending, reading = tables
    count = signal.shape[0] // block
    pieces = signal.reshape(count, block, signal.shape[1])
    inner = jnp.einsum("ijc,kjc->kic", toeplitz, pieces, precision=lax.Precision.HIGHEST)
    local_end = jnp.einsum("njc,kjc->knc", ending, pieces, precision=lax.Precision.HIGHEST)
    group_decay = jnp.exp(-decay_rate * block)

    def advance(state, piece):
        return (group_decay * state + piece, state)

    final, starts = lax.scan(advance, start_state, local_end)
    carried = jnp.einsum("nic,knc->kic", reading, starts, precision=lax.Precision.HIGHEST)
    return ((inner + carried).reshape(signal.shape), final)


def long_part(product, decay_rate, residue, skip_gain):
    signal = product.astype(jnp.float32)
    section = signal.shape[0]
    block = math.gcd(section, block_len)
    count = section // block
    scaled = residue * jnp.sqrt(1.0 - jnp.exp(-2.0 * decay_rate))
    tables = modal_tables(decay_rate, scaled, block)
    zero_state = jnp.zeros_like(decay_rate)
    longconv, end_state = modal_conv(signal, decay_rate, tables, zero_state, block)
    section_decay = jnp.exp(-decay_rate * section)

    def advance_section(turn_index, carry_state):
        return from_behind(section_decay * carry_state + end_state, "seq", 1)

    incoming = lax.fori_loop(0, lax.axis_size("seq") - 1, advance_section, zero_state)
    block_starts = (jnp.arange(count).astype(jnp.float32) * block)[:, None, None]
    entering = jnp.exp(-decay_rate[None, :, :] * block_starts) * incoming[None, :, :]
    correction = jnp.einsum(
        "nic,knc->kic", tables[2], entering, precision=lax.Precision.HIGHEST
    ).reshape(signal.shape)
    return (longconv + correction + skip_gain[None, :] * signal).astype(jnp.bfloat16)


def local(features, short_weight, decay_rate, residue, skip_gain):
    taps = short_weight.shape[1]
    chan_width = decay_rate.shape[1]
    columns = lax.all_to_all(features, "chan", split_axis=2, concat_axis=1, tiled=True)
    border = from_behind(columns[:, columns.shape[1] - (taps - 1) :, :], "seq", 1)
    weights = lax.dynamic_slice_in_dim(
        short_weight, lax.axis_index("chan") * chan_width, chan_width, 2
    )
    padded = jnp.concatenate([border, columns], axis=1)
    filtered = lax.optimization_barrier(short_filter(padded, weights, taps).astype(jnp.bfloat16))
    product = lax.optimization_barrier(
        (filtered[1].astype(jnp.float32) * filtered[2].astype(jnp.float32)).astype(jnp.bfloat16)
    )
    conv_out = lax.optimization_barrier(long_part(product, decay_rate, residue, skip_gain))
    gated = (filtered[0].astype(jnp.float32) * conv_out.astype(jnp.float32)).astype(jnp.bfloat16)
    return lax.all_to_all(gated, "chan", split_axis=0, concat_axis=1, tiled=True)


def solution(mesh):
    return jax.shard_map(
        local,
        mesh=mesh,
        in_specs=(P(None, ("seq", "chan"), None), P(), P(None, "chan"), P(None, "chan"), P("chan")),
        out_specs=P(("seq", "chan"), None),
        check_vma=False,
    )
```

profile of v0, /device:TPU:384, one launch (start us, length us, event | category | flops | bytes accessed | tf_op | source)
XLA Modules:
  0.0 380.7 jit_solution(5982548783155374658)
XLA Ops:
  0.0 7.2 %copy.25 = bf16[3,128,4096]{1,0,2:T(4,128)(2,1)} copy(bf16[3,128,4096]{2,1,0:T(8,128)(2,1)} %param.9) | data formatting | bytes 6291456 | tf_op args[0]
  7.2 7.2 %all-to-all-start = ((bf16[3,128,4096]{1,0,2:T(4,128)(2,1)}), bf16[3,128,4096]{1,0,2:T(4,128)(2,1)}, u32[]{:S(2)}, u32[]{:S(2)}) async-start(bf16[3,128,4096]{1,0,2:T(4,128)(2,1)} %copy.25), calls=%async_computation | async-start | bytes 8388608 | tf_op jit(solution)/shard_map/all_to_all | solution.py:88
  17.4 3.8 %fusion.10 = f32[64,64,256]{2,1,0:T(8,128)} fusion(s32[64,64]{1,0:T(8,128)S(1)} %iota_subtract_fusion, f32[64,256]{0,1:T(8,128)S(1)} %multiply_reduce_fusion), kind=kOutput, calls=%fused_computation.24 | convolution fusion | flops 805568512 | bytes 4276224 | tf_op jit(solution)/shard_map/dot_general | solution.py:36
  21.2 56.6 %all-to-all-done = bf16[3,128,4096]{1,0,2:T(4,128)(2,1)} async-done(((bf16[3,128,4096]{1,0,2:T(4,128)(2,1)}), bf16[3,128,4096]{1,0,2:T(4,128)(2,1)}, u32[]{:S(2)}, u32[]{:S(2)}) %all-to-all-start) | async-done | bytes 3145760 | tf_op jit(solution)/shard_map/all_to_all | solution.py:88
  77.8 5.5 %copy.26 = bf16[3,128,16,256]{3,1,2,0:T(8,128)(2,1)S(1)} copy(bf16[3,128,16,256]{1,0,3,2:T(4,128)(2,1)} %bitcast) | data formatting | bytes 6291456 | tf_op jit(solution)/shard_map/all_to_all | solution.py:88
  85.4 9.2 %copy.31 = f32[64,64,256]{1,0,2:T(8,128)} copy(f32[64,64,256]{2,1,0:T(8,128)} %fusion.10) | data formatting | bytes 8388608 | tf_op jit(solution)/shard_map/dot_general | solution.py:36
  98.7 3.1 copy.30
  101.8 10.3 %fusion.28 = f32[256,32,64]{2,1,0:T(8,128)} fusion(bf16[32,64,256]{1,0,2:T(8,128)(2,1)S(1)} %copy.30, f32[64,64,256]{1,0,2:T(8,128)} %copy.31), kind=kOutput, calls=%fused_computation.55 | convolution fusion | flops 402653184 | bytes 7340032 | tf_op jit(solution)/shard_map/ijc,kjc->kic/dot_general | solution.py:50
  112.1 4.8 %fusion.11 = f32[32,16,256]{0,1,2:T(8,128)} fusion(bf16[32,64,256]{1,0,2:T(8,128)(2,1)S(1)} %copy.30, f32[64]{0:T(128)S(1)} %broadcast_subtract_fusion, f32[16,256]{0,1:T(8,128)S(1)} %copy.28), kind=kOutput, calls=%fused_computation.25 | convolution fusion | flops 100925440 | bytes 1589504 | tf_op jit(solution)/shard_map/njc,kjc->knc/dot_general | solution.py:51
  116.8 2.7 copy.33
  119.5 19.8 %while.24 = (s32[]{:T(128)}, f32[16,256]{1,0:T(8,128)S(1)}, f32[32,16,256]{2,1,0:T(8,128)}, f32[16,256]{1,0:T(8,128)S(1)}, f32[32,16,256]{2,1,0:T(8,128)S(1)}, /*index=5*/s32[]{:T(128)}, s32[]{:T(128)}) while((s32[]{:T(128)}, f32[16,256]{1,0:T(8,128)S(1)}, f32[32,16,256]{2,1,0:T(8,128)}, f32[16,256]{1,0:T(8,128)S(1)}, ...), condition=%wide.region_2.3_spmd.clone, body=%wide.region_1.2_spmd.clone.sunk | while | flops 16387 | bytes 98908 | solution.py:57
  141.7 194.2 %while.23 = (s32[]{:T(128)}, f32[16,256]{1,0:T(8,128)S(1)}, f32[16,256]{1,0:T(8,128)S(1)}, f32[16,256]{1,0:T(8,128)S(1)}, s32[]{:T(128)}) while((s32[]{:T(128)}, f32[16,256]{1,0:T(8,128)S(1)}, f32[16,256]{1,0:T(8,128)S(1)}, f32[16,256]{1,0:T(8,128)S(1)}, s32[]{:T(128)}) %tuple.47), condition=%wide.region_4.5_spmd, body=%wide.region_3.4_spmd.sunk | while | flops 8194 | bytes 131173 | solution.py:76
  141.7 3.0 collective-permute-start
  144.8 3.2 collective-permute-done
  149.9 4.3 %collective-permute-done = f32[16,256]{1,0:T(8,128)S(1)} collective-permute-done((f32[16,256]{1,0:T(8,128)S(1)}, f32[16,256]{1,0:T(8,128)S(1)}, u32[]{:S(2)}, u32[]{:S(2)}) %collective-permute-start) | collective-permute-done | bytes 16416 | tf_op jit(solution)/shard_map/while/body/eval_jaxpr/ppermute | solution.py:14
  156.2 4.3 %collective-permute-done = f32[16,256]{1,0:T(8,128)S(1)} collective-permute-done((f32[16,256]{1,0:T(8,128)S(1)}, f32[16,256]{1,0:T(8,128)S(1)}, u32[]{:S(2)}, u32[]{:S(2)}) %collective-permute-start) | collective-permute-done | bytes 16416 | tf_op jit(solution)/shard_map/while/body/eval_jaxpr/ppermute | solution.py:14
  162.5 4.3 %collective-permute-done = f32[16,256]{1,0:T(8,128)S(1)} collective-permute-done((f32[16,256]{1,0:T(8,128)S(1)}, f32[16,256]{1,0:T(8,128)S(1)}, u32[]{:S(2)}, u32[]{:S(2)}) %collective-permute-start) | collective-permute-done | bytes 16416 | tf_op jit(solution)/shard_map/while/body/eval_jaxpr/ppermute | solution.py:14
  168.7 4.3 %collective-permute-done = f32[16,256]{1,0:T(8,128)S(1)} collective-permute-done((f32[16,256]{1,0:T(8,128)S(1)}, f32[16,256]{1,0:T(8,128)S(1)}, u32[]{:S(2)}, u32[]{:S(2)}) %collective-permute-start) | collective-permute-done | bytes 16416 | tf_op jit(solution)/shard_map/while/body/eval_jaxpr/ppermute | solution.py:14
  175.0 4.3 %collective-permute-done = f32[16,256]{1,0:T(8,128)S(1)} collective-permute-done((f32[16,256]{1,0:T(8,128)S(1)}, f32[16,256]{1,0:T(8,128)S(1)}, u32[]{:S(2)}, u32[]{:S(2)}) %collective-permute-start) | collective-permute-done | bytes 16416 | tf_op jit(solution)/shard_map/while/body/eval_jaxpr/ppermute | solution.py:14
  181.3 4.3 %collective-permute-done = f32[16,256]{1,0:T(8,128)S(1)} collective-permute-done((f32[16,256]{1,0:T(8,128)S(1)}, f32[16,256]{1,0:T(8,128)S(1)}, u32[]{:S(2)}, u32[]{:S(2)}) %collective-permute-start) | collective-permute-done | bytes 16416 | tf_op jit(solution)/shard_map/while/body/eval_jaxpr/ppermute | solution.py:14
  187.5 4.3 %collective-permute-done = f32[16,256]{1,0:T(8,128)S(1)} collective-permute-done((f32[16,256]{1,0:T(8,128)S(1)}, f32[16,256]{1,0:T(8,128)S(1)}, u32[]{:S(2)}, u32[]{:S(2)}) %collective-permute-start) | collective-permute-done | bytes 16416 | tf_op jit(solution)/shard_map/while/body/eval_jaxpr/ppermute | solution.py:14
  193.8 4.3 %collective-permute-done = f32[16,256]{1,0:T(8,128)S(1)} collective-permute-done((f32[16,256]{1,0:T(8,128)S(1)}, f32[16,256]{1,0:T(8,128)S(1)}, u32[]{:S(2)}, u32[]{:S(2)}) %collective-permute-start) | collective-permute-done | bytes 16416 | tf_op jit(solution)/shard_map/while/body/eval_jaxpr/ppermute | solution.py:14
  200.1 4.3 %collective-permute-done = f32[16,256]{1,0:T(8,128)S(1)} collective-permute-done((f32[16,256]{1,0:T(8,128)S(1)}, f32[16,256]{1,0:T(8,128)S(1)}, u32[]{:S(2)}, u32[]{:S(2)}) %collective-permute-start) | collective-permute-done | bytes 16416 | tf_op jit(solution)/shard_map/while/body/eval_jaxpr/ppermute | solution.py:14
  206.3 4.3 %collective-permute-done = f32[16,256]{1,0:T(8,128)S(1)} collective-permute-done((f32[16,256]{1,0:T(8,128)S(1)}, f32[16,256]{1,0:T(8,128)S(1)}, u32[]{:S(2)}, u32[]{:S(2)}) %collective-permute-start) | collective-permute-done | bytes 16416 | tf_op jit(solution)/shard_map/while/body/eval_jaxpr/ppermute | solution.py:14
  212.6 4.3 %collective-permute-done = f32[16,256]{1,0:T(8,128)S(1)} collective-permute-done((f32[16,256]{1,0:T(8,128)S(1)}, f32[16,256]{1,0:T(8,128)S(1)}, u32[]{:S(2)}, u32[]{:S(2)}) %collective-permute-start) | collective-permute-done | bytes 16416 | tf_op jit(solution)/shard_map/while/body/eval_jaxpr/ppermute | solution.py:14
  218.8 4.3 %collective-permute-done = f32[16,256]{1,0:T(8,128)S(1)} collective-permute-done((f32[16,256]{1,0:T(8,128)S(1)}, f32[16,256]{1,0:T(8,128)S(1)}, u32[]{:S(2)}, u32[]{:S(2)}) %collective-permute-start) | collective-permute-done | bytes 16416 | tf_op jit(solution)/shard_map/while/body/eval_jaxpr/ppermute | solution.py:14
  225.1 4.3 %collective-permute-done = f32[16,256]{1,0:T(8,128)S(1)} collective-permute-done((f32[16,256]{1,0:T(8,128)S(1)}, f32[16,256]{1,0:T(8,128)S(1)}, u32[]{:S(2)}, u32[]{:S(2)}) %collective-permute-start) | collective-permute-done | bytes 16416 | tf_op jit(solution)/shard_map/while/body/eval_jaxpr/ppermute | solution.py:14
  231.4 4.3 %collective-permute-done = f32[16,256]{1,0:T(8,128)S(1)} collective-permute-done((f32[16,256]{1,0:T(8,128)S(1)}, f32[16,256]{1,0:T(8,128)S(1)}, u32[]{:S(2)}, u32[]{:S(2)}) %collective-permute-start) | collective-permute-done | bytes 16416 | tf_op jit(solution)/shard_map/while/body/eval_jaxpr/ppermute | solution.py:14
  237.6 4.3 %collective-permute-done = f32[16,256]{1,0:T(8,128)S(1)} collective-permute-done((f32[16,256]{1,0:T(8,128)S(1)}, f32[16,256]{1,0:T(8,128)S(1)}, u32[]{:S(2)}, u32[]{:S(2)}) %collective-permute-start) | collective-permute-done | bytes 16416 | tf_op jit(solution)/shard_map/while/body/eval_jaxpr/ppermute | solution.py:14
  243.9 4.3 %collective-permute-done = f32[16,256]{1,0:T(8,128)S(1)} collective-permute-done((f32[16,256]{1,0:T(8,128)S(1)}, f32[16,256]{1,0:T(8,128)S(1)}, u32[]{:S(2)}, u32[]{:S(2)}) %collective-permute-start) | collective-permute-done | bytes 16416 | tf_op jit(solution)/shard_map/while/body/eval_jaxpr/ppermute | solution.py:14
  250.2 4.3 %collective-permute-done = f32[16,256]{1,0:T(8,128)S(1)} collective-permute-done((f32[16,256]{1,0:T(8,128)S(1)}, f32[16,256]{1,0:T(8,128)S(1)}, u32[]{:S(2)}, u32[]{:S(2)}) %collective-permute-start) | collective-permute-done | bytes 16416 | tf_op jit(solution)/shard_map/while/body/eval_jaxpr/ppermute | solution.py:14
  256.4 4.3 %collective-permute-done = f32[16,256]{1,0:T(8,128)S(1)} collective-permute-done((f32[16,256]{1,0:T(8,128)S(1)}, f32[16,256]{1,0:T(8,128)S(1)}, u32[]{:S(2)}, u32[]{:S(2)}) %collective-permute-start) | collective-permute-done | bytes 16416 | tf_op jit(solution)/shard_map/while/body/eval_jaxpr/ppermute | solution.py:14
  262.7 4.3 %collective-permute-done = f32[16,256]{1,0:T(8,128)S(1)} collective-permute-done((f32[16,256]{1,0:T(8,128)S(1)}, f32[16,256]{1,0:T(8,128)S(1)}, u32[]{:S(2)}, u32[]{:S(2)}) %collective-permute-start) | collective-permute-done | bytes 16416 | tf_op jit(solution)/shard_map/while/body/eval_jaxpr/ppermute | solution.py:14
  269.0 4.3 %collective-permute-done = f32[16,256]{1,0:T(8,128)S(1)} collective-permute-done((f32[16,256]{1,0:T(8,128)S(1)}, f32[16,256]{1,0:T(8,128)S(1)}, u32[]{:S(2)}, u32[]{:S(2)}) %collective-permute-start) | collective-permute-done | bytes 16416 | tf_op jit(solution)/shard_map/while/body/eval_jaxpr/ppermute | solution.py:14
  275.2 4.3 %collective-permute-done = f32[16,256]{1,0:T(8,128)S(1)} collective-permute-done((f32[16,256]{1,0:T(8,128)S(1)}, f32[16,256]{1,0:T(8,128)S(1)}, u32[]{:S(2)}, u32[]{:S(2)}) %collective-permute-start) | collective-permute-done | bytes 16416 | tf_op jit(solution)/shard_map/while/body/eval_jaxpr/ppermute | solution.py:14
  281.5 4.3 %collective-permute-done = f32[16,256]{1,0:T(8,128)S(1)} collective-permute-done((f32[16,256]{1,0:T(8,128)S(1)}, f32[16,256]{1,0:T(8,128)S(1)}, u32[]{:S(2)}, u32[]{:S(2)}) %collective-permute-start) | collective-permute-done | bytes 16416 | tf_op jit(solution)/shard_map/while/body/eval_jaxpr/ppermute | solution.py:14
  287.7 4.3 %collective-permute-done = f32[16,256]{1,0:T(8,128)S(1)} collective-permute-done((f32[16,256]{1,0:T(8,128)S(1)}, f32[16,256]{1,0:T(8,128)S(1)}, u32[]{:S(2)}, u32[]{:S(2)}) %collective-permute-start) | collective-permute-done | bytes 16416 | tf_op jit(solution)/shard_map/while/body/eval_jaxpr/ppermute | solution.py:14
  294.0 4.3 %collective-permute-done = f32[16,256]{1,0:T(8,128)S(1)} collective-permute-done((f32[16,256]{1,0:T(8,128)S(1)}, f32[16,256]{1,0:T(8,128)S(1)}, u32[]{:S(2)}, u32[]{:S(2)}) %collective-permute-start) | collective-permute-done | bytes 16416 | tf_op jit(solution)/shard_map/while/body/eval_jaxpr/ppermute | solution.py:14
  300.3 4.3 %collective-permute-done = f32[16,256]{1,0:T(8,128)S(1)} collective-permute-done((f32[16,256]{1,0:T(8,128)S(1)}, f32[16,256]{1,0:T(8,128)S(1)}, u32[]{:S(2)}, u32[]{:S(2)}) %collective-permute-start) | collective-permute-done | bytes 16416 | tf_op jit(solution)/shard_map/while/body/eval_jaxpr/ppermute | solution.py:14
  306.5 4.3 %collective-permute-done = f32[16,256]{1,0:T(8,128)S(1)} collective-permute-done((f32[16,256]{1,0:T(8,128)S(1)}, f32[16,256]{1,0:T(8,128)S(1)}, u32[]{:S(2)}, u32[]{:S(2)}) %collective-permute-start) | collective-permute-done | bytes 16416 | tf_op jit(solution)/shard_map/while/body/eval_jaxpr/ppermute | solution.py:14
  312.8 4.3 %collective-permute-done = f32[16,256]{1,0:T(8,128)S(1)} collective-permute-done((f32[16,256]{1,0:T(8,128)S(1)}, f32[16,256]{1,0:T(8,128)S(1)}, u32[]{:S(2)}, u32[]{:S(2)}) %collective-permute-start) | collective-permute-done | bytes 16416 | tf_op jit(solution)/shard_map/while/body/eval_jaxpr/ppermute | solution.py:14
  319.1 4.3 %collective-permute-done = f32[16,256]{1,0:T(8,128)S(1)} collective-permute-done((f32[16,256]{1,0:T(8,128)S(1)}, f32[16,256]{1,0:T(8,128)S(1)}, u32[]{:S(2)}, u32[]{:S(2)}) %collective-permute-start) | collective-permute-done | bytes 16416 | tf_op jit(solution)/shard_map/while/body/eval_jaxpr/ppermute | solution.py:14
  325.3 4.3 %collective-permute-done = f32[16,256]{1,0:T(8,128)S(1)} collective-permute-done((f32[16,256]{1,0:T(8,128)S(1)}, f32[16,256]{1,0:T(8,128)S(1)}, u32[]{:S(2)}, u32[]{:S(2)}) %collective-permute-start) | collective-permute-done | bytes 16416 | tf_op jit(solution)/shard_map/while/body/eval_jaxpr/ppermute | solution.py:14
  331.6 4.3 %collective-permute-done = f32[16,256]{1,0:T(8,128)S(1)} collective-permute-done((f32[16,256]{1,0:T(8,128)S(1)}, f32[16,256]{1,0:T(8,128)S(1)}, u32[]{:S(2)}, u32[]{:S(2)}) %collective-permute-start) | collective-permute-done | bytes 16416 | tf_op jit(solution)/shard_map/while/body/eval_jaxpr/ppermute | solution.py:14
  336.7 7.9 %fusion.6 = f32[256,32,64]{2,1,0:T(8,128)S(1)} fusion(f32[32,16,256]{0,1,2:T(8,128)S(1)} %copy.34, f32[64]{0:T(128)S(1)} %broadcast_add_fusion, f32[16,256]{0,1:T(8,128)S(1)} %copy.28, f32[16,256]{0,1:T(8,128)S(1)} %copy.27), kind=kOutput, calls=%fused_computation.17 | convolution fusion | flops 101187584 | bytes 2654464 | tf_op jit(solution)/shard_map/nic,knc->kic/dot_general | solution.py:58
  344.7 10.9 %add_bitcast_fusion = f32[32,64,256]{1,0,2:T(8,128)} fusion(f32[256,32,64]{2,1,0:T(8,128)S(1)} %copy-done, f32[256,32,64]{2,1,0:T(8,128)S(1)} %fusion.6, f32[16,256]{0,1:T(8,128)S(1)} %copy-done.2, f32[32]{0:T(128)S(1)} %convert_multiply_fusion.1, f32[16,256]{0,1:T(8,128)S(1)} %copy.28, f32[64]{0:T(128)S(1)} %broadcast_add_fusion, f32[16,256]{0,1:T(8,128)S(1)} %copy.27), kind=kOutput, calls=%fused_computation.4 | convolution fusion | flops 102498304 | bytes 6340992 | tf_op jit(solution)/shard_map/nic,knc->kic/dot_general | solution.py:79
  355.5 3.6 copy.37
  360.9 18.7 %all_to_all.37 = bf16[16,128,256]{2,1,0:T(8,128)(2,1)S(1)} all-to-all(bf16[16,128,256]{2,1,0:T(8,128)(2,1)S(1)} %bitcast.49), channel_id=1, replica_groups=mesh['seq'=32,'chan'=16] {'chan'}, dimensions={0} | all-to-all | bytes 2097152 | tf_op jit(solution)/shard_map/all_to_all | solution.py:100
  (162 shorter events, 92.3 us)
Async XLA Ops:
  7.2 7.2 %copy-start.3 = (f32[16,256]{1,0:T(8,128)S(1)}, f32[16,256]{1,0:T(8,128)}, u32[]{:S(2)}) copy-start(f32[16,256]{1,0:T(8,128)} %param.11) | copy-start | bytes 49156
  7.2 7.2 %copy-start.4 = (f32[16,256]{1,0:T(8,128)S(1)}, f32[16,256]{1,0:T(8,128)}, u32[]{:S(2)}) copy-start(f32[16,256]{1,0:T(8,128)} %param.12) | copy-start | bytes 49156
  7.2 70.5 %all-to-all-start = ((bf16[3,128,4096]{1,0,2:T(4,128)(2,1)}), bf16[3,128,4096]{1,0,2:T(4,128)(2,1)}, u32[]{:S(2)}, u32[]{:S(2)}) async-start(bf16[3,128,4096]{1,0,2:T(4,128)(2,1)} %copy.25), calls=%async_computation | async-start | bytes 8388608 | tf_op jit(solution)/shard_map/all_to_all | solution.py:88
  83.3 11.3 %collective-permute-start.1 = (bf16[3,2,256]{2,1,0:T(2,128)(2,1)S(1)}, bf16[3,2,256]{2,1,0:T(2,128)(2,1)S(1)}, u32[]{:S(2)}, u32[]{:S(2)}) collective-permute-start(bf16[3,2,256]{2,1,0:T(2,128)(2,1)S(1)} %slice.36), channel_id=1, source_target_pairs={{0,16},{16,32},{32,48},{48,64},{64,80},{80,96},{96,112},{112,128},... | collective-permute-start | bytes 9224 | tf_op jit(solution)/shard_map/ppermute | solution.py:14
  97.1 1.6 copy-start.1
  141.7 6.3 %collective-permute-start = (f32[16,256]{1,0:T(8,128)S(1)}, f32[16,256]{1,0:T(8,128)S(1)}, u32[]{:S(2)}, u32[]{:S(2)}) collective-permute-start(f32[16,256]{1,0:T(8,128)S(1)} %multiply_add_fusion.2), channel_id=1, source_target_pairs={{0,16},{16,32},{32,48},{48,64},{64,80},{80,96},{96,112},{112,128},... | collective-permute-start | bytes 49160 | tf_op jit(solution)/shard_map/while/body/eval_jaxpr/ppermute | solution.py:14
  148.0 6.3 %collective-permute-start = (f32[16,256]{1,0:T(8,128)S(1)}, f32[16,256]{1,0:T(8,128)S(1)}, u32[]{:S(2)}, u32[]{:S(2)}) collective-permute-start(f32[16,256]{1,0:T(8,128)S(1)} %multiply_add_fusion.2), channel_id=1, source_target_pairs={{0,16},{16,32},{32,48},{48,64},{64,80},{80,96},{96,112},{112,128},... | collective-permute-start | bytes 49160 | tf_op jit(solution)/shard_map/while/body/eval_jaxpr/ppermute | solution.py:14
  154.3 6.3 %collective-permute-start = (f32[16,256]{1,0:T(8,128)S(1)}, f32[16,256]{1,0:T(8,128)S(1)}, u32[]{:S(2)}, u32[]{:S(2)}) collective-permute-start(f32[16,256]{1,0:T(8,128)S(1)} %multiply_add_fusion.2), channel_id=1, source_target_pairs={{0,16},{16,32},{32,48},{48,64},{64,80},{80,96},{96,112},{112,128},... | collective-permute-start | bytes 49160 | tf_op jit(solution)/shard_map/while/body/eval_jaxpr/ppermute | solution.py:14
  160.6 6.3 %collective-permute-start = (f32[16,256]{1,0:T(8,128)S(1)}, f32[16,256]{1,0:T(8,128)S(1)}, u32[]{:S(2)}, u32[]{:S(2)}) collective-permute-start(f32[16,256]{1,0:T(8,128)S(1)} %multiply_add_fusion.2), channel_id=1, source_target_pairs={{0,16},{16,32},{32,48},{48,64},{64,80},{80,96},{96,112},{112,128},... | collective-permute-start | bytes 49160 | tf_op jit(solution)/shard_map/while/body/eval_jaxpr/ppermute | solution.py:14
  166.8 6.3 %collective-permute-start = (f32[16,256]{1,0:T(8,128)S(1)}, f32[16,256]{1,0:T(8,128)S(1)}, u32[]{:S(2)}, u32[]{:S(2)}) collective-permute-start(f32[16,256]{1,0:T(8,128)S(1)} %multiply_add_fusion.2), channel_id=1, source_target_pairs={{0,16},{16,32},{32,48},{48,64},{64,80},{80,96},{96,112},{112,128},... | collective-permute-start | bytes 49160 | tf_op jit(solution)/shard_map/while/body/eval_jaxpr/ppermute | solution.py:14
  173.1 6.3 %collective-permute-start = (f32[16,256]{1,0:T(8,128)S(1)}, f32[16,256]{1,0:T(8,128)S(1)}, u32[]{:S(2)}, u32[]{:S(2)}) collective-permute-start(f32[16,256]{1,0:T(8,128)S(1)} %multiply_add_fusion.2), channel_id=1, source_target_pairs={{0,16},{16,32},{32,48},{48,64},{64,80},{80,96},{96,112},{112,128},... | collective-permute-start | bytes 49160 | tf_op jit(solution)/shard_map/while/body/eval_jaxpr/ppermute | solution.py:14
  179.3 6.3 %collective-permute-start = (f32[16,256]{1,0:T(8,128)S(1)}, f32[16,256]{1,0:T(8,128)S(1)}, u32[]{:S(2)}, u32[]{:S(2)}) collective-permute-start(f32[16,256]{1,0:T(8,128)S(1)} %multiply_add_fusion.2), channel_id=1, source_target_pairs={{0,16},{16,32},{32,48},{48,64},{64,80},{80,96},{96,112},{112,128},... | collective-permute-start | bytes 49160 | tf_op jit(solution)/shard_map/while/body/eval_jaxpr/ppermute | solution.py:14
  185.6 6.3 %collective-permute-start = (f32[16,256]{1,0:T(8,128)S(1)}, f32[16,256]{1,0:T(8,128)S(1)}, u32[]{:S(2)}, u32[]{:S(2)}) collective-permute-start(f32[16,256]{1,0:T(8,128)S(1)} %multiply_add_fusion.2), channel_id=1, source_target_pairs={{0,16},{16,32},{32,48},{48,64},{64,80},{80,96},{96,112},{112,128},... | collective-permute-start | bytes 49160 | tf_op jit(solution)/shard_map/while/body/eval_jaxpr/ppermute | solution.py:14
  191.9 6.3 %collective-permute-start = (f32[16,256]{1,0:T(8,128)S(1)}, f32[16,256]{1,0:T(8,128)S(1)}, u32[]{:S(2)}, u32[]{:S(2)}) collective-permute-start(f32[16,256]{1,0:T(8,128)S(1)} %multiply_add_fusion.2), channel_id=1, source_target_pairs={{0,16},{16,32},{32,48},{48,64},{64,80},{80,96},{96,112},{112,128},... | collective-permute-start | bytes 49160 | tf_op jit(solution)/shard_map/while/body/eval_jaxpr/ppermute | solution.py:14
  198.1 6.3 %collective-permute-start = (f32[16,256]{1,0:T(8,128)S(1)}, f32[16,256]{1,0:T(8,128)S(1)}, u32[]{:S(2)}, u32[]{:S(2)}) collective-permute-start(f32[16,256]{1,0:T(8,128)S(1)} %multiply_add_fusion.2), channel_id=1, source_target_pairs={{0,16},{16,32},{32,48},{48,64},{64,80},{80,96},{96,112},{112,128},... | collective-permute-start | bytes 49160 | tf_op jit(solution)/shard_map/while/body/eval_jaxpr/ppermute | solution.py:14
  204.4 6.3 %collective-permute-start = (f32[16,256]{1,0:T(8,128)S(1)}, f32[16,256]{1,0:T(8,128)S(1)}, u32[]{:S(2)}, u32[]{:S(2)}) collective-permute-start(f32[16,256]{1,0:T(8,128)S(1)} %multiply_add_fusion.2), channel_id=1, source_target_pairs={{0,16},{16,32},{32,48},{48,64},{64,80},{80,96},{96,112},{112,128},... | collective-permute-start | bytes 49160 | tf_op jit(solution)/shard_map/while/body/eval_jaxpr/ppermute | solution.py:14
  210.7 6.3 %collective-permute-start = (f32[16,256]{1,0:T(8,128)S(1)}, f32[16,256]{1,0:T(8,128)S(1)}, u32[]{:S(2)}, u32[]{:S(2)}) collective-permute-start(f32[16,256]{1,0:T(8,128)S(1)} %multiply_add_fusion.2), channel_id=1, source_target_pairs={{0,16},{16,32},{32,48},{48,64},{64,80},{80,96},{96,112},{112,128},... | collective-permute-start | bytes 49160 | tf_op jit(solution)/shard_map/while/body/eval_jaxpr/ppermute | solution.py:14
  216.9 6.3 %collective-permute-start = (f32[16,256]{1,0:T(8,128)S(1)}, f32[16,256]{1,0:T(8,128)S(1)}, u32[]{:S(2)}, u32[]{:S(2)}) collective-permute-start(f32[16,256]{1,0:T(8,128)S(1)} %multiply_add_fusion.2), channel_id=1, source_target_pairs={{0,16},{16,32},{32,48},{48,64},{64,80},{80,96},{96,112},{112,128},... | collective-permute-start | bytes 49160 | tf_op jit(solution)/shard_map/while/body/eval_jaxpr/ppermute | solution.py:14
  223.2 6.3 %collective-permute-start = (f32[16,256]{1,0:T(8,128)S(1)}, f32[16,256]{1,0:T(8,128)S(1)}, u32[]{:S(2)}, u32[]{:S(2)}) collective-permute-start(f32[16,256]{1,0:T(8,128)S(1)} %multiply_add_fusion.2), channel_id=1, source_target_pairs={{0,16},{16,32},{32,48},{48,64},{64,80},{80,96},{96,112},{112,128},... | collective-permute-start | bytes 49160 | tf_op jit(solution)/shard_map/while/body/eval_jaxpr/ppermute | solution.py:14
  229.5 6.3 %collective-permute-start = (f32[16,256]{1,0:T(8,128)S(1)}, f32[16,256]{1,0:T(8,128)S(1)}, u32[]{:S(2)}, u32[]{:S(2)}) collective-permute-start(f32[16,256]{1,0:T(8,128)S(1)} %multiply_add_fusion.2), channel_id=1, source_target_pairs={{0,16},{16,32},{32,48},{48,64},{64,80},{80,96},{96,112},{112,128},... | collective-permute-start | bytes 49160 | tf_op jit(solution)/shard_map/while/body/eval_jaxpr/ppermute | solution.py:14
  235.7 6.3 %collective-permute-start = (f32[16,256]{1,0:T(8,128)S(1)}, f32[16,256]{1,0:T(8,128)S(1)}, u32[]{:S(2)}, u32[]{:S(2)}) collective-permute-start(f32[16,256]{1,0:T(8,128)S(1)} %multiply_add_fusion.2), channel_id=1, source_target_pairs={{0,16},{16,32},{32,48},{48,64},{64,80},{80,96},{96,112},{112,128},... | collective-permute-start | bytes 49160 | tf_op jit(solution)/shard_map/while/body/eval_jaxpr/ppermute | solution.py:14
  242.0 6.3 %collective-permute-start = (f32[16,256]{1,0:T(8,128)S(1)}, f32[16,256]{1,0:T(8,128)S(1)}, u32[]{:S(2)}, u32[]{:S(2)}) collective-permute-start(f32[16,256]{1,0:T(8,128)S(1)} %multiply_add_fusion.2), channel_id=1, source_target_pairs={{0,16},{16,32},{32,48},{48,64},{64,80},{80,96},{96,112},{112,128},... | collective-permute-start | bytes 49160 | tf_op jit(solution)/shard_map/while/body/eval_jaxpr/ppermute | solution.py:14
  248.2 6.3 %collective-permute-start = (f32[16,256]{1,0:T(8,128)S(1)}, f32[16,256]{1,0:T(8,128)S(1)}, u32[]{:S(2)}, u32[]{:S(2)}) collective-permute-start(f32[16,256]{1,0:T(8,128)S(1)} %multiply_add_fusion.2), channel_id=1, source_target_pairs={{0,16},{16,32},{32,48},{48,64},{64,80},{80,96},{96,112},{112,128},... | collective-permute-start | bytes 49160 | tf_op jit(solution)/shard_map/while/body/eval_jaxpr/ppermute | solution.py:14
  254.5 6.3 %collective-permute-start = (f32[16,256]{1,0:T(8,128)S(1)}, f32[16,256]{1,0:T(8,128)S(1)}, u32[]{:S(2)}, u32[]{:S(2)}) collective-permute-start(f32[16,256]{1,0:T(8,128)S(1)} %multiply_add_fusion.2), channel_id=1, source_target_pairs={{0,16},{16,32},{32,48},{48,64},{64,80},{80,96},{96,112},{112,128},... | collective-permute-start | bytes 49160 | tf_op jit(solution)/shard_map/while/body/eval_jaxpr/ppermute | solution.py:14
  260.8 6.3 %collective-permute-start = (f32[16,256]{1,0:T(8,128)S(1)}, f32[16,256]{1,0:T(8,128)S(1)}, u32[]{:S(2)}, u32[]{:S(2)}) collective-permute-start(f32[16,256]{1,0:T(8,128)S(1)} %multiply_add_fusion.2), channel_id=1, source_target_pairs={{0,16},{16,32},{32,48},{48,64},{64,80},{80,96},{96,112},{112,128},... | collective-permute-start | bytes 49160 | tf_op jit(solution)/shard_map/while/body/eval_jaxpr/ppermute | solution.py:14
  267.0 6.3 %collective-permute-start = (f32[16,256]{1,0:T(8,128)S(1)}, f32[16,256]{1,0:T(8,128)S(1)}, u32[]{:S(2)}, u32[]{:S(2)}) collective-permute-start(f32[16,256]{1,0:T(8,128)S(1)} %multiply_add_fusion.2), channel_id=1, source_target_pairs={{0,16},{16,32},{32,48},{48,64},{64,80},{80,96},{96,112},{112,128},... | collective-permute-start | bytes 49160 | tf_op jit(solution)/shard_map/while/body/eval_jaxpr/ppermute | solution.py:14
  273.3 6.3 %collective-permute-start = (f32[16,256]{1,0:T(8,128)S(1)}, f32[16,256]{1,0:T(8,128)S(1)}, u32[]{:S(2)}, u32[]{:S(2)}) collective-permute-start(f32[16,256]{1,0:T(8,128)S(1)} %multiply_add_fusion.2), channel_id=1, source_target_pairs={{0,16},{16,32},{32,48},{48,64},{64,80},{80,96},{96,112},{112,128},... | collective-permute-start | bytes 49160 | tf_op jit(solution)/shard_map/while/body/eval_jaxpr/ppermute | solution.py:14
  279.6 6.3 %collective-permute-start = (f32[16,256]{1,0:T(8,128)S(1)}, f32[16,256]{1,0:T(8,128)S(1)}, u32[]{:S(2)}, u32[]{:S(2)}) collective-permute-start(f32[16,256]{1,0:T(8,128)S(1)} %multiply_add_fusion.2), channel_id=1, source_target_pairs={{0,16},{16,32},{32,48},{48,64},{64,80},{80,96},{96,112},{112,128},... | collective-permute-start | bytes 49160 | tf_op jit(solution)/shard_map/while/body/eval_jaxpr/ppermute | solution.py:14
  285.8 6.3 %collective-permute-start = (f32[16,256]{1,0:T(8,128)S(1)}, f32[16,256]{1,0:T(8,128)S(1)}, u32[]{:S(2)}, u32[]{:S(2)}) collective-permute-start(f32[16,256]{1,0:T(8,128)S(1)} %multiply_add_fusion.2), channel_id=1, source_target_pairs={{0,16},{16,32},{32,48},{48,64},{64,80},{80,96},{96,112},{112,128},... | collective-permute-start | bytes 49160 | tf_op jit(solution)/shard_map/while/body/eval_jaxpr/ppermute | solution.py:14
  292.1 6.3 %collective-permute-start = (f32[16,256]{1,0:T(8,128)S(1)}, f32[16,256]{1,0:T(8,128)S(1)}, u32[]{:S(2)}, u32[]{:S(2)}) collective-permute-start(f32[16,256]{1,0:T(8,128)S(1)} %multiply_add_fusion.2), channel_id=1, source_target_pairs={{0,16},{16,32},{32,48},{48,64},{64,80},{80,96},{96,112},{112,128},... | collective-permute-start | bytes 49160 | tf_op jit(solution)/shard_map/while/body/eval_jaxpr/ppermute | solution.py:14
  298.4 6.3 %collective-permute-start = (f32[16,256]{1,0:T(8,128)S(1)}, f32[16,256]{1,0:T(8,128)S(1)}, u32[]{:S(2)}, u32[]{:S(2)}) collective-permute-start(f32[16,256]{1,0:T(8,128)S(1)} %multiply_add_fusion.2), channel_id=1, source_target_pairs={{0,16},{16,32},{32,48},{48,64},{64,80},{80,96},{96,112},{112,128},... | collective-permute-start | bytes 49160 | tf_op jit(solution)/shard_map/while/body/eval_jaxpr/ppermute | solution.py:14
  304.6 6.3 %collective-permute-start = (f32[16,256]{1,0:T(8,128)S(1)}, f32[16,256]{1,0:T(8,128)S(1)}, u32[]{:S(2)}, u32[]{:S(2)}) collective-permute-start(f32[16,256]{1,0:T(8,128)S(1)} %multiply_add_fusion.2), channel_id=1, source_target_pairs={{0,16},{16,32},{32,48},{48,64},{64,80},{80,96},{96,112},{112,128},... | collective-permute-start | bytes 49160 | tf_op jit(solution)/shard_map/while/body/eval_jaxpr/ppermute | solution.py:14
  310.9 6.3 %collective-permute-start = (f32[16,256]{1,0:T(8,128)S(1)}, f32[16,256]{1,0:T(8,128)S(1)}, u32[]{:S(2)}, u32[]{:S(2)}) collective-permute-start(f32[16,256]{1,0:T(8,128)S(1)} %multiply_add_fusion.2), channel_id=1, source_target_pairs={{0,16},{16,32},{32,48},{48,64},{64,80},{80,96},{96,112},{112,128},... | collective-permute-start | bytes 49160 | tf_op jit(solution)/shard_map/while/body/eval_jaxpr/ppermute | solution.py:14
  317.1 6.3 %collective-permute-start = (f32[16,256]{1,0:T(8,128)S(1)}, f32[16,256]{1,0:T(8,128)S(1)}, u32[]{:S(2)}, u32[]{:S(2)}) collective-permute-start(f32[16,256]{1,0:T(8,128)S(1)} %multiply_add_fusion.2), channel_id=1, source_target_pairs={{0,16},{16,32},{32,48},{48,64},{64,80},{80,96},{96,112},{112,128},... | collective-permute-start | bytes 49160 | tf_op jit(solution)/shard_map/while/body/eval_jaxpr/ppermute | solution.py:14
  323.4 6.3 %collective-permute-start = (f32[16,256]{1,0:T(8,128)S(1)}, f32[16,256]{1,0:T(8,128)S(1)}, u32[]{:S(2)}, u32[]{:S(2)}) collective-permute-start(f32[16,256]{1,0:T(8,128)S(1)} %multiply_add_fusion.2), channel_id=1, source_target_pairs={{0,16},{16,32},{32,48},{48,64},{64,80},{80,96},{96,112},{112,128},... | collective-permute-start | bytes 49160 | tf_op jit(solution)/shard_map/while/body/eval_jaxpr/ppermute | solution.py:14
  329.7 6.3 %collective-permute-start = (f32[16,256]{1,0:T(8,128)S(1)}, f32[16,256]{1,0:T(8,128)S(1)}, u32[]{:S(2)}, u32[]{:S(2)}) collective-permute-start(f32[16,256]{1,0:T(8,128)S(1)} %multiply_add_fusion.2), channel_id=1, source_target_pairs={{0,16},{16,32},{32,48},{48,64},{64,80},{80,96},{96,112},{112,128},... | collective-permute-start | bytes 49160 | tf_op jit(solution)/shard_map/while/body/eval_jaxpr/ppermute | solution.py:14
  336.7 8.0 %copy-start = (f32[256,32,64]{2,1,0:T(8,128)S(1)}, f32[256,32,64]{2,1,0:T(8,128)}, u32[]{:S(2)}) copy-start(f32[256,32,64]{2,1,0:T(8,128)} %fusion.28) | copy-start | bytes 6291460
  336.7 8.0 %copy-start.2 = (f32[16,256]{0,1:T(8,128)S(1)}, f32[16,256]{0,1:T(8,128)}, u32[]{:S(2)}) copy-start(f32[16,256]{0,1:T(8,128)} %copy.36) | copy-start | bytes 49156
  355.5 3.6 copy-start.5
where the time goes:
time: 383 us; the launch traced here: 381 us
  waiting for transfers between devices  190 us (50%)
  starting transfers between devices  69.6 us (18%)
  local copies, waits for them, and re-layouts  38 us (10%)
  matrix products  37.7 us (10%)
  other arithmetic  26.2 us (7%)
  blocking collectives  18.7 us (5%)
    ppermute x32, waiting for transfers between devices, from_behind(): return lax.ppermute(block, axis, route)  133 us
    ppermute x32, starting transfers between devices, from_behind(): return lax.ppermute(block, axis, route)  62.4 us
    all_to_all x1, waiting for transfers between devices, local(): lax.all_to_all(features, 'chan', split_axis=2, concat_axis=1, tiled=True)  56.6 us
    dynamic_update_slice x32, other arithmetic, modal_conv(): final, starts = lax.scan(advance, start_state, local_end)  19.5 us
    all_to_all x1, blocking collectives, local(): lax.all_to_all(gated, 'chan', split_axis=0, concat_axis=1, tiled=True)  18.7 us
    unnamed x16, local copies, waits for them, and re-layouts  11.3 us
    dot_general x1, matrix products, long_part(): jnp.einsum('nic,knc->kic', tables[2], entering, precision=lax.Precision.H...  10.9 us
    dot_general x1, matrix products, modal_conv(): jnp.einsum('ijc,kjc->kic', toeplitz, pieces, precision=lax.Precision.HIGH...  10.3 us
  transfers between devices with their start and end apart: 33, of which 32 were waited for; matrix products, arithmetic and copies ran while one was open for 4% of the time, Pallas kernels for 0%

commit v1 on v0

--- a/solution.py
+++ b/solution.py
@@ -68,12 +68,15 @@
     tables = modal_tables(decay_rate, scaled, block)
     zero_state = jnp.zeros_like(decay_rate)
     longconv, end_state = modal_conv(signal, decay_rate, tables, zero_state, block)
-    section_decay = jnp.exp(-decay_rate * section)
 
-    def advance_section(turn_index, carry_state):
-        return from_behind(section_decay * carry_state + end_state, "seq", 1)
-
-    incoming = lax.fori_loop(0, lax.axis_size("seq") - 1, advance_section, zero_state)
+    sections = lax.axis_size("seq")
+    gathered = lax.all_gather(end_state, "seq")
+    here = lax.axis_index("seq")
+    earlier = jnp.arange(sections)
+    lag = jnp.maximum(here - 1 - earlier, 0).astype(jnp.float32)
+    weight = jnp.exp(-decay_rate[None, :, :] * (section * lag)[:, None, None])
+    weight = jnp.where((earlier < here)[:, None, None], weight, 0.0)
+    incoming = jnp.sum(weight * gathered, axis=0)
     block_starts = (jnp.arange(count).astype(jnp.float32) * block)[:, None, None]
     entering = jnp.exp(-decay_rate[None, :, :] * block_starts) * incoming[None, :, :]
     correction = jnp.einsum(

time: 383 us -> 231 us (0.60)
  the two profiles are of different devices: /device:TPU:384 before, /device:TPU:1 now
where the time goes in v1:
time: 231 us; the launch traced here: 230 us
  blocking collectives  56.7 us (25%)
  waiting for transfers between devices  47.1 us (20%)
  local copies, waits for them, and re-layouts  40.8 us (18%)
  matrix products  36.7 us (16%)
  other arithmetic  27.1 us (12%)
  starting transfers between devices  21.8 us (9%)
    all_to_all x1, waiting for transfers between devices, local(): lax.all_to_all(features, 'chan', split_axis=2, concat_axis=1, tiled=True)  47 us
    all_gather x1, blocking collectives, long_part(): gathered = lax.all_gather(end_state, 'seq')  36 us
    all_to_all x1, blocking collectives, local(): lax.all_to_all(gated, 'chan', split_axis=0, concat_axis=1, tiled=True)  20.7 us
    dynamic_update_slice x32, other arithmetic, modal_conv(): final, starts = lax.scan(advance, start_state, local_end)  19.5 us
    ppermute x1, starting transfers between devices, from_behind(): return lax.ppermute(block, axis, route)  14 us
    unnamed x16, local copies, waits for them, and re-layouts  11.2 us
    dot_general x1, matrix products, modal_conv(): jnp.einsum('ijc,kjc->kic', toeplitz, pieces, precision=lax.Precision.HIGH...  10.3 us
    dot_general x1, matrix products, long_part(): jnp.einsum('nic,knc->kic', tables[2], entering, precision=lax.Precision.H...  9.82 us
  transfers between devices with their start and end apart: 2, of which 1 were waited for; matrix products, arithmetic and copies ran while one was open for 7% of the time, Pallas kernels for 0%

profile of v1, /device:TPU:1, one launch (start us, length us, event | category | flops | bytes accessed | tf_op | source)
XLA Modules:
  0.0 230.4 jit_solution(1023157833966102798)
XLA Ops:
  0.0 7.2 %copy.23 = bf16[3,128,4096]{1,0,2:T(4,128)(2,1)} copy(bf16[3,128,4096]{2,1,0:T(8,128)(2,1)} %param.7) | data formatting | bytes 6291456 | tf_op args[0]
  7.2 7.8 %all-to-all-start = ((bf16[3,128,4096]{1,0,2:T(4,128)(2,1)}), bf16[3,128,4096]{1,0,2:T(4,128)(2,1)}, u32[]{:S(2)}, u32[]{:S(2)}) async-start(bf16[3,128,4096]{1,0,2:T(4,128)(2,1)} %copy.23), calls=%async_computation | async-start | bytes 8388608 | tf_op jit(solution)/shard_map/all_to_all | solution.py:91
  15.3 1.0 constant_dynamic-slice_fusion.1
  16.2 1.6 multiply_reduce_fusion
  17.9 3.8 %fusion.7 = f32[64,64,256]{2,1,0:T(8,128)} fusion(s32[64,64]{1,0:T(8,128)S(1)} %iota_subtract_fusion, f32[64,256]{0,1:T(8,128)S(1)} %multiply_reduce_fusion), kind=kOutput, calls=%fused_computation.20 | convolution fusion | flops 805568512 | bytes 4276224 | tf_op jit(solution)/shard_map/dot_general | solution.py:36
  21.7 47.0 %all-to-all-done = bf16[3,128,4096]{1,0,2:T(4,128)(2,1)} async-done(((bf16[3,128,4096]{1,0,2:T(4,128)(2,1)}), bf16[3,128,4096]{1,0,2:T(4,128)(2,1)}, u32[]{:S(2)}, u32[]{:S(2)}) %all-to-all-start) | async-done | bytes 3145760 | tf_op jit(solution)/shard_map/all_to_all | solution.py:91
  68.8 5.5 %copy.24 = bf16[3,128,16,256]{3,1,2,0:T(8,128)(2,1)S(1)} copy(bf16[3,128,16,256]{1,0,3,2:T(4,128)(2,1)} %bitcast) | data formatting | bytes 6291456 | tf_op jit(solution)/shard_map/all_to_all | solution.py:91
  74.3 14.0 %collective-permute-start = (bf16[3,2,256]{2,1,0:T(2,128)(2,1)S(1)}, bf16[3,2,256]{2,1,0:T(2,128)(2,1)S(1)}, u32[]{:S(2)}, u32[]{:S(2)}) collective-permute-start(bf16[3,2,256]{2,1,0:T(2,128)(2,1)S(1)} %slice.36), channel_id=1, source_target_pairs={{0,16},{16,32},{32,48},{48,64},{64,80},{80,96},{96,112},{112,128},... | collective-permute-start | bytes 9224 | tf_op jit(solution)/shard_map/ppermute | solution.py:14
  88.4 9.2 %copy.29 = f32[64,64,256]{1,0,2:T(8,128)} copy(f32[64,64,256]{2,1,0:T(8,128)} %fusion.7) | data formatting | bytes 8388608 | tf_op jit(solution)/shard_map/dot_general | solution.py:36
  97.5 2.5 %add_convert_fusion = bf16[3,2048,256]{2,1,0:T(8,128)(2,1)S(1)} fusion(bf16[3,2048,256]{2,1,0:T(8,128)(2,1)S(1)} %bitcast.51, bf16[3,2,256]{2,1,0:T(2,128)(2,1)S(1)} %collective-permute-done, f32[3,256]{1,0:T(4,128)S(1)} %get-tuple-element.84, f32[3,256]{1,0:T(4,128)S(1)} %get-tuple-element.85, f32[3,256]{1,0:T(4,128)S(1)} %bitcast.56), kind=kLoop, calls=%fused_computation.2 | loop fusion | flops 23592960 | bytes 6303744 | tf_op jit(solution)/shard_map/convert_element_type | solution.py:97
  100.4 1.3 copy-done.1
  101.7 3.1 %copy.28 = bf16[32,64,256]{1,0,2:T(8,128)(2,1)S(1)} copy(bf16[32,64,256]{2,1,0:T(8,128)(2,1)S(1)} %bitcast.52) | data formatting | bytes 2097152 | tf_op jit(solution)/shard_map/reshape | solution.py:49
  104.8 10.3 %fusion.22 = f32[256,32,64]{2,1,0:T(8,128)} fusion(bf16[32,64,256]{1,0,2:T(8,128)(2,1)S(1)} %copy.28, f32[64,64,256]{1,0,2:T(8,128)} %copy.29), kind=kOutput, calls=%fused_computation.51 | convolution fusion | flops 402653184 | bytes 7340032 | tf_op jit(solution)/shard_map/ijc,kjc->kic/dot_general | solution.py:50
  115.0 4.8 %fusion.8 = f32[32,16,256]{0,1,2:T(8,128)} fusion(bf16[32,64,256]{1,0,2:T(8,128)(2,1)S(1)} %copy.28, f32[64]{0:T(128)S(1)} %broadcast_subtract_fusion, f32[16,256]{0,1:T(8,128)S(1)} %copy.26), kind=kOutput, calls=%fused_computation.21 | convolution fusion | flops 100925440 | bytes 1589504 | tf_op jit(solution)/shard_map/njc,kjc->knc/dot_general | solution.py:51
  119.8 2.7 %copy.31 = f32[32,16,256]{2,1,0:T(8,128)S(1)} copy(f32[32,16,256]{0,1,2:T(8,128)} %fusion.8) | data formatting | bytes 1048576
  122.5 19.8 %while.14 = (s32[]{:T(128)}, f32[16,256]{1,0:T(8,128)S(1)}, f32[32,16,256]{2,1,0:T(8,128)}, f32[16,256]{1,0:T(8,128)S(1)}, f32[32,16,256]{2,1,0:T(8,128)S(1)}) while((s32[]{:T(128)}, f32[16,256]{1,0:T(8,128)S(1)}, f32[32,16,256]{2,1,0:T(8,128)}, f32[16,256]{1,0:T(8,128)S(1)}, f32[32,16,256]{2,1,0:T(8,128)S(1)}) %tuple.33), condition=%wide.region_2.3_spmd.clone.clone, body=%wide.region_1.2_spmd.clone.sunk.clone | while | flops 16387 | bytes 98892 | solution.py:57
  122.5 0.6 bitcast_dynamic-update-slice_fusion.3
  123.1 0.6 bitcast_dynamic-update-slice_fusion.3
  123.8 0.6 bitcast_dynamic-update-slice_fusion.3
  124.4 0.6 bitcast_dynamic-update-slice_fusion.3
  125.0 0.6 bitcast_dynamic-update-slice_fusion.3
  125.6 0.6 bitcast_dynamic-update-slice_fusion.3
  126.2 0.6 bitcast_dynamic-update-slice_fusion.3
  126.8 0.6 bitcast_dynamic-update-slice_fusion.3
  127.5 0.6 bitcast_dynamic-update-slice_fusion.3
  128.1 0.6 bitcast_dynamic-update-slice_fusion.3
  128.7 0.6 bitcast_dynamic-update-slice_fusion.3
  129.3 0.6 bitcast_dynamic-update-slice_fusion.3
  129.9 0.6 bitcast_dynamic-update-slice_fusion.3
  130.5 0.6 bitcast_dynamic-update-slice_fusion.3
  131.2 0.6 bitcast_dynamic-update-slice_fusion.3
  131.8 0.6 bitcast_dynamic-update-slice_fusion.3
  132.4 0.6 bitcast_dynamic-update-slice_fusion.3
  133.0 0.6 bitcast_dynamic-update-slice_fusion.3
  133.6 0.6 bitcast_dynamic-update-slice_fusion.3
  134.3 0.6 bitcast_dynamic-update-slice_fusion.3
  134.9 0.6 bitcast_dynamic-update-slice_fusion.3
  135.5 0.6 bitcast_dynamic-update-slice_fusion.3
  142.3 2.4 %copy.32 = f32[32,16,256]{0,1,2:T(8,128)S(1)} copy(f32[32,16,256]{2,1,0:T(8,128)} %get-tuple-element.33) | data formatting | bytes 1048576 | tf_op jit(solution)/shard_map/while | solution.py:57
  144.7 36.0 %all-gather = f32[512,256]{1,0:T(8,128)S(1)} all-gather(f32[16,256]{1,0:T(8,128)S(1)} %get-tuple-element.34), channel_id=2, replica_groups=mesh['seq'=32,'chan'=16] {'seq'}, dimensions={0}, use_global_device_ids=true | all-gather | bytes 540672 | tf_op jit(solution)/shard_map/all_gather | solution.py:73
  180.9 0.9 exponential_multiply_fusion.3
  181.8 3.6 %copy.33 = f32[32,16,256]{0,1,2:T(8,128)} copy(f32[32,16,256]{2,1,0:T(8,128)} %exponential_multiply_fusion.3) | data formatting | bytes 1048576 | tf_op jit(solution)/shard_map/mul | solution.py:81
  185.4 7.9 %fusion.3 = f32[256,32,64]{2,1,0:T(8,128)S(1)} fusion(f32[32,16,256]{0,1,2:T(8,128)S(1)} %copy.32, f32[64]{0:T(128)S(1)} %broadcast_add_fusion, f32[16,256]{0,1:T(8,128)S(1)} %copy.26, f32[16,256]{0,1:T(8,128)S(1)} %copy.25), kind=kOutput, calls=%fused_computation.13 | convolution fusion | flops 101187584 | bytes 2654464 | tf_op jit(solution)/shard_map/nic,knc->kic/dot_general | solution.py:58
  193.4 9.8 %add_bitcast_fusion = f32[32,64,256]{1,0,2:T(8,128)} fusion(f32[256,32,64]{2,1,0:T(8,128)S(1)} %copy-done, f32[256,32,64]{2,1,0:T(8,128)S(1)} %fusion.3, f32[32,16,256]{0,1,2:T(8,128)S(1)} %copy-done.2, f32[64]{0:T(128)S(1)} %broadcast_add_fusion, f32[16,256]{0,1:T(8,128)S(1)} %copy.26, f32[16,256]{0,1:T(8,128)S(1)} %copy.25), kind=kOutput, calls=%fused_computation.3 | convolution fusion | flops 102236160 | bytes 6848768 | tf_op jit(solution)/shard_map/nic,knc->kic/dot_general | solution.py:82
  203.2 3.6 %copy.34 = f32[32,64,256]{2,1,0:T(8,128)S(1)} copy(f32[32,64,256]{1,0,2:T(8,128)} %add_bitcast_fusion) | data formatting | bytes 4194304 | tf_op jit(solution)/shard_map/add | solution.py:85
  207.0 1.5 fusion.1
  208.6 20.7 %all_to_all.37 = bf16[16,128,256]{2,1,0:T(8,128)(2,1)S(1)} all-to-all(bf16[16,128,256]{2,1,0:T(8,128)(2,1)S(1)} %bitcast.53), channel_id=1, replica_groups=mesh['seq'=32,'chan'=16] {'chan'}, dimensions={0} | all-to-all | bytes 2097152 | tf_op jit(solution)/shard_map/all_to_all | solution.py:103
  229.3 1.1 copy.41
  (72 shorter events, 7.3 us)
Async XLA Ops:
  7.2 7.8 %copy-start.3 = (f32[16,256]{1,0:T(8,128)S(1)}, f32[16,256]{1,0:T(8,128)}, u32[]{:S(2)}) copy-start(f32[16,256]{1,0:T(8,128)} %param.9) | copy-start | bytes 49156
  7.2 7.8 %copy-start.4 = (f32[16,256]{1,0:T(8,128)S(1)}, f32[16,256]{1,0:T(8,128)}, u32[]{:S(2)}) copy-start(f32[16,256]{1,0:T(8,128)} %param.10) | copy-start | bytes 49156
  7.2 61.6 %all-to-all-start = ((bf16[3,128,4096]{1,0,2:T(4,128)(2,1)}), bf16[3,128,4096]{1,0,2:T(4,128)(2,1)}, u32[]{:S(2)}, u32[]{:S(2)}) async-start(bf16[3,128,4096]{1,0,2:T(4,128)(2,1)} %copy.23), calls=%async_computation | async-start | bytes 8388608 | tf_op jit(solution)/shard_map/all_to_all | solution.py:91
  74.3 23.2 %collective-permute-start = (bf16[3,2,256]{2,1,0:T(2,128)(2,1)S(1)}, bf16[3,2,256]{2,1,0:T(2,128)(2,1)S(1)}, u32[]{:S(2)}, u32[]{:S(2)}) collective-permute-start(bf16[3,2,256]{2,1,0:T(2,128)(2,1)S(1)} %slice.36), channel_id=1, source_target_pairs={{0,16},{16,32},{32,48},{48,64},{64,80},{80,96},{96,112},{112,128},... | collective-permute-start | bytes 9224 | tf_op jit(solution)/shard_map/ppermute | solution.py:14
  100.0 1.6 copy-start.1
  185.4 7.9 %copy-start = (f32[256,32,64]{2,1,0:T(8,128)S(1)}, f32[256,32,64]{2,1,0:T(8,128)}, u32[]{:S(2)}) copy-start(f32[256,32,64]{2,1,0:T(8,128)} %fusion.22) | copy-start | bytes 6291460
  185.4 8.0 %copy-start.2 = (f32[32,16,256]{0,1,2:T(8,128)S(1)}, f32[32,16,256]{0,1,2:T(8,128)}, u32[]{:S(2)}) copy-start(f32[32,16,256]{0,1,2:T(8,128)} %copy.33) | copy-start | bytes 1572868
  203.2 3.6 %copy-start.5 = (f32[256]{0:T(256)S(1)}, f32[256]{0:T(256)}, u32[]{:S(2)}) copy-start(f32[256]{0:T(256)} %param.11) | copy-start | bytes 3076

commit v2 on v0

--- a/solution.py
+++ b/solution.py
@@ -43,20 +43,9 @@
     return (toeplitz, ending, reading)
 
 
-def modal_conv(signal, decay_rate, tables, start_state, block):
-    toeplitz, ending, reading = tables
-    count = signal.shape[0] // block
-    pieces = signal.reshape(count, block, signal.shape[1])
-    inner = jnp.einsum("ijc,kjc->kic", toeplitz, pieces, precision=lax.Precision.HIGHEST)
-    local_end = jnp.einsum("njc,kjc->knc", ending, pieces, precision=lax.Precision.HIGHEST)
-    group_decay = jnp.exp(-decay_rate * block)
-
-    def advance(state, piece):
-        return (group_decay * state + piece, state)
-
-    final, starts = lax.scan(advance, start_state, local_end)
-    carried = jnp.einsum("nic,knc->kic", reading, starts, precision=lax.Precision.HIGHEST)
-    return ((inner + carried).reshape(signal.shape), final)
+def shifted(values, distance):
+    padding = jnp.zeros((distance,) + values.shape[1:], values.dtype)
+    return jnp.concatenate([padding, values[: values.shape[0] - distance]], axis=0)
 
 
 def long_part(product, decay_rate, residue, skip_gain):
@@ -65,21 +54,31 @@
     block = math.gcd(section, block_len)
     count = section // block
     scaled = residue * jnp.sqrt(1.0 - jnp.exp(-2.0 * decay_rate))
-    tables = modal_tables(decay_rate, scaled, block)
-    zero_state = jnp.zeros_like(decay_rate)
-    longconv, end_state = modal_conv(signal, decay_rate, tables, zero_state, block)
-    section_decay = jnp.exp(-decay_rate * section)
-
-    def advance_section(turn_index, carry_state):
-        return from_behind(section_decay * carry_state + end_state, "seq", 1)
-
-    incoming = lax.fori_loop(0, lax.axis_size("seq") - 1, advance_section, zero_state)
+    toeplitz, ending, reading = modal_tables(decay_rate, scaled, block)
+    pieces = signal.reshape(count, block, signal.shape[1])
+    local_end = jnp.einsum("njc,kjc->knc", ending, pieces, precision=lax.Precision.HIGHEST)
+    starts = shifted(local_end, 1)
+    step = 1
+    while step < count:
+        starts = starts + jnp.exp(-decay_rate * float(block * step)) * shifted(starts, step)
+        step *= 2
+    end_state = jnp.exp(-decay_rate * float(block)) * starts[count - 1] + local_end[count - 1]
+    sections = lax.axis_size("seq")
+    incoming = from_behind(end_state, "seq", 1)
+    if sections > 2:
+        incoming = incoming + jnp.exp(-decay_rate * float(section)) * from_behind(end_state, "seq", 2)
+    step = 2
+    while step < sections:
+        incoming = incoming + jnp.exp(-decay_rate * float(section * step)) * from_behind(
+            incoming, "seq", step
+        )
+        step *= 2
+    inner = jnp.einsum("ijc,kjc->kic", toeplitz, pieces, precision=lax.Precision.HIGHEST)
     block_starts = (jnp.arange(count).astype(jnp.float32) * block)[:, None, None]
-    entering = jnp.exp(-decay_rate[None, :, :] * block_starts) * incoming[None, :, :]
-    correction = jnp.einsum(
-        "nic,knc->kic", tables[2], entering, precision=lax.Precision.HIGHEST
-    ).reshape(signal.shape)
-    return (longconv + correction + skip_gain[None, :] * signal).astype(jnp.bfloat16)
+    starts = starts + jnp.exp(-decay_rate[None, :, :] * block_starts) * incoming[None, :, :]
+    carried = jnp.einsum("nic,knc->kic", reading, starts, precision=lax.Precision.HIGHEST)
+    longconv = (inner + carried).reshape(signal.shape)
+    return (longconv + skip_gain[None, :] * signal).astype(jnp.bfloat16)
 
 
 def local(features, short_weight, decay_rate, residue, skip_gain):

time: 383 us -> 233 us (0.61)
  the two profiles are of different devices: /device:TPU:384 before, /device:TPU:2 now
where the time goes in v2:
time: 233 us; the launch traced here: 232 us
  starting transfers between devices  61.2 us (26%)
  waiting for transfers between devices  56.5 us (24%)
  local copies, waits for them, and re-layouts  48.3 us (21%)
  matrix products  30.5 us (13%)
  blocking collectives  20.2 us (9%)
  other arithmetic  15.2 us (7%)
    ppermute x7, starting transfers between devices, from_behind(): return lax.ppermute(block, axis, route)  50.9 us
    all_to_all x1, waiting for transfers between devices, local(): lax.all_to_all(features, 'chan', split_axis=2, concat_axis=1, tiled=True)  49.4 us
    all_to_all x1, blocking collectives, local(): lax.all_to_all(gated, 'chan', split_axis=0, concat_axis=1, tiled=True)  20.2 us
    dot_general x1, matrix products, long_part(): jnp.einsum('nic,knc->kic', reading, starts, precision=lax.Precision.HIGHEST)  12.4 us
    unnamed x19, local copies, waits for them, and re-layouts  11.4 us
    all_to_all x1, starting transfers between devices, local(): lax.all_to_all(features, 'chan', split_axis=2, concat_axis=1, tiled=True)  10.3 us
    dot_general x1, matrix products, long_part(): jnp.einsum('ijc,kjc->kic', toeplitz, pieces, precision=lax.Precision.HIGH...  10.3 us
    dot_general x1, local copies, waits for them, and re-layouts, modal_tables(): jnp.dot(one_hot.reshape(block * block, block), kernel, precision=lax.Prec...  9.18 us
  transfers between devices with their start and end apart: 8, of which 6 were waited for; matrix products, arithmetic and copies ran while one was open for 3% of the time, Pallas kernels for 0%

profile of v2, /device:TPU:2, one launch (start us, length us, event | category | flops | bytes accessed | tf_op | source)
XLA Modules:
  0.0 232.2 jit_solution(7204095979553046049)
XLA Ops:
  0.0 7.2 %copy.38 = bf16[3,128,4096]{1,0,2:T(4,128)(2,1)} copy(bf16[3,128,4096]{2,1,0:T(8,128)(2,1)} %param.5) | data formatting | bytes 6291456 | tf_op args[0]
  7.2 10.3 %all-to-all-start = ((bf16[3,128,4096]{1,0,2:T(4,128)(2,1)}), bf16[3,128,4096]{1,0,2:T(4,128)(2,1)}, u32[]{:S(2)}, u32[]{:S(2)}) async-start(bf16[3,128,4096]{1,0,2:T(4,128)(2,1)} %copy.38), calls=%async_computation | async-start | bytes 8388608 | tf_op jit(solution)/shard_map/all_to_all | solution.py:87
  17.5 0.9 constant_dynamic-slice_fusion.1
  18.4 0.6 copy_bitcast_fusion
  19.0 0.6 multiply_exponential_fusion
  19.7 49.4 %all-to-all-done = bf16[3,128,4096]{1,0,2:T(4,128)(2,1)} async-done(((bf16[3,128,4096]{1,0,2:T(4,128)(2,1)}), bf16[3,128,4096]{1,0,2:T(4,128)(2,1)}, u32[]{:S(2)}, u32[]{:S(2)}) %all-to-all-start) | async-done | bytes 3145760 | tf_op jit(solution)/shard_map/all_to_all | solution.py:87
  69.0 5.5 %copy.39 = bf16[3,128,16,256]{3,1,2,0:T(8,128)(2,1)S(1)} copy(bf16[3,128,16,256]{1,0,3,2:T(4,128)(2,1)} %bitcast) | data formatting | bytes 6291456 | tf_op jit(solution)/shard_map/all_to_all | solution.py:87
  74.5 0.6 slice.68
  75.1 1.9 collective-permute-start
  78.2 0.8 copy.46
  79.0 0.8 copy.47
  79.7 0.8 copy.48
  80.6 0.8 copy.50
  81.4 3.3 %add_convert_fusion = bf16[3,2048,256]{2,1,0:T(8,128)(2,1)S(1)} fusion(bf16[3,2048,256]{2,1,0:T(8,128)(2,1)S(1)} %bitcast.55, bf16[3,2,256]{2,1,0:T(2,128)(2,1)} %collective-permute-done, f32[3,256]{1,0:T(4,128)} %get-tuple-element.16, f32[3,256]{1,0:T(4,128)} %get-tuple-element.17, f32[3,256]{1,0:T(4,128)} %bitcast.59), kind=kLoop, calls=%fused_computation | loop fusion | flops 23592960 | bytes 6303744 | tf_op jit(solution)/shard_map/convert_element_type | solution.py:93
  85.0 1.3 copy-done.1
  86.3 3.1 %copy.43 = bf16[32,64,256]{1,0,2:T(8,128)(2,1)S(1)} copy(bf16[32,64,256]{2,1,0:T(8,128)(2,1)S(1)} %bitcast.56) | data formatting | bytes 2097152 | tf_op jit(solution)/shard_map/reshape | solution.py:58
  89.4 4.0 %fusion.14 = f32[32,16,256]{0,1,2:T(8,128)S(1)} fusion(bf16[32,64,256]{1,0,2:T(8,128)(2,1)S(1)} %copy.43, f32[64]{0:T(128)} %broadcast_subtract_fusion, f32[16,256]{0,1:T(8,128)S(1)} %copy.41), kind=kOutput, calls=%fused_computation.30 | convolution fusion | flops 100925440 | bytes 1589504 | tf_op jit(solution)/shard_map/njc,kjc->knc/dot_general | solution.py:59
  93.4 1.9 slice.80
  95.4 0.6 pad_slice_fusion.2
  96.3 1.8 multiply_add_fusion.4
  98.1 1.3 multiply_add_fusion.3
  99.4 1.3 multiply_add_fusion.2
  100.7 1.3 multiply_add_fusion.1
  101.9 1.4 multiply_add_fusion
  103.4 1.3 copy-done
  104.7 1.9 slice.79
  106.6 2.5 %copy.52 = f32[1,16,256]{2,1,0:T(8,128)S(1)} copy(f32[1,16,256]{0,1,2:T(8,128)} %slice.79) | data formatting | bytes 32768 | tf_op jit(solution)/shard_map/slice | solution.py:65
  109.1 2.5 %copy.53 = f32[1,16,256]{2,1,0:T(8,128)S(1)} copy(f32[1,16,256]{0,1,2:T(8,128)} %slice.80) | data formatting | bytes 32768 | tf_op jit(solution)/shard_map/slice | solution.py:65
  111.7 9.0 %collective-permute-start.1 = (f32[16,256]{1,0:T(8,128)S(1)}, f32[16,256]{1,0:T(8,128)S(1)}, u32[]{:S(2)}, u32[]{:S(2)}) collective-permute-start(f32[16,256]{1,0:T(8,128)S(1)} %bitcast_add_fusion.1), channel_id=1, source_target_pairs={{0,16},{16,32},{32,48},{48,64},{64,80},{80,96},{96,112},{112,128},... | collective-permute-start | bytes 49160 | tf_op jit(solution)/shard_map/ppermute | solution.py:14
  120.6 3.8 %collective-permute-start.2 = (f32[16,256]{1,0:T(8,128)S(1)}, f32[16,256]{1,0:T(8,128)S(1)}, u32[]{:S(2)}, u32[]{:S(2)}) collective-permute-start(f32[16,256]{1,0:T(8,128)S(1)} %bitcast_add_fusion.1), channel_id=1, source_target_pairs={{0,32},{16,48},{32,64},{48,80},{64,96},{80,112},{96,128},{112,144}... | collective-permute-start | bytes 49160 | tf_op jit(solution)/shard_map/ppermute | solution.py:14
  124.5 1.4 collective-permute-done.2
  125.9 4.2 %collective-permute-start.3 = (f32[16,256]{1,0:T(8,128)S(1)}, f32[16,256]{1,0:T(8,128)S(1)}, u32[]{:S(2)}, u32[]{:S(2)}) collective-permute-start(f32[16,256]{1,0:T(8,128)S(1)} %multiply_add_fusion.9), channel_id=1, source_target_pairs={{0,32},{16,48},{32,64},{48,80},{64,96},{80,112},{96,128},{112,144}... | collective-permute-start | bytes 49160 | tf_op jit(solution)/shard_map/ppermute | solution.py:14
  130.1 1.4 collective-permute-done.3
  131.6 6.4 %collective-permute-start.4 = (f32[16,256]{1,0:T(8,128)S(1)}, f32[16,256]{1,0:T(8,128)S(1)}, u32[]{:S(2)}, u32[]{:S(2)}) collective-permute-start(f32[16,256]{1,0:T(8,128)S(1)} %multiply_add_fusion.8), channel_id=1, source_target_pairs={{0,64},{16,80},{32,96},{48,112},{64,128},{80,144},{96,160},{112,17... | collective-permute-start | bytes 49160 | tf_op jit(solution)/shard_map/ppermute | solution.py:14
  138.0 1.4 collective-permute-done.4
  139.4 11.8 %collective-permute-start.5 = (f32[16,256]{1,0:T(8,128)S(1)}, f32[16,256]{1,0:T(8,128)S(1)}, u32[]{:S(2)}, u32[]{:S(2)}) collective-permute-start(f32[16,256]{1,0:T(8,128)S(1)} %multiply_add_fusion.7), channel_id=1, source_target_pairs={{0,128},{16,144},{32,160},{48,176},{64,192},{80,208},{96,224},{112... | collective-permute-start | bytes 49160 | tf_op jit(solution)/shard_map/ppermute | solution.py:14
  151.2 1.4 collective-permute-done.5
  152.7 13.8 %collective-permute-start.6 = (f32[16,256]{1,0:T(8,128)S(1)}, f32[16,256]{1,0:T(8,128)S(1)}, u32[]{:S(2)}, u32[]{:S(2)}) collective-permute-start(f32[16,256]{1,0:T(8,128)S(1)} %multiply_add_fusion.6), channel_id=1, source_target_pairs={{0,256},{16,272},{32,288},{48,304},{64,320},{80,336},{96,352},{112... | collective-permute-start | bytes 49160 | tf_op jit(solution)/shard_map/ppermute | solution.py:14
  166.5 1.4 collective-permute-done.6
  168.0 1.6 multiply_reduce_fusion
  169.7 3.8 %fusion.13 = f32[64,64,256]{2,1,0:T(8,128)} fusion(s32[64,64]{1,0:T(8,128)S(1)} %iota_subtract_fusion, f32[64,256]{0,1:T(8,128)S(1)} %multiply_reduce_fusion), kind=kOutput, calls=%fused_computation.28 | convolution fusion | flops 805568512 | bytes 4276224 | tf_op jit(solution)/shard_map/dot_general | solution.py:36
  173.5 9.2 %copy.44 = f32[64,64,256]{1,0,2:T(8,128)} copy(f32[64,64,256]{2,1,0:T(8,128)} %fusion.13) | data formatting | bytes 8388608 | tf_op jit(solution)/shard_map/dot_general | solution.py:36
  182.7 10.3 %fusion.28 = f32[256,32,64]{2,1,0:T(8,128)} fusion(bf16[32,64,256]{1,0,2:T(8,128)(2,1)S(1)} %copy.43, f32[64,64,256]{1,0,2:T(8,128)} %copy.44), kind=kOutput, calls=%fused_computation.67 | convolution fusion | flops 402653184 | bytes 7340032 | tf_op jit(solution)/shard_map/ijc,kjc->kic/dot_general | solution.py:76
  193.0 12.4 %add_bitcast_fusion = f32[32,64,256]{1,0,2:T(8,128)} fusion(f32[256,32,64]{2,1,0:T(8,128)} %fusion.28, f32[32,16,256]{0,1,2:T(8,128)} %copy-done, f32[64]{0:T(128)S(1)} %broadcast_add_fusion, f32[16,256]{0,1:T(8,128)S(1)} %copy.54, f32[32]{0:T(128)S(1)} %convert_multiply_fusion.1, f32[16,256]{0,1:T(8,128)S(1)} %copy.41, f32[16,256]{0,1:T(8,128)S(1)} %copy.40), kind=kOutput, calls=%fused_computation.1 | convolution fusion | flops 102105088 | bytes 4768128 | tf_op jit(solution)/shard_map/nic,knc->kic/dot_general | solution.py:79
  205.5 3.6 %copy.55 = f32[32,64,256]{2,1,0:T(8,128)S(1)} copy(f32[32,64,256]{1,0,2:T(8,128)} %add_bitcast_fusion) | data formatting | bytes 4194304 | tf_op jit(solution)/shard_map/add | solution.py:80
  209.3 1.5 fusion.1
  210.8 20.2 %all_to_all.37 = bf16[16,128,256]{2,1,0:T(8,128)(2,1)S(1)} all-to-all(bf16[16,128,256]{2,1,0:T(8,128)(2,1)S(1)} %bitcast.57), channel_id=1, replica_groups=mesh['seq'=32,'chan'=16] {'chan'}, dimensions={0} | all-to-all | bytes 2097152 | tf_op jit(solution)/shard_map/all_to_all | solution.py:99
  231.1 1.1 copy.62
  (34 shorter events, 2.5 us)
Async XLA Ops:
  7.2 11.8 %copy-start.2 = (f32[16,256]{1,0:T(8,128)S(1)}, f32[16,256]{1,0:T(8,128)}, u32[]{:S(2)}) copy-start(f32[16,256]{1,0:T(8,128)} %param.7) | copy-start | bytes 49156
  7.2 61.8 %all-to-all-start = ((bf16[3,128,4096]{1,0,2:T(4,128)(2,1)}), bf16[3,128,4096]{1,0,2:T(4,128)(2,1)}, u32[]{:S(2)}, u32[]{:S(2)}) async-start(bf16[3,128,4096]{1,0,2:T(4,128)(2,1)} %copy.38), calls=%async_computation | async-start | bytes 8388608 | tf_op jit(solution)/shard_map/all_to_all | solution.py:87
  75.1 6.3 %collective-permute-start = (bf16[3,2,256]{2,1,0:T(2,128)(2,1)}, bf16[3,2,256]{2,1,0:T(2,128)(2,1)}, u32[]{:S(2)}, u32[]{:S(2)}) collective-permute-start(bf16[3,2,256]{2,1,0:T(2,128)(2,1)} %slice.68), channel_id=1, source_target_pairs={{0,16},{16,32},{32,48},{48,64},{64,80},{80,96},{96,112},{112,128},... | collective-permute-start | bytes 9224 | tf_op jit(solution)/shard_map/ppermute | solution.py:14
  84.7 1.6 copy-start.1
  95.4 0.9 copy-start.5
  96.3 1.8 copy-start.4
  98.1 1.3 copy-start.3
  103.4 1.3 copy-start
  106.6 61.3 %copy-start.6 = (f32[16,256]{1,0:T(8,128)S(1)}, f32[16,256]{1,0:T(8,128)}, u32[]{:S(2)}) copy-start(f32[16,256]{1,0:T(8,128)} %param.8) | copy-start | bytes 49156
  111.7 12.8 %collective-permute-start.1 = (f32[16,256]{1,0:T(8,128)S(1)}, f32[16,256]{1,0:T(8,128)S(1)}, u32[]{:S(2)}, u32[]{:S(2)}) collective-permute-start(f32[16,256]{1,0:T(8,128)S(1)} %bitcast_add_fusion.1), channel_id=1, source_target_pairs={{0,16},{16,32},{32,48},{48,64},{64,80},{80,96},{96,112},{112,128},... | collective-permute-start | bytes 49160 | tf_op jit(solution)/shard_map/ppermute | solution.py:14
  120.6 5.3 %collective-permute-start.2 = (f32[16,256]{1,0:T(8,128)S(1)}, f32[16,256]{1,0:T(8,128)S(1)}, u32[]{:S(2)}, u32[]{:S(2)}) collective-permute-start(f32[16,256]{1,0:T(8,128)S(1)} %bitcast_add_fusion.1), channel_id=1, source_target_pairs={{0,32},{16,48},{32,64},{48,80},{64,96},{80,112},{96,128},{112,144}... | collective-permute-start | bytes 49160 | tf_op jit(solution)/shard_map/ppermute | solution.py:14
  125.9 5.6 %collective-permute-start.3 = (f32[16,256]{1,0:T(8,128)S(1)}, f32[16,256]{1,0:T(8,128)S(1)}, u32[]{:S(2)}, u32[]{:S(2)}) collective-permute-start(f32[16,256]{1,0:T(8,128)S(1)} %multiply_add_fusion.9), channel_id=1, source_target_pairs={{0,32},{16,48},{32,64},{48,80},{64,96},{80,112},{96,128},{112,144}... | collective-permute-start | bytes 49160 | tf_op jit(solution)/shard_map/ppermute | solution.py:14
  131.6 7.8 %collective-permute-start.4 = (f32[16,256]{1,0:T(8,128)S(1)}, f32[16,256]{1,0:T(8,128)S(1)}, u32[]{:S(2)}, u32[]{:S(2)}) collective-permute-start(f32[16,256]{1,0:T(8,128)S(1)} %multiply_add_fusion.8), channel_id=1, source_target_pairs={{0,64},{16,80},{32,96},{48,112},{64,128},{80,144},{96,160},{112,17... | collective-permute-start | bytes 49160 | tf_op jit(solution)/shard_map/ppermute | solution.py:14
  139.4 13.2 %collective-permute-start.5 = (f32[16,256]{1,0:T(8,128)S(1)}, f32[16,256]{1,0:T(8,128)S(1)}, u32[]{:S(2)}, u32[]{:S(2)}) collective-permute-start(f32[16,256]{1,0:T(8,128)S(1)} %multiply_add_fusion.7), channel_id=1, source_target_pairs={{0,128},{16,144},{32,160},{48,176},{64,192},{80,208},{96,224},{112... | collective-permute-start | bytes 49160 | tf_op jit(solution)/shard_map/ppermute | solution.py:14
  152.7 15.3 %collective-permute-start.6 = (f32[16,256]{1,0:T(8,128)S(1)}, f32[16,256]{1,0:T(8,128)S(1)}, u32[]{:S(2)}, u32[]{:S(2)}) collective-permute-start(f32[16,256]{1,0:T(8,128)S(1)} %multiply_add_fusion.6), channel_id=1, source_target_pairs={{0,256},{16,272},{32,288},{48,304},{64,320},{80,336},{96,352},{112... | collective-permute-start | bytes 49160 | tf_op jit(solution)/shard_map/ppermute | solution.py:14
  205.5 3.6 %copy-start.7 = (f32[256]{0:T(256)S(1)}, f32[256]{0:T(256)}, u32[]{:S(2)}) copy-start(f32[256]{0:T(256)} %param.9) | copy-start | bytes 3076

commit v3 on v2

--- a/solution.py
+++ b/solution.py
@@ -48,7 +48,7 @@
     return jnp.concatenate([padding, values[: values.shape[0] - distance]], axis=0)
 
 
-def long_part(product, decay_rate, residue, skip_gain):
+def long_part(product, decay_rate, residue, skip_gain, passenger):
     signal = product.astype(jnp.float32)
     section = signal.shape[0]
     block = math.gcd(section, block_len)
@@ -63,6 +63,7 @@
         starts = starts + jnp.exp(-decay_rate * float(block * step)) * shifted(starts, step)
         step *= 2
     end_state = jnp.exp(-decay_rate * float(block)) * starts[count - 1] + local_end[count - 1]
+    end_state, passenger = lax.optimization_barrier((end_state, passenger))
     sections = lax.axis_size("seq")
     incoming = from_behind(end_state, "seq", 1)
     if sections > 2:
@@ -78,24 +79,34 @@
     starts = starts + jnp.exp(-decay_rate[None, :, :] * block_starts) * incoming[None, :, :]
     carried = jnp.einsum("nic,knc->kic", reading, starts, precision=lax.Precision.HIGHEST)
     longconv = (inner + carried).reshape(signal.shape)
-    return (longconv + skip_gain[None, :] * signal).astype(jnp.bfloat16)
+    return (longconv + skip_gain[None, :] * signal).astype(jnp.bfloat16), passenger
 
 
 def local(features, short_weight, decay_rate, residue, skip_gain):
     taps = short_weight.shape[1]
     chan_width = decay_rate.shape[1]
-    columns = lax.all_to_all(features, "chan", split_axis=2, concat_axis=1, tiled=True)
-    border = from_behind(columns[:, columns.shape[1] - (taps - 1) :, :], "seq", 1)
     weights = lax.dynamic_slice_in_dim(
         short_weight, lax.axis_index("chan") * chan_width, chan_width, 2
     )
-    padded = jnp.concatenate([border, columns], axis=1)
-    filtered = lax.optimization_barrier(short_filter(padded, weights, taps).astype(jnp.bfloat16))
+
+    def arrive(streams):
+        columns = lax.all_to_all(streams, "chan", split_axis=2, concat_axis=1, tiled=True)
+        border = from_behind(columns[:, columns.shape[1] - (taps - 1) :, :], "seq", 1)
+        return jnp.concatenate([border, columns], axis=1)
+
+    keys_values = arrive(features[1:])
+    keys_values, queries = lax.optimization_barrier((keys_values, features[:1]))
+    queries = arrive(queries)
+    gates = short_filter(keys_values, weights[1:], taps).astype(jnp.bfloat16)
+    gates = lax.optimization_barrier(gates)
     product = lax.optimization_barrier(
-        (filtered[1].astype(jnp.float32) * filtered[2].astype(jnp.float32)).astype(jnp.bfloat16)
+        (gates[0].astype(jnp.float32) * gates[1].astype(jnp.float32)).astype(jnp.bfloat16)
     )
-    conv_out = lax.optimization_barrier(long_part(product, decay_rate, residue, skip_gain))
-    gated = (filtered[0].astype(jnp.float32) * conv_out.astype(jnp.float32)).astype(jnp.bfloat16)
+    conv_out, queries = lax.optimization_barrier(
+        long_part(product, decay_rate, residue, skip_gain, queries)
+    )
+    query = short_filter(queries, weights[:1], taps).astype(jnp.bfloat16)[0]
+    gated = (query.astype(jnp.float32) * conv_out.astype(jnp.float32)).astype(jnp.bfloat16)
     return lax.all_to_all(gated, "chan", split_axis=0, concat_axis=1, tiled=True)
 
 

time: 233 us -> 245 us (1.052)
  waiting for transfers between devices: 56.5 us -> 31.4 us
  other arithmetic: 15.2 us -> 38.6 us
  starting transfers between devices: 61.2 us -> 70.5 us
  local copies, waits for them, and re-layouts: 48.3 us -> 54.5 us
  blocking collectives: 20.2 us -> 17.6 us
    all_to_all x1 -> x2, waiting for transfers between devices: 49.4 us -> 24.4 us  [arrive(): lax.all_to_all(streams, 'chan', split_axis=2, concat_axis=1, tiled=True)]
    unnamed x0 -> x1, other arithmetic: none -> 23.5 us
    all_to_all x1 -> x2, starting transfers between devices: 10.3 us -> 16 us  [arrive(): lax.all_to_all(streams, 'chan', split_axis=2, concat_axis=1, tiled=True)]
    optimization_barrier x0 -> x1, local copies, waits for them, and re-layouts: none -> 3.9 us  [local(): keys_values, queries = lax.optimization_barrier((keys_values, features[:1]))]
    ppermute x7 -> x8, starting transfers between devices: 50.9 us -> 54.6 us  [from_behind(): return lax.ppermute(block, axis, route)]
    all_to_all x1, blocking collectives: 20.2 us -> 17.6 us  [local(): lax.all_to_all(gated, 'chan', split_axis=0, concat_axis=1, tiled=True)]
    unnamed x19 -> x31, local copies, waits for them, and re-layouts: 11.4 us -> 10.2 us
    all_to_all x1 -> x2, local copies, waits for them, and re-layouts: 5.5 us -> 5.25 us  [arrive(): lax.all_to_all(streams, 'chan', split_axis=2, concat_axis=1, tiled=True)]
  transfers between devices with their start and end apart: 8 -> 10, of which waited for: 6 -> 7; matrix products, arithmetic and copies ran while one was open for 3% -> 9% of each run, Pallas kernels for 0% -> 0%
where the time goes in v3:
time: 245 us; the launch traced here: 244 us
  starting transfers between devices  70.5 us (29%)
  local copies, waits for them, and re-layouts  54.5 us (22%)
  other arithmetic  38.6 us (16%)
  matrix products  31.6 us (13%)
  waiting for transfers between devices  31.4 us (13%)
  blocking collectives  17.6 us (7%)
    ppermute x8, starting transfers between devices, from_behind(): return lax.ppermute(block, axis, route)  54.6 us
    all_to_all x2, waiting for transfers between devices, arrive(): lax.all_to_all(streams, 'chan', split_axis=2, concat_axis=1, tiled=True)  24.4 us
    unnamed x1, other arithmetic  23.5 us
    all_to_all x1, blocking collectives, local(): lax.all_to_all(gated, 'chan', split_axis=0, concat_axis=1, tiled=True)  17.6 us
    all_to_all x2, starting transfers between devices, arrive(): lax.all_to_all(streams, 'chan', split_axis=2, concat_axis=1, tiled=True)  16 us
    dot_general x1, matrix products, long_part(): jnp.einsum('nic,knc->kic', reading, starts, precision=lax.Precision.HIGHEST)  12.4 us
    dot_general x1, matrix products, long_part(): jnp.einsum('ijc,kjc->kic', toeplitz, pieces, precision=lax.Precision.HIGH...  10.3 us
    unnamed x31, local copies, waits for them, and re-layouts  10.2 us
  transfers between devices with their start and end apart: 10, of which 7 were waited for; matrix products, arithmetic and copies ran while one was open for 9% of the time, Pallas kernels for 0%

profile of v3, /device:TPU:2, one launch (start us, length us, event | category | flops | bytes accessed | tf_op | source)
XLA Modules:
  0.0 244.5 jit_solution(15128718562046589440)
XLA Ops:
  0.0 1.6 slice-done
  1.6 3.8 %copy.89 = bf16[2,128,4096]{1,0,2:T(2,128)(2,1)} copy(bf16[2,128,4096]{2,1,0:T(8,128)(2,1)S(1)} %slice-done) | data formatting | bytes 4194304
  5.3 9.5 %all-to-all-start = ((bf16[2,128,4096]{1,0,2:T(2,128)(2,1)}), bf16[2,128,4096]{1,0,2:T(2,128)(2,1)S(1)}, u32[]{:S(2)}, u32[]{:S(2)}) async-start(bf16[2,128,4096]{1,0,2:T(2,128)(2,1)} %copy.89), calls=%async_computation | async-start | bytes 4194304 | tf_op jit(solution)/shard_map/all_to_all | solution.py:93
  15.8 24.4 %all-to-all-done = bf16[2,128,4096]{1,0,2:T(2,128)(2,1)S(1)} async-done(((bf16[2,128,4096]{1,0,2:T(2,128)(2,1)}), bf16[2,128,4096]{1,0,2:T(2,128)(2,1)S(1)}, u32[]{:S(2)}, u32[]{:S(2)}) %all-to-all-start) | async-done | bytes 2097184 | tf_op jit(solution)/shard_map/all_to_all | solution.py:93
  40.2 1.3 copy-done.4
  41.5 4.7 %copy.63 = bf16[2,128,16,256]{3,1,2,0:T(8,128)(2,1)S(1)} copy(bf16[2,128,16,256]{1,0,3,2:T(2,128)(2,1)} %bitcast.67) | data formatting | bytes 4194304 | tf_op jit(solution)/shard_map/all_to_all | solution.py:93
  46.3 1.4 collective-permute-start
  47.7 3.9 %copy.90 = bf16[1,128,4096]{1,0,2:T(2,128)(2,1)} copy(bf16[1,128,4096]{2,1,0:T(8,128)(2,1)S(1)} %slice-done.1) | data formatting | bytes 2097152 | tf_op jit(solution)/shard_map/optimization_barrier | solution.py:98
  55.3 1.4 add_convert_fusion
  57.1 1.0 copy-done.2
  58.0 3.8 %copy.68 = bf16[32,64,256]{1,0,2:T(8,128)(2,1)} copy(bf16[32,64,256]{2,1,0:T(8,128)(2,1)S(1)} %bitcast.63) | data formatting | bytes 2097152 | tf_op jit(solution)/shard_map/reshape | solution.py:58
  61.8 5.0 %fusion.13 = f32[32,16,256]{0,1,2:T(8,128)S(1)} fusion(bf16[32,64,256]{1,0,2:T(8,128)(2,1)} %copy.68, f32[64]{0:T(128)S(1)} %broadcast_subtract_fusion, f32[16,256]{0,1:T(8,128)S(1)} %copy.66), kind=kOutput, calls=%fused_computation.28 | convolution fusion | flops 100925440 | bytes 1589504 | tf_op jit(solution)/shard_map/njc,kjc->knc/dot_general | solution.py:59
  66.9 1.9 slice.121
  68.8 2.0 pad_slice_fusion
  71.3 23.5 %reduce = bf16[4096,128]{1,0:T(8,128)(2,1)S(1)} reduce(bf16[4096,1,128]{2,1,0:T(2,128)(2,1)} %bitcast.68, bf16[]{:T(256)} %broadcast.57), dimensions={1}, to_apply=%bitcast.46.reduce_sub_computation | reduce | bytes 2097154
  94.8 1.1 reshape.77
  96.0 6.4 %all-to-all-start.1 = ((bf16[16,2,16384]{2,1,0:T(2,128)(2,1)}), bf16[16,2,16384]{2,1,0:T(2,128)(2,1)S(1)}, u32[]{:S(2)}, u32[]{:S(2)}) async-start(bf16[16,2,16384]{2,1,0:T(2,128)(2,1)} %reshape.77), calls=%async_computation.1 | async-start | bytes 2097152 | tf_op jit(solution)/shard_map/all_to_all | solution.py:93
  102.4 3.1 %multiply_add_fusion.4 = f32[32,16,256]{0,1,2:T(8,128)S(1)} fusion(f32[31,16,256]{0,1,2:T(8,128)} %pad_slice_fusion, f32[31,16,256]{0,1,2:T(8,128)S(1)} %bitcast.58, f32[16,256]{0,1:T(8,128)} %copy.71), kind=kLoop, calls=%fused_computation.19 | loop fusion | flops 262144 | bytes 1556480 | tf_op jit(solution)/shard_map/add | solution.py:63
  105.5 1.3 multiply_add_fusion.3
  106.8 1.3 multiply_add_fusion.2
  108.0 1.3 multiply_add_fusion.1
  109.3 1.3 multiply_add_fusion
  110.6 1.3 copy-done.1
  111.9 1.9 slice.120
  113.8 2.7 %copy.77 = f32[1,16,256]{2,1,0:T(8,128)S(1)} copy(f32[1,16,256]{0,1,2:T(8,128)} %slice.120) | data formatting | bytes 32768 | tf_op jit(solution)/shard_map/slice | solution.py:65
  116.5 1.0 copy.78
  117.5 1.0 reshape.78
  119.3 5.9 %collective-permute-start.1 = (bf16[1,2,256]{2,1,0:T(2,128)(2,1)S(1)}, bf16[1,2,256]{2,1,0:T(2,128)(2,1)S(1)}, u32[]{:S(2)}, u32[]{:S(2)}) collective-permute-start(bf16[1,2,256]{2,1,0:T(2,128)(2,1)S(1)} %slice.122), channel_id=1, source_target_pairs={{0,16},{16,32},{32,48},{48,64},{64,80},{80,96},{96,112},{112,128},... | collective-permute-start | bytes 3080 | tf_op jit(solution)/shard_map/ppermute | solution.py:14
  126.3 3.3 %collective-permute-start.2 = (f32[16,256]{1,0:T(8,128)S(1)}, f32[16,256]{1,0:T(8,128)S(1)}, u32[]{:S(2)}, u32[]{:S(2)}) collective-permute-start(f32[16,256]{1,0:T(8,128)S(1)} %bitcast_add_fusion.1), channel_id=1, source_target_pairs={{0,16},{16,32},{32,48},{48,64},{64,80},{80,96},{96,112},{112,128},... | collective-permute-start | bytes 49160 | tf_op jit(solution)/shard_map/ppermute | solution.py:14
  129.6 4.1 %collective-permute-start.3 = (f32[16,256]{1,0:T(8,128)S(1)}, f32[16,256]{1,0:T(8,128)S(1)}, u32[]{:S(2)}, u32[]{:S(2)}) collective-permute-start(f32[16,256]{1,0:T(8,128)S(1)} %bitcast_add_fusion.1), channel_id=1, source_target_pairs={{0,32},{16,48},{32,64},{48,80},{64,96},{80,112},{96,128},{112,144}... | collective-permute-start | bytes 49160 | tf_op jit(solution)/shard_map/ppermute | solution.py:14
  133.7 1.4 collective-permute-done.3
  135.1 4.2 %collective-permute-start.4 = (f32[16,256]{1,0:T(8,128)S(1)}, f32[16,256]{1,0:T(8,128)S(1)}, u32[]{:S(2)}, u32[]{:S(2)}) collective-permute-start(f32[16,256]{1,0:T(8,128)S(1)} %multiply_add_fusion.9), channel_id=1, source_target_pairs={{0,32},{16,48},{32,64},{48,80},{64,96},{80,112},{96,128},{112,144}... | collective-permute-start | bytes 49160 | tf_op jit(solution)/shard_map/ppermute | solution.py:14
  140.7 7.2 %collective-permute-start.5 = (f32[16,256]{1,0:T(8,128)S(1)}, f32[16,256]{1,0:T(8,128)S(1)}, u32[]{:S(2)}, u32[]{:S(2)}) collective-permute-start(f32[16,256]{1,0:T(8,128)S(1)} %multiply_add_fusion.8), channel_id=1, source_target_pairs={{0,64},{16,80},{32,96},{48,112},{64,128},{80,144},{96,160},{112,17... | collective-permute-start | bytes 49160 | tf_op jit(solution)/shard_map/ppermute | solution.py:14
  148.0 1.4 collective-permute-done.5
  149.4 12.2 %collective-permute-start.6 = (f32[16,256]{1,0:T(8,128)S(1)}, f32[16,256]{1,0:T(8,128)S(1)}, u32[]{:S(2)}, u32[]{:S(2)}) collective-permute-start(f32[16,256]{1,0:T(8,128)S(1)} %multiply_add_fusion.7), channel_id=1, source_target_pairs={{0,128},{16,144},{32,160},{48,176},{64,192},{80,208},{96,224},{112... | collective-permute-start | bytes 49160 | tf_op jit(solution)/shard_map/ppermute | solution.py:14
  161.6 1.4 collective-permute-done.6
  163.1 16.2 %collective-permute-start.7 = (f32[16,256]{1,0:T(8,128)S(1)}, f32[16,256]{1,0:T(8,128)S(1)}, u32[]{:S(2)}, u32[]{:S(2)}) collective-permute-start(f32[16,256]{1,0:T(8,128)S(1)} %multiply_add_fusion.6), channel_id=1, source_target_pairs={{0,256},{16,272},{32,288},{48,304},{64,320},{80,336},{96,352},{112... | collective-permute-start | bytes 49160 | tf_op jit(solution)/shard_map/ppermute | solution.py:14
  179.3 1.4 collective-permute-done.7
  180.9 1.6 multiply_reduce_fusion
  182.5 3.8 %fusion.12 = f32[64,64,256]{2,1,0:T(8,128)} fusion(s32[64,64]{1,0:T(8,128)S(1)} %iota_subtract_fusion, f32[64,256]{0,1:T(8,128)S(1)} %multiply_reduce_fusion), kind=kOutput, calls=%fused_computation.26 | convolution fusion | flops 805568512 | bytes 4276224 | tf_op jit(solution)/shard_map/dot_general | solution.py:36
  186.3 9.3 %copy.69 = f32[64,64,256]{1,0,2:T(8,128)} copy(f32[64,64,256]{2,1,0:T(8,128)} %fusion.12) | data formatting | bytes 8388608 | tf_op jit(solution)/shard_map/dot_general | solution.py:36
  195.6 10.3 %fusion.28 = f32[256,32,64]{2,1,0:T(8,128)} fusion(bf16[32,64,256]{1,0,2:T(8,128)(2,1)S(1)} %copy-done, f32[64,64,256]{1,0,2:T(8,128)} %copy.69), kind=kOutput, calls=%fused_computation.67 | convolution fusion | flops 402653184 | bytes 7340032 | tf_op jit(solution)/shard_map/ijc,kjc->kic/dot_general | solution.py:77
  206.0 12.4 %add_bitcast_fusion = f32[32,64,256]{1,0,2:T(8,128)} fusion(f32[256,32,64]{2,1,0:T(8,128)} %fusion.28, f32[32,16,256]{0,1,2:T(8,128)} %copy-done.1, f32[64]{0:T(128)S(1)} %broadcast_add_fusion, f32[16,256]{0,1:T(8,128)S(1)} %copy.80, f32[32]{0:T(128)S(1)} %convert_multiply_fusion.1, f32[16,256]{0,1:T(8,128)S(1)} %copy.66, f32[16,256]{0,1:T(8,128)S(1)} %copy.65), kind=kOutput, calls=%fused_computation | convolution fusion | flops 102105088 | bytes 4768128 | tf_op jit(solution)/shard_map/nic,knc->kic/dot_general | solution.py:80
  218.4 4.6 %copy.81 = f32[32,64,256]{2,1,0:T(8,128)} copy(f32[32,64,256]{1,0,2:T(8,128)} %add_bitcast_fusion) | data formatting | bytes 4194304 | tf_op jit(solution)/shard_map/add | solution.py:81
  223.1 1.8 fusion.1
  224.9 0.9 fusion
  225.8 17.6 %all_to_all.55 = bf16[16,128,256]{2,1,0:T(8,128)(2,1)S(1)} all-to-all(bf16[16,128,256]{2,1,0:T(8,128)(2,1)S(1)} %bitcast.73), channel_id=1, replica_groups=mesh['seq'=32,'chan'=16] {'chan'}, dimensions={0} | all-to-all | bytes 2097152 | tf_op jit(solution)/shard_map/all_to_all | solution.py:110
  243.4 1.1 copy.91
  (61 shorter events, 8.9 us)
Async XLA Ops:
  0.0 1.6 slice-start
  5.3 10.4 %copy-start.6 = (f32[16,256]{1,0:T(8,128)S(1)}, f32[16,256]{1,0:T(8,128)}, u32[]{:S(2)}) copy-start(f32[16,256]{1,0:T(8,128)} %param.7) | copy-start | bytes 49156
  5.3 34.8 %all-to-all-start = ((bf16[2,128,4096]{1,0,2:T(2,128)(2,1)}), bf16[2,128,4096]{1,0,2:T(2,128)(2,1)S(1)}, u32[]{:S(2)}, u32[]{:S(2)}) async-start(bf16[2,128,4096]{1,0,2:T(2,128)(2,1)} %copy.89), calls=%async_computation | async-start | bytes 4194304 | tf_op jit(solution)/shard_map/all_to_all | solution.py:93
  40.2 1.3 copy-start.4
  46.2 1.5 slice-start.1
  46.3 8.6 %collective-permute-start = (bf16[2,2,256]{2,1,0:T(2,128)(2,1)S(1)}, bf16[2,2,256]{2,1,0:T(2,128)(2,1)S(1)}, u32[]{:S(2)}, u32[]{:S(2)}) collective-permute-start(bf16[2,2,256]{2,1,0:T(2,128)(2,1)S(1)} %slice.112), channel_id=1, source_target_pairs={{0,16},{16,32},{32,48},{48,64},{64,80},{80,96},{96,112},{112,128},... | collective-permute-start | bytes 6152 | tf_op jit(solution)/shard_map/ppermute | solution.py:14
  57.1 1.0 copy-start.2
  96.0 21.5 %all-to-all-start.1 = ((bf16[16,2,16384]{2,1,0:T(2,128)(2,1)}), bf16[16,2,16384]{2,1,0:T(2,128)(2,1)S(1)}, u32[]{:S(2)}, u32[]{:S(2)}) async-start(bf16[16,2,16384]{2,1,0:T(2,128)(2,1)} %reshape.77), calls=%async_computation.1 | async-start | bytes 2097152 | tf_op jit(solution)/shard_map/all_to_all | solution.py:93
  102.4 3.1 %copy-start.9 = (f32[16,256]{0,1:T(8,128)S(1)}, f32[16,256]{0,1:T(8,128)}, u32[]{:S(2)}) copy-start(f32[16,256]{0,1:T(8,128)} %copy.72) | copy-start | bytes 49156
  105.5 1.3 copy-start.8
  108.0 1.3 copy-start.7
  110.6 1.3 copy-start.1
  113.8 2.7 %copy-start.5 = (f32[1,16,256]{0,1,2:T(8,128)S(1)}, f32[1,16,256]{0,1,2:T(8,128)}, u32[]{:S(2)}) copy-start(f32[1,16,256]{0,1,2:T(8,128)} %slice.121) | copy-start | bytes 49156
  118.7 62.0 %copy-start.10 = (f32[16,256]{1,0:T(8,128)S(1)}, f32[16,256]{1,0:T(8,128)}, u32[]{:S(2)}) copy-start(f32[16,256]{1,0:T(8,128)} %param.8) | copy-start | bytes 49156
  119.3 6.7 %collective-permute-start.1 = (bf16[1,2,256]{2,1,0:T(2,128)(2,1)S(1)}, bf16[1,2,256]{2,1,0:T(2,128)(2,1)S(1)}, u32[]{:S(2)}, u32[]{:S(2)}) collective-permute-start(bf16[1,2,256]{2,1,0:T(2,128)(2,1)S(1)} %slice.122), channel_id=1, source_target_pairs={{0,16},{16,32},{32,48},{48,64},{64,80},{80,96},{96,112},{112,128},... | collective-permute-start | bytes 3080 | tf_op jit(solution)/shard_map/ppermute | solution.py:14
  126.3 7.4 %collective-permute-start.2 = (f32[16,256]{1,0:T(8,128)S(1)}, f32[16,256]{1,0:T(8,128)S(1)}, u32[]{:S(2)}, u32[]{:S(2)}) collective-permute-start(f32[16,256]{1,0:T(8,128)S(1)} %bitcast_add_fusion.1), channel_id=1, source_target_pairs={{0,16},{16,32},{32,48},{48,64},{64,80},{80,96},{96,112},{112,128},... | collective-permute-start | bytes 49160 | tf_op jit(solution)/shard_map/ppermute | solution.py:14
  129.6 5.5 %collective-permute-start.3 = (f32[16,256]{1,0:T(8,128)S(1)}, f32[16,256]{1,0:T(8,128)S(1)}, u32[]{:S(2)}, u32[]{:S(2)}) collective-permute-start(f32[16,256]{1,0:T(8,128)S(1)} %bitcast_add_fusion.1), channel_id=1, source_target_pairs={{0,32},{16,48},{32,64},{48,80},{64,96},{80,112},{96,128},{112,144}... | collective-permute-start | bytes 49160 | tf_op jit(solution)/shard_map/ppermute | solution.py:14
  135.1 5.6 %collective-permute-start.4 = (f32[16,256]{1,0:T(8,128)S(1)}, f32[16,256]{1,0:T(8,128)S(1)}, u32[]{:S(2)}, u32[]{:S(2)}) collective-permute-start(f32[16,256]{1,0:T(8,128)S(1)} %multiply_add_fusion.9), channel_id=1, source_target_pairs={{0,32},{16,48},{32,64},{48,80},{64,96},{80,112},{96,128},{112,144}... | collective-permute-start | bytes 49160 | tf_op jit(solution)/shard_map/ppermute | solution.py:14
  140.7 8.7 %collective-permute-start.5 = (f32[16,256]{1,0:T(8,128)S(1)}, f32[16,256]{1,0:T(8,128)S(1)}, u32[]{:S(2)}, u32[]{:S(2)}) collective-permute-start(f32[16,256]{1,0:T(8,128)S(1)} %multiply_add_fusion.8), channel_id=1, source_target_pairs={{0,64},{16,80},{32,96},{48,112},{64,128},{80,144},{96,160},{112,17... | collective-permute-start | bytes 49160 | tf_op jit(solution)/shard_map/ppermute | solution.py:14
  149.4 13.6 %collective-permute-start.6 = (f32[16,256]{1,0:T(8,128)S(1)}, f32[16,256]{1,0:T(8,128)S(1)}, u32[]{:S(2)}, u32[]{:S(2)}) collective-permute-start(f32[16,256]{1,0:T(8,128)S(1)} %multiply_add_fusion.7), channel_id=1, source_target_pairs={{0,128},{16,144},{32,160},{48,176},{64,192},{80,208},{96,224},{112... | collective-permute-start | bytes 49160 | tf_op jit(solution)/shard_map/ppermute | solution.py:14
  163.1 17.7 %collective-permute-start.7 = (f32[16,256]{1,0:T(8,128)S(1)}, f32[16,256]{1,0:T(8,128)S(1)}, u32[]{:S(2)}, u32[]{:S(2)}) collective-permute-start(f32[16,256]{1,0:T(8,128)S(1)} %multiply_add_fusion.6), channel_id=1, source_target_pairs={{0,256},{16,272},{32,288},{48,304},{64,320},{80,336},{96,352},{112... | collective-permute-start | bytes 49160 | tf_op jit(solution)/shard_map/ppermute | solution.py:14
  186.3 9.3 %copy-start = (bf16[32,64,256]{1,0,2:T(8,128)(2,1)S(1)}, bf16[32,64,256]{1,0,2:T(8,128)(2,1)}, u32[]{:S(2)}) copy-start(bf16[32,64,256]{1,0,2:T(8,128)(2,1)} %copy.68) | copy-start | bytes 3145732
  218.4 4.6 %copy-start.3 = (bf16[2048,256]{1,0:T(8,128)(2,1)S(1)}, bf16[2048,256]{1,0:T(8,128)(2,1)}, u32[]{:S(2)}) copy-start(bf16[2048,256]{1,0:T(8,128)(2,1)} %copy-done.2) | copy-start | bytes 3145732
  218.4 4.6 %copy-start.11 = (f32[256]{0:T(256)S(1)}, f32[256]{0:T(256)}, u32[]{:S(2)}) copy-start(f32[256]{0:T(256)} %param.9) | copy-start | bytes 3076

commit v4 on v3

--- a/solution.py
+++ b/solution.py
@@ -95,8 +95,11 @@
         return jnp.concatenate([border, columns], axis=1)
 
     keys_values = arrive(features[1:])
-    keys_values, queries = lax.optimization_barrier((keys_values, features[:1]))
-    queries = arrive(queries)
+    keys_values, queries = lax.optimization_barrier((keys_values, features[0]))
+    queries = lax.all_to_all(queries, "chan", split_axis=1, concat_axis=0, tiled=True)
+    queries = queries[None]
+    border = from_behind(queries[:, queries.shape[1] - (taps - 1) :, :], "seq", 1)
+    queries = jnp.concatenate([border, queries], axis=1)
     gates = short_filter(keys_values, weights[1:], taps).astype(jnp.bfloat16)
     gates = lax.optimization_barrier(gates)
     product = lax.optimization_barrier(

time: 245 us -> 216 us (0.88)
  other arithmetic: 38.6 us -> 16.3 us
  local copies, waits for them, and re-layouts: 54.5 us -> 49.6 us
    unnamed x1 -> x0, other arithmetic: 23.5 us -> none
    all_to_all x0 -> x1, starting transfers between devices: none -> 6.44 us  [local(): lax.all_to_all(queries, 'chan', split_axis=1, concat_axis=0, tiled=True)]
    all_to_all x2 -> x1, starting transfers between devices: 16 us -> 9.52 us  [arrive(): lax.all_to_all(streams, 'chan', split_axis=2, concat_axis=1, tiled=True)]
    optimization_barrier x1 -> x0, local copies, waits for them, and re-layouts: 3.9 us -> none  [local(): keys_values, queries = lax.optimization_barrier((keys_values, features[:1]))]
    unnamed x31 -> x29, local copies, waits for them, and re-layouts: 10.2 us -> 7.42 us
    all_to_all x2 -> x1, waiting for transfers between devices: 24.4 us -> 23.1 us  [arrive(): lax.all_to_all(streams, 'chan', split_axis=2, concat_axis=1, tiled=True)]
    all_to_all x2 -> x1, local copies, waits for them, and re-layouts: 5.25 us -> 4.72 us  [arrive(): lax.all_to_all(streams, 'chan', split_axis=2, concat_axis=1, tiled=True)]
where the time goes in v4:
time: 216 us; the launch traced here: 215 us
  starting transfers between devices  70.3 us (33%)
  local copies, waits for them, and re-layouts  49.6 us (23%)
  matrix products  31.6 us (15%)
  waiting for transfers between devices  29.8 us (14%)
  blocking collectives  17.3 us (8%)
  other arithmetic  16.3 us (8%)
    ppermute x8, starting transfers between devices, from_behind(): return lax.ppermute(block, axis, route)  54.3 us
    all_to_all x1, waiting for transfers between devices, arrive(): lax.all_to_all(streams, 'chan', split_axis=2, concat_axis=1, tiled=True)  23.1 us
    all_to_all x1, blocking collectives, local(): lax.all_to_all(gated, 'chan', split_axis=0, concat_axis=1, tiled=True)  17.3 us
    dot_general x1, matrix products, long_part(): jnp.einsum('nic,knc->kic', reading, starts, precision=lax.Precision.HIGHEST)  12.4 us
    dot_general x1, matrix products, long_part(): jnp.einsum('ijc,kjc->kic', toeplitz, pieces, precision=lax.Precision.HIGH...  10.3 us
    all_to_all x1, starting transfers between devices, arrive(): lax.all_to_all(streams, 'chan', split_axis=2, concat_axis=1, tiled=True)  9.52 us
    dot_general x1, local copies, waits for them, and re-layouts, modal_tables(): jnp.dot(one_hot.reshape(block * block, block), kernel, precision=lax.Prec...  9.31 us
    add x5, other arithmetic, long_part(): starts + jnp.exp(-decay_rate * float(block * step)) * shifted(starts, step)  8.07 us
  transfers between devices with their start and end apart: 10, of which 7 were waited for; matrix products, arithmetic and copies ran while one was open for 9% of the time, Pallas kernels for 0%

profile of v4, /device:TPU:2, one launch (start us, length us, event | category | flops | bytes accessed | tf_op | source)
XLA Modules:
  0.0 215.2 jit_solution(1908403894335349260)
XLA Ops:
  0.0 1.6 slice-done
  1.6 3.8 %copy.66 = bf16[2,128,4096]{1,0,2:T(2,128)(2,1)} copy(bf16[2,128,4096]{2,1,0:T(8,128)(2,1)S(1)} %slice-done) | data formatting | bytes 4194304
  5.4 9.5 %all-to-all-start = ((bf16[2,128,4096]{1,0,2:T(2,128)(2,1)}), bf16[2,128,4096]{1,0,2:T(2,128)(2,1)S(1)}, u32[]{:S(2)}, u32[]{:S(2)}) async-start(bf16[2,128,4096]{1,0,2:T(2,128)(2,1)} %copy.66), calls=%async_computation | async-start | bytes 4194304 | tf_op jit(solution)/shard_map/all_to_all | solution.py:93
  15.8 1.3 slice_bitcast_fusion
  17.1 23.1 %all-to-all-done = bf16[2,128,4096]{1,0,2:T(2,128)(2,1)S(1)} async-done(((bf16[2,128,4096]{1,0,2:T(2,128)(2,1)}), bf16[2,128,4096]{1,0,2:T(2,128)(2,1)S(1)}, u32[]{:S(2)}, u32[]{:S(2)}) %all-to-all-start) | async-done | bytes 2097184 | tf_op jit(solution)/shard_map/all_to_all | solution.py:93
  40.2 1.3 copy-done.4
  41.5 4.7 %copy.42 = bf16[2,128,16,256]{3,1,2,0:T(8,128)(2,1)S(1)} copy(bf16[2,128,16,256]{1,0,3,2:T(2,128)(2,1)} %bitcast.69) | data formatting | bytes 4194304 | tf_op jit(solution)/shard_map/all_to_all | solution.py:93
  46.3 1.3 collective-permute-start
  51.3 1.4 add_convert_fusion
  53.1 1.0 copy-done.2
  54.0 3.8 %copy.46 = bf16[32,64,256]{1,0,2:T(8,128)(2,1)} copy(bf16[32,64,256]{2,1,0:T(8,128)(2,1)S(1)} %bitcast.66) | data formatting | bytes 2097152 | tf_op jit(solution)/shard_map/reshape | solution.py:58
  57.8 5.0 %fusion.13 = f32[32,16,256]{0,1,2:T(8,128)S(1)} fusion(bf16[32,64,256]{1,0,2:T(8,128)(2,1)} %copy.46, f32[64]{0:T(128)S(1)} %broadcast_subtract_fusion, f32[16,256]{0,1:T(8,128)S(1)} %copy.44), kind=kOutput, calls=%fused_computation.28 | convolution fusion | flops 100925440 | bytes 1589504 | tf_op jit(solution)/shard_map/njc,kjc->knc/dot_general | solution.py:59
  62.9 1.9 slice.121
  64.8 1.9 pad_slice_fusion
  66.7 1.1 copy.73
  67.8 6.4 %all-to-all-start.1 = ((bf16[128,16,256]{2,0,1:T(8,128)(2,1)}), bf16[128,16,256]{2,0,1:T(8,128)(2,1)S(1)}, u32[]{:S(2)}, u32[]{:S(2)}) async-start(bf16[128,16,256]{2,0,1:T(8,128)(2,1)} %bitcast.73), calls=%async_computation.1 | async-start | bytes 2097152 | tf_op jit(solution)/shard_map/all_to_all | solution.py:99
  74.3 3.1 %multiply_add_fusion.4 = f32[32,16,256]{0,1,2:T(8,128)S(1)} fusion(f32[31,16,256]{0,1,2:T(8,128)} %pad_slice_fusion, f32[31,16,256]{0,1,2:T(8,128)S(1)} %bitcast.61, f32[16,256]{0,1:T(8,128)} %copy.49), kind=kLoop, calls=%fused_computation.19 | loop fusion | flops 262144 | bytes 1556480 | tf_op jit(solution)/shard_map/add | solution.py:63
  77.4 1.3 multiply_add_fusion.3
  78.6 1.3 multiply_add_fusion.2
  79.9 1.3 multiply_add_fusion.1
  81.2 1.3 multiply_add_fusion
  82.4 1.3 copy-done.1
  83.8 1.9 slice.120
  85.7 2.7 %copy.55 = f32[1,16,256]{2,1,0:T(8,128)S(1)} copy(f32[1,16,256]{0,1,2:T(8,128)} %slice.120) | data formatting | bytes 32768 | tf_op jit(solution)/shard_map/slice | solution.py:65
  88.3 1.0 copy.56
  89.4 5.9 %collective-permute-start.1 = (bf16[1,2,256]{2,1,0:T(2,128)(2,1)S(1)}, bf16[1,2,256]{2,1,0:T(2,128)(2,1)S(1)}, u32[]{:S(2)}, u32[]{:S(2)}) collective-permute-start(bf16[1,2,256]{2,1,0:T(2,128)(2,1)S(1)} %slice.122), channel_id=1, source_target_pairs={{0,16},{16,32},{32,48},{48,64},{64,80},{80,96},{96,112},{112,128},... | collective-permute-start | bytes 3080 | tf_op jit(solution)/shard_map/ppermute | solution.py:14
  96.1 1.5 pad_maximum_fusion.1
  97.6 3.3 %collective-permute-start.2 = (f32[16,256]{1,0:T(8,128)S(1)}, f32[16,256]{1,0:T(8,128)S(1)}, u32[]{:S(2)}, u32[]{:S(2)}) collective-permute-start(f32[16,256]{1,0:T(8,128)S(1)} %bitcast_add_fusion.1), channel_id=1, source_target_pairs={{0,16},{16,32},{32,48},{48,64},{64,80},{80,96},{96,112},{112,128},... | collective-permute-start | bytes 49160 | tf_op jit(solution)/shard_map/ppermute | solution.py:14
  100.9 4.1 %collective-permute-start.3 = (f32[16,256]{1,0:T(8,128)S(1)}, f32[16,256]{1,0:T(8,128)S(1)}, u32[]{:S(2)}, u32[]{:S(2)}) collective-permute-start(f32[16,256]{1,0:T(8,128)S(1)} %bitcast_add_fusion.1), channel_id=1, source_target_pairs={{0,32},{16,48},{32,64},{48,80},{64,96},{80,112},{96,128},{112,144}... | collective-permute-start | bytes 49160 | tf_op jit(solution)/shard_map/ppermute | solution.py:14
  105.0 1.4 collective-permute-done.3
  106.4 4.2 %collective-permute-start.4 = (f32[16,256]{1,0:T(8,128)S(1)}, f32[16,256]{1,0:T(8,128)S(1)}, u32[]{:S(2)}, u32[]{:S(2)}) collective-permute-start(f32[16,256]{1,0:T(8,128)S(1)} %multiply_add_fusion.9), channel_id=1, source_target_pairs={{0,32},{16,48},{32,64},{48,80},{64,96},{80,112},{96,128},{112,144}... | collective-permute-start | bytes 49160 | tf_op jit(solution)/shard_map/ppermute | solution.py:14
  110.6 0.9 constant_dynamic-slice_fusion.2
  112.1 9.7 %collective-permute-start.5 = (f32[16,256]{1,0:T(8,128)S(1)}, f32[16,256]{1,0:T(8,128)S(1)}, u32[]{:S(2)}, u32[]{:S(2)}) collective-permute-start(f32[16,256]{1,0:T(8,128)S(1)} %multiply_add_fusion.8), channel_id=1, source_target_pairs={{0,64},{16,80},{32,96},{48,112},{64,128},{80,144},{96,160},{112,17... | collective-permute-start | bytes 49160 | tf_op jit(solution)/shard_map/ppermute | solution.py:14
  121.7 1.4 collective-permute-done.5
  123.1 12.2 %collective-permute-start.6 = (f32[16,256]{1,0:T(8,128)S(1)}, f32[16,256]{1,0:T(8,128)S(1)}, u32[]{:S(2)}, u32[]{:S(2)}) collective-permute-start(f32[16,256]{1,0:T(8,128)S(1)} %multiply_add_fusion.7), channel_id=1, source_target_pairs={{0,128},{16,144},{32,160},{48,176},{64,192},{80,208},{96,224},{112... | collective-permute-start | bytes 49160 | tf_op jit(solution)/shard_map/ppermute | solution.py:14
  135.4 1.4 collective-permute-done.6
  136.8 13.7 %collective-permute-start.7 = (f32[16,256]{1,0:T(8,128)S(1)}, f32[16,256]{1,0:T(8,128)S(1)}, u32[]{:S(2)}, u32[]{:S(2)}) collective-permute-start(f32[16,256]{1,0:T(8,128)S(1)} %multiply_add_fusion.6), channel_id=1, source_target_pairs={{0,256},{16,272},{32,288},{48,304},{64,320},{80,336},{96,352},{112... | collective-permute-start | bytes 49160 | tf_op jit(solution)/shard_map/ppermute | solution.py:14
  150.5 1.2 collective-permute-done.7
  151.8 1.6 multiply_reduce_fusion
  153.4 3.8 %fusion.12 = f32[64,64,256]{2,1,0:T(8,128)} fusion(s32[64,64]{1,0:T(8,128)S(1)} %iota_subtract_fusion, f32[64,256]{0,1:T(8,128)S(1)} %multiply_reduce_fusion), kind=kOutput, calls=%fused_computation.26 | convolution fusion | flops 805568512 | bytes 4276224 | tf_op jit(solution)/shard_map/dot_general | solution.py:36
  157.3 9.3 %copy.47 = f32[64,64,256]{1,0,2:T(8,128)} copy(f32[64,64,256]{2,1,0:T(8,128)} %fusion.12) | data formatting | bytes 8388608 | tf_op jit(solution)/shard_map/dot_general | solution.py:36
  166.6 10.3 %fusion.28 = f32[256,32,64]{2,1,0:T(8,128)} fusion(bf16[32,64,256]{1,0,2:T(8,128)(2,1)S(1)} %copy-done, f32[64,64,256]{1,0,2:T(8,128)} %copy.47), kind=kOutput, calls=%fused_computation.69 | convolution fusion | flops 402653184 | bytes 7340032 | tf_op jit(solution)/shard_map/ijc,kjc->kic/dot_general | solution.py:77
  177.0 12.4 %add_bitcast_fusion = f32[32,64,256]{1,0,2:T(8,128)} fusion(f32[256,32,64]{2,1,0:T(8,128)} %fusion.28, f32[32,16,256]{0,1,2:T(8,128)} %copy-done.1, f32[64]{0:T(128)S(1)} %broadcast_add_fusion, f32[16,256]{0,1:T(8,128)S(1)} %copy.58, f32[32]{0:T(128)S(1)} %convert_multiply_fusion.1, f32[16,256]{0,1:T(8,128)S(1)} %copy.44, f32[16,256]{0,1:T(8,128)S(1)} %copy.43), kind=kOutput, calls=%fused_computation | convolution fusion | flops 102105088 | bytes 4768128 | tf_op jit(solution)/shard_map/nic,knc->kic/dot_general | solution.py:80
  189.4 4.6 %copy.59 = f32[32,64,256]{2,1,0:T(8,128)} copy(f32[32,64,256]{1,0,2:T(8,128)} %add_bitcast_fusion) | data formatting | bytes 4194304 | tf_op jit(solution)/shard_map/add | solution.py:81
  194.1 1.8 fusion.1
  195.9 0.9 fusion
  196.8 17.3 %all_to_all.53 = bf16[16,128,256]{2,1,0:T(8,128)(2,1)S(1)} all-to-all(bf16[16,128,256]{2,1,0:T(8,128)(2,1)S(1)} %bitcast.75), channel_id=1, replica_groups=mesh['seq'=32,'chan'=16] {'chan'}, dimensions={0} | all-to-all | bytes 2097152 | tf_op jit(solution)/shard_map/all_to_all | solution.py:113
  214.1 1.1 copy.68
  (56 shorter events, 6.6 us)
Async XLA Ops:
  0.0 1.6 slice-start
  5.4 10.4 %copy-start.7 = (f32[16,256]{1,0:T(8,128)S(1)}, f32[16,256]{1,0:T(8,128)}, u32[]{:S(2)}) copy-start(f32[16,256]{1,0:T(8,128)} %param.7) | copy-start | bytes 49156
  5.4 34.8 %all-to-all-start = ((bf16[2,128,4096]{1,0,2:T(2,128)(2,1)}), bf16[2,128,4096]{1,0,2:T(2,128)(2,1)S(1)}, u32[]{:S(2)}, u32[]{:S(2)}) async-start(bf16[2,128,4096]{1,0,2:T(2,128)(2,1)} %copy.66), calls=%async_computation | async-start | bytes 4194304 | tf_op jit(solution)/shard_map/all_to_all | solution.py:93
  40.2 1.3 copy-start.4
  46.3 4.5 %collective-permute-start = (bf16[2,2,256]{2,1,0:T(2,128)(2,1)S(1)}, bf16[2,2,256]{2,1,0:T(2,128)(2,1)S(1)}, u32[]{:S(2)}, u32[]{:S(2)}) collective-permute-start(bf16[2,2,256]{2,1,0:T(2,128)(2,1)S(1)} %slice.112), channel_id=1, source_target_pairs={{0,16},{16,32},{32,48},{48,64},{64,80},{80,96},{96,112},{112,128},... | collective-permute-start | bytes 6152 | tf_op jit(solution)/shard_map/ppermute | solution.py:14
  53.0 1.0 copy-start.2
  67.8 21.5 %all-to-all-start.1 = ((bf16[128,16,256]{2,0,1:T(8,128)(2,1)}), bf16[128,16,256]{2,0,1:T(8,128)(2,1)S(1)}, u32[]{:S(2)}, u32[]{:S(2)}) async-start(bf16[128,16,256]{2,0,1:T(8,128)(2,1)} %bitcast.73), calls=%async_computation.1 | async-start | bytes 2097152 | tf_op jit(solution)/shard_map/all_to_all | solution.py:99
  74.3 3.1 %copy-start.10 = (f32[16,256]{0,1:T(8,128)S(1)}, f32[16,256]{0,1:T(8,128)}, u32[]{:S(2)}) copy-start(f32[16,256]{0,1:T(8,128)} %copy.50) | copy-start | bytes 49156
  77.4 1.3 copy-start.9
  79.9 1.3 copy-start.8
  82.4 1.3 copy-start.1
  85.7 2.7 %copy-start.5 = (f32[1,16,256]{0,1,2:T(8,128)S(1)}, f32[1,16,256]{0,1,2:T(8,128)}, u32[]{:S(2)}) copy-start(f32[1,16,256]{0,1,2:T(8,128)} %slice.121) | copy-start | bytes 49156
  88.3 63.4 %copy-start.11 = (f32[16,256]{1,0:T(8,128)S(1)}, f32[16,256]{1,0:T(8,128)}, u32[]{:S(2)}) copy-start(f32[16,256]{1,0:T(8,128)} %param.8) | copy-start | bytes 49156
  89.4 6.0 %copy-start.6 = (bf16[128,16,256]{2,0,1:T(8,128)(2,1)}, bf16[128,16,256]{2,0,1:T(8,128)(2,1)S(1)}, u32[]{:S(2)}) copy-start(bf16[128,16,256]{2,0,1:T(8,128)(2,1)S(1)} %all-to-all-done.1) | copy-start | bytes 3145732
  89.4 6.7 %collective-permute-start.1 = (bf16[1,2,256]{2,1,0:T(2,128)(2,1)S(1)}, bf16[1,2,256]{2,1,0:T(2,128)(2,1)S(1)}, u32[]{:S(2)}, u32[]{:S(2)}) collective-permute-start(bf16[1,2,256]{2,1,0:T(2,128)(2,1)S(1)} %slice.122), channel_id=1, source_target_pairs={{0,16},{16,32},{32,48},{48,64},{64,80},{80,96},{96,112},{112,128},... | collective-permute-start | bytes 3080 | tf_op jit(solution)/shard_map/ppermute | solution.py:14
  97.6 7.4 %collective-permute-start.2 = (f32[16,256]{1,0:T(8,128)S(1)}, f32[16,256]{1,0:T(8,128)S(1)}, u32[]{:S(2)}, u32[]{:S(2)}) collective-permute-start(f32[16,256]{1,0:T(8,128)S(1)} %bitcast_add_fusion.1), channel_id=1, source_target_pairs={{0,16},{16,32},{32,48},{48,64},{64,80},{80,96},{96,112},{112,128},... | collective-permute-start | bytes 49160 | tf_op jit(solution)/shard_map/ppermute | solution.py:14
  100.9 5.5 %collective-permute-start.3 = (f32[16,256]{1,0:T(8,128)S(1)}, f32[16,256]{1,0:T(8,128)S(1)}, u32[]{:S(2)}, u32[]{:S(2)}) collective-permute-start(f32[16,256]{1,0:T(8,128)S(1)} %bitcast_add_fusion.1), channel_id=1, source_target_pairs={{0,32},{16,48},{32,64},{48,80},{64,96},{80,112},{96,128},{112,144}... | collective-permute-start | bytes 49160 | tf_op jit(solution)/shard_map/ppermute | solution.py:14
  106.4 5.6 %collective-permute-start.4 = (f32[16,256]{1,0:T(8,128)S(1)}, f32[16,256]{1,0:T(8,128)S(1)}, u32[]{:S(2)}, u32[]{:S(2)}) collective-permute-start(f32[16,256]{1,0:T(8,128)S(1)} %multiply_add_fusion.9), channel_id=1, source_target_pairs={{0,32},{16,48},{32,64},{48,80},{64,96},{80,112},{96,128},{112,144}... | collective-permute-start | bytes 49160 | tf_op jit(solution)/shard_map/ppermute | solution.py:14
  112.1 11.1 %collective-permute-start.5 = (f32[16,256]{1,0:T(8,128)S(1)}, f32[16,256]{1,0:T(8,128)S(1)}, u32[]{:S(2)}, u32[]{:S(2)}) collective-permute-start(f32[16,256]{1,0:T(8,128)S(1)} %multiply_add_fusion.8), channel_id=1, source_target_pairs={{0,64},{16,80},{32,96},{48,112},{64,128},{80,144},{96,160},{112,17... | collective-permute-start | bytes 49160 | tf_op jit(solution)/shard_map/ppermute | solution.py:14
  123.1 13.6 %collective-permute-start.6 = (f32[16,256]{1,0:T(8,128)S(1)}, f32[16,256]{1,0:T(8,128)S(1)}, u32[]{:S(2)}, u32[]{:S(2)}) collective-permute-start(f32[16,256]{1,0:T(8,128)S(1)} %multiply_add_fusion.7), channel_id=1, source_target_pairs={{0,128},{16,144},{32,160},{48,176},{64,192},{80,208},{96,224},{112... | collective-permute-start | bytes 49160 | tf_op jit(solution)/shard_map/ppermute | solution.py:14
  136.8 14.9 %collective-permute-start.7 = (f32[16,256]{1,0:T(8,128)S(1)}, f32[16,256]{1,0:T(8,128)S(1)}, u32[]{:S(2)}, u32[]{:S(2)}) collective-permute-start(f32[16,256]{1,0:T(8,128)S(1)} %multiply_add_fusion.6), channel_id=1, source_target_pairs={{0,256},{16,272},{32,288},{48,304},{64,320},{80,336},{96,352},{112... | collective-permute-start | bytes 49160 | tf_op jit(solution)/shard_map/ppermute | solution.py:14
  157.3 9.3 %copy-start = (bf16[32,64,256]{1,0,2:T(8,128)(2,1)S(1)}, bf16[32,64,256]{1,0,2:T(8,128)(2,1)}, u32[]{:S(2)}) copy-start(bf16[32,64,256]{1,0,2:T(8,128)(2,1)} %copy.46) | copy-start | bytes 3145732
  189.4 4.7 %copy-start.3 = (bf16[2048,256]{1,0:T(8,128)(2,1)S(1)}, bf16[2048,256]{1,0:T(8,128)(2,1)}, u32[]{:S(2)}) copy-start(bf16[2048,256]{1,0:T(8,128)(2,1)} %copy-done.2) | copy-start | bytes 3145732
  189.4 4.7 %copy-start.12 = (f32[256]{0:T(256)S(1)}, f32[256]{0:T(256)}, u32[]{:S(2)}) copy-start(f32[256]{0:T(256)} %param.9) | copy-start | bytes 3076

commit v5 on v4

--- a/solution.py
+++ b/solution.py
@@ -48,13 +48,12 @@
     return jnp.concatenate([padding, values[: values.shape[0] - distance]], axis=0)
 
 
-def long_part(product, decay_rate, residue, skip_gain, passenger):
+def long_part(product, decay_rate, scaled, toeplitz, skip_gain, passenger):
     signal = product.astype(jnp.float32)
     section = signal.shape[0]
     block = math.gcd(section, block_len)
     count = section // block
-    scaled = residue * jnp.sqrt(1.0 - jnp.exp(-2.0 * decay_rate))
-    toeplitz, ending, reading = modal_tables(decay_rate, scaled, block)
+    unused_toeplitz, ending, reading = modal_tables(decay_rate, scaled, block)
     pieces = signal.reshape(count, block, signal.shape[1])
     local_end = jnp.einsum("njc,kjc->knc", ending, pieces, precision=lax.Precision.HIGHEST)
     starts = shifted(local_end, 1)
@@ -94,8 +93,11 @@
         border = from_behind(columns[:, columns.shape[1] - (taps - 1) :, :], "seq", 1)
         return jnp.concatenate([border, columns], axis=1)
 
+    scaled = residue * jnp.sqrt(1.0 - jnp.exp(-2.0 * decay_rate))
+    section = features.shape[1] * lax.axis_size("chan")
+    toeplitz = modal_tables(decay_rate, scaled, math.gcd(section, block_len))[0]
     keys_values = arrive(features[1:])
-    keys_values, queries = lax.optimization_barrier((keys_values, features[0]))
+    keys_values, queries, toeplitz = lax.optimization_barrier((keys_values, features[0], toeplitz))
     queries = lax.all_to_all(queries, "chan", split_axis=1, concat_axis=0, tiled=True)
     queries = queries[None]
     border = from_behind(queries[:, queries.shape[1] - (taps - 1) :, :], "seq", 1)
@@ -106,7 +108,7 @@
         (gates[0].astype(jnp.float32) * gates[1].astype(jnp.float32)).astype(jnp.bfloat16)
     )
     conv_out, queries = lax.optimization_barrier(
-        long_part(product, decay_rate, residue, skip_gain, queries)
+        long_part(product, decay_rate, scaled, toeplitz, skip_gain, queries)
     )
     query = short_filter(queries, weights[:1], taps).astype(jnp.bfloat16)[0]
     gated = (query.astype(jnp.float32) * conv_out.astype(jnp.float32)).astype(jnp.bfloat16)

time: 216 us -> 209 us (0.968)
  the two profiles are of different devices: /device:TPU:2 before, /device:TPU:1 now
where the time goes in v5:
time: 209 us; the launch traced here: 206 us
  starting transfers between devices  69.7 us (33%)
  local copies, waits for them, and re-layouts  47.6 us (23%)
  matrix products  31.6 us (15%)
  waiting for transfers between devices  24 us (11%)
  other arithmetic  16.3 us (8%)
  blocking collectives  15.8 us (8%)
    ppermute x8, starting transfers between devices, from_behind(): return lax.ppermute(block, axis, route)  58.2 us
    all_to_all x1, waiting for transfers between devices, arrive(): lax.all_to_all(streams, 'chan', split_axis=2, concat_axis=1, tiled=True)  18.5 us
    all_to_all x1, blocking collectives, local(): lax.all_to_all(gated, 'chan', split_axis=0, concat_axis=1, tiled=True)  15.8 us
    dot_general x1, matrix products, long_part(): jnp.einsum('nic,knc->kic', reading, starts, precision=lax.Precision.HIGHEST)  12.4 us
    dot_general x1, matrix products, long_part(): jnp.einsum('ijc,kjc->kic', toeplitz, pieces, precision=lax.Precision.HIGH...  10.3 us
    optimization_barrier x1, local copies, waits for them, and re-layouts, local(): lax.optimization_barrier((keys_values, features[0], toeplitz))  9.31 us
    add x5, other arithmetic, long_part(): starts + jnp.exp(-decay_rate * float(block * step)) * shifted(starts, step)  8.07 us
    all_to_all x1, starting transfers between devices, arrive(): lax.all_to_all(streams, 'chan', split_axis=2, concat_axis=1, tiled=True)  7.7 us
  transfers between devices with their start and end apart: 10, of which 5 were waited for; matrix products, arithmetic and copies ran while one was open for 20% of the time, Pallas kernels for 0%

profile of v5, /device:TPU:1, one launch (start us, length us, event | category | flops | bytes accessed | tf_op | source)
XLA Modules:
  0.0 205.5 jit_solution(17173726016856009830)
XLA Ops:
  0.0 1.6 slice-done
  1.6 3.8 %copy.68 = bf16[2,128,4096]{1,0,2:T(2,128)(2,1)} copy(bf16[2,128,4096]{2,1,0:T(8,128)(2,1)S(1)} %slice-done) | data formatting | bytes 4194304
  5.4 7.7 %all-to-all-start = ((bf16[2,128,4096]{1,0,2:T(2,128)(2,1)}), bf16[2,128,4096]{1,0,2:T(2,128)(2,1)S(1)}, u32[]{:S(2)}, u32[]{:S(2)}) async-start(bf16[2,128,4096]{1,0,2:T(2,128)(2,1)} %copy.68), calls=%async_computation | async-start | bytes 4194304 | tf_op jit(solution)/shard_map/all_to_all | solution.py:92
  13.4 0.9 constant_dynamic-slice_fusion.1
  14.3 1.6 multiply_reduce_fusion
  15.9 3.8 %fusion.12 = f32[64,64,256]{2,1,0:T(8,128)} fusion(s32[64,64]{1,0:T(8,128)S(1)} %iota_subtract_fusion, f32[64,256]{0,1:T(8,128)S(1)} %multiply_reduce_fusion), kind=kOutput, calls=%fused_computation.26 | convolution fusion | flops 805568512 | bytes 4276224 | tf_op jit(solution)/shard_map/dot_general | solution.py:36
  19.9 18.5 %all-to-all-done = bf16[2,128,4096]{1,0,2:T(2,128)(2,1)S(1)} async-done(((bf16[2,128,4096]{1,0,2:T(2,128)(2,1)}), bf16[2,128,4096]{1,0,2:T(2,128)(2,1)S(1)}, u32[]{:S(2)}, u32[]{:S(2)}) %all-to-all-start) | async-done | bytes 2097184 | tf_op jit(solution)/shard_map/all_to_all | solution.py:92
  38.4 1.3 copy-done.4
  39.7 4.7 %copy.44 = bf16[2,128,16,256]{3,1,2,0:T(8,128)(2,1)S(1)} copy(bf16[2,128,16,256]{1,0,3,2:T(2,128)(2,1)} %bitcast.69) | data formatting | bytes 4194304 | tf_op jit(solution)/shard_map/all_to_all | solution.py:92
  44.4 10.9 %collective-permute-start = (bf16[2,2,256]{2,1,0:T(2,128)(2,1)S(1)}, bf16[2,2,256]{2,1,0:T(2,128)(2,1)S(1)}, u32[]{:S(2)}, u32[]{:S(2)}) collective-permute-start(bf16[2,2,256]{2,1,0:T(2,128)(2,1)S(1)} %slice.112), channel_id=1, source_target_pairs={{0,16},{16,32},{32,48},{48,64},{64,80},{80,96},{96,112},{112,128},... | collective-permute-start | bytes 6152 | tf_op jit(solution)/shard_map/ppermute | solution.py:14
  55.3 0.8 copy.51
  56.1 0.8 copy.52
  59.6 1.4 add_convert_fusion
  61.4 1.0 copy-done.2
  62.3 3.8 %copy.48 = bf16[32,64,256]{1,0,2:T(8,128)(2,1)} copy(bf16[32,64,256]{2,1,0:T(8,128)(2,1)S(1)} %bitcast.66) | data formatting | bytes 2097152 | tf_op jit(solution)/shard_map/reshape | solution.py:57
  66.1 5.0 %fusion.13 = f32[32,16,256]{0,1,2:T(8,128)S(1)} fusion(bf16[32,64,256]{1,0,2:T(8,128)(2,1)} %copy.48, f32[64]{0:T(128)S(1)} %broadcast_subtract_fusion, f32[16,256]{0,1:T(8,128)S(1)} %copy.46), kind=kOutput, calls=%fused_computation.28 | convolution fusion | flops 100925440 | bytes 1589504 | tf_op jit(solution)/shard_map/njc,kjc->knc/dot_general | solution.py:58
  71.2 1.9 slice.121
  73.1 1.9 pad_slice_fusion
  75.0 2.5 %copy.58 = f32[1,16,256]{2,1,0:T(8,128)S(1)} copy(f32[1,16,256]{0,1,2:T(8,128)} %slice.121) | data formatting | bytes 32768 | tf_op jit(solution)/shard_map/slice | solution.py:64
  77.5 1.1 copy.75
  78.6 3.8 %all-to-all-start.1 = ((bf16[128,16,256]{2,0,1:T(8,128)(2,1)}), bf16[128,16,256]{2,0,1:T(8,128)(2,1)S(1)}, u32[]{:S(2)}, u32[]{:S(2)}) async-start(bf16[128,16,256]{2,0,1:T(8,128)(2,1)} %bitcast.73), calls=%async_computation.1 | async-start | bytes 2097152 | tf_op jit(solution)/shard_map/all_to_all | solution.py:101
  82.5 3.1 %multiply_add_fusion.4 = f32[32,16,256]{0,1,2:T(8,128)S(1)} fusion(f32[31,16,256]{0,1,2:T(8,128)} %pad_slice_fusion, f32[31,16,256]{0,1,2:T(8,128)S(1)} %bitcast.61, f32[16,256]{0,1:T(8,128)} %copy.51), kind=kLoop, calls=%fused_computation.19 | loop fusion | flops 262144 | bytes 1556480 | tf_op jit(solution)/shard_map/add | solution.py:62
  85.6 1.3 multiply_add_fusion.3
  86.9 1.3 multiply_add_fusion.2
  88.1 1.3 multiply_add_fusion.1
  89.4 1.3 multiply_add_fusion
  90.7 1.3 copy-done.1
  92.6 1.0 copy.57
  93.6 3.2 %all-to-all-done.1 = bf16[128,16,256]{2,0,1:T(8,128)(2,1)S(1)} async-done(((bf16[128,16,256]{2,0,1:T(8,128)(2,1)}), bf16[128,16,256]{2,0,1:T(8,128)(2,1)S(1)}, u32[]{:S(2)}, u32[]{:S(2)}) %all-to-all-start.1) | async-done | bytes 1048608 | tf_op jit(solution)/shard_map/all_to_all | solution.py:101
  96.8 5.0 %collective-permute-start.1 = (bf16[1,2,256]{2,1,0:T(2,128)(2,1)S(1)}, bf16[1,2,256]{2,1,0:T(2,128)(2,1)S(1)}, u32[]{:S(2)}, u32[]{:S(2)}) collective-permute-start(bf16[1,2,256]{2,1,0:T(2,128)(2,1)S(1)} %slice.122), channel_id=1, source_target_pairs={{0,16},{16,32},{32,48},{48,64},{64,80},{80,96},{96,112},{112,128},... | collective-permute-start | bytes 3080 | tf_op jit(solution)/shard_map/ppermute | solution.py:14
  102.4 1.5 pad_maximum_fusion.1
  103.9 4.2 %collective-permute-start.2 = (f32[16,256]{1,0:T(8,128)S(1)}, f32[16,256]{1,0:T(8,128)S(1)}, u32[]{:S(2)}, u32[]{:S(2)}) collective-permute-start(f32[16,256]{1,0:T(8,128)S(1)} %bitcast_add_fusion.1), channel_id=1, source_target_pairs={{0,16},{16,32},{32,48},{48,64},{64,80},{80,96},{96,112},{112,128},... | collective-permute-start | bytes 49160 | tf_op jit(solution)/shard_map/ppermute | solution.py:14
  108.1 3.5 %collective-permute-start.3 = (f32[16,256]{1,0:T(8,128)S(1)}, f32[16,256]{1,0:T(8,128)S(1)}, u32[]{:S(2)}, u32[]{:S(2)}) collective-permute-start(f32[16,256]{1,0:T(8,128)S(1)} %bitcast_add_fusion.1), channel_id=1, source_target_pairs={{0,32},{16,48},{32,64},{48,80},{64,96},{80,112},{96,128},{112,144}... | collective-permute-start | bytes 49160 | tf_op jit(solution)/shard_map/ppermute | solution.py:14
  111.7 0.8 collective-permute-done.3
  112.5 3.6 %collective-permute-start.4 = (f32[16,256]{1,0:T(8,128)S(1)}, f32[16,256]{1,0:T(8,128)S(1)}, u32[]{:S(2)}, u32[]{:S(2)}) collective-permute-start(f32[16,256]{1,0:T(8,128)S(1)} %multiply_add_fusion.9), channel_id=1, source_target_pairs={{0,32},{16,48},{32,64},{48,80},{64,96},{80,112},{96,128},{112,144}... | collective-permute-start | bytes 49160 | tf_op jit(solution)/shard_map/ppermute | solution.py:14
  116.2 0.9 constant_dynamic-slice_fusion.2
  117.1 9.1 %collective-permute-start.5 = (f32[16,256]{1,0:T(8,128)S(1)}, f32[16,256]{1,0:T(8,128)S(1)}, u32[]{:S(2)}, u32[]{:S(2)}) collective-permute-start(f32[16,256]{1,0:T(8,128)S(1)} %multiply_add_fusion.8), channel_id=1, source_target_pairs={{0,64},{16,80},{32,96},{48,112},{64,128},{80,144},{96,160},{112,17... | collective-permute-start | bytes 49160 | tf_op jit(solution)/shard_map/ppermute | solution.py:14
  126.2 0.8 collective-permute-done.5
  127.0 10.6 %collective-permute-start.6 = (f32[16,256]{1,0:T(8,128)S(1)}, f32[16,256]{1,0:T(8,128)S(1)}, u32[]{:S(2)}, u32[]{:S(2)}) collective-permute-start(f32[16,256]{1,0:T(8,128)S(1)} %multiply_add_fusion.7), channel_id=1, source_target_pairs={{0,128},{16,144},{32,160},{48,176},{64,192},{80,208},{96,224},{112... | collective-permute-start | bytes 49160 | tf_op jit(solution)/shard_map/ppermute | solution.py:14
  137.7 9.3 %copy.49 = f32[64,64,256]{1,0,2:T(8,128)} copy(f32[64,64,256]{2,1,0:T(8,128)} %fusion.12) | data formatting | bytes 8388608 | tf_op jit(solution)/shard_map/optimization_barrier | solution.py:100
  147.0 11.3 %collective-permute-start.7 = (f32[16,256]{1,0:T(8,128)S(1)}, f32[16,256]{1,0:T(8,128)S(1)}, u32[]{:S(2)}, u32[]{:S(2)}) collective-permute-start(f32[16,256]{1,0:T(8,128)S(1)} %multiply_add_fusion.6), channel_id=1, source_target_pairs={{0,256},{16,272},{32,288},{48,304},{64,320},{80,336},{96,352},{112... | collective-permute-start | bytes 49160 | tf_op jit(solution)/shard_map/ppermute | solution.py:14
  158.3 10.3 %fusion.28 = f32[256,32,64]{2,1,0:T(8,128)} fusion(bf16[32,64,256]{1,0,2:T(8,128)(2,1)S(1)} %copy-done, f32[64,64,256]{1,0,2:T(8,128)} %copy.49), kind=kOutput, calls=%fused_computation.69 | convolution fusion | flops 402653184 | bytes 7340032 | tf_op jit(solution)/shard_map/ijc,kjc->kic/dot_general | solution.py:76
  168.7 12.4 %add_bitcast_fusion = f32[32,64,256]{1,0,2:T(8,128)} fusion(f32[256,32,64]{2,1,0:T(8,128)} %fusion.28, f32[32,16,256]{0,1,2:T(8,128)} %copy-done.1, f32[64]{0:T(128)S(1)} %broadcast_add_fusion, f32[16,256]{0,1:T(8,128)S(1)} %copy.60, f32[32]{0:T(128)S(1)} %convert_multiply_fusion.1, f32[16,256]{0,1:T(8,128)S(1)} %copy.46, f32[16,256]{0,1:T(8,128)S(1)} %copy.45), kind=kOutput, calls=%fused_computation | convolution fusion | flops 102105088 | bytes 4768128 | tf_op jit(solution)/shard_map/nic,knc->kic/dot_general | solution.py:79
  181.2 4.6 %copy.61 = f32[32,64,256]{2,1,0:T(8,128)} copy(f32[32,64,256]{1,0,2:T(8,128)} %add_bitcast_fusion) | data formatting | bytes 4194304 | tf_op jit(solution)/shard_map/add | solution.py:80
  185.8 1.8 fusion.1
  187.7 0.9 fusion
  188.6 15.8 %all_to_all.53 = bf16[16,128,256]{2,1,0:T(8,128)(2,1)S(1)} all-to-all(bf16[16,128,256]{2,1,0:T(8,128)(2,1)S(1)} %bitcast.75), channel_id=1, replica_groups=mesh['seq'=32,'chan'=16] {'chan'}, dimensions={0} | all-to-all | bytes 2097152 | tf_op jit(solution)/shard_map/all_to_all | solution.py:115
  204.4 1.1 copy.70
  (58 shorter events, 4.9 us)
Async XLA Ops:
  0.0 1.6 slice-start
  5.4 7.7 %copy-start.7 = (f32[16,256]{1,0:T(8,128)S(1)}, f32[16,256]{1,0:T(8,128)}, u32[]{:S(2)}) copy-start(f32[16,256]{1,0:T(8,128)} %param.7) | copy-start | bytes 49156
  5.4 7.7 %copy-start.12 = (f32[16,256]{1,0:T(8,128)S(1)}, f32[16,256]{1,0:T(8,128)}, u32[]{:S(2)}) copy-start(f32[16,256]{1,0:T(8,128)} %param.8) | copy-start | bytes 49156
  5.4 33.0 %all-to-all-start = ((bf16[2,128,4096]{1,0,2:T(2,128)(2,1)}), bf16[2,128,4096]{1,0,2:T(2,128)(2,1)S(1)}, u32[]{:S(2)}, u32[]{:S(2)}) async-start(bf16[2,128,4096]{1,0,2:T(2,128)(2,1)} %copy.68), calls=%async_computation | async-start | bytes 4194304 | tf_op jit(solution)/shard_map/all_to_all | solution.py:92
  15.9 3.9 %copy-start.5 = (bf16[3,128,4096]{2,1,0:T(8,128)(2,1)S(1)}, bf16[3,128,4096]{2,1,0:T(8,128)(2,1)}, u32[]{:S(2)}) copy-start(bf16[3,128,4096]{2,1,0:T(8,128)(2,1)} %param.5) | copy-start | bytes 9437188
  38.4 1.3 copy-start.4
  44.4 14.7 %collective-permute-start = (bf16[2,2,256]{2,1,0:T(2,128)(2,1)S(1)}, bf16[2,2,256]{2,1,0:T(2,128)(2,1)S(1)}, u32[]{:S(2)}, u32[]{:S(2)}) collective-permute-start(bf16[2,2,256]{2,1,0:T(2,128)(2,1)S(1)} %slice.112), channel_id=1, source_target_pairs={{0,16},{16,32},{32,48},{48,64},{64,80},{80,96},{96,112},{112,128},... | collective-permute-start | bytes 6152 | tf_op jit(solution)/shard_map/ppermute | solution.py:14
  61.4 1.0 copy-start.2
  78.6 18.1 %all-to-all-start.1 = ((bf16[128,16,256]{2,0,1:T(8,128)(2,1)}), bf16[128,16,256]{2,0,1:T(8,128)(2,1)S(1)}, u32[]{:S(2)}, u32[]{:S(2)}) async-start(bf16[128,16,256]{2,0,1:T(8,128)(2,1)} %bitcast.73), calls=%async_computation.1 | async-start | bytes 2097152 | tf_op jit(solution)/shard_map/all_to_all | solution.py:101
  82.5 3.1 %copy-start.11 = (f32[16,256]{0,1:T(8,128)S(1)}, f32[16,256]{0,1:T(8,128)}, u32[]{:S(2)}) copy-start(f32[16,256]{0,1:T(8,128)} %copy.52) | copy-start | bytes 49156
  85.6 1.3 copy-start.10
  86.8 1.3 copy-start.8
  88.1 1.3 copy-start.9
  90.7 1.3 copy-start.1
  96.8 5.0 %copy-start.6 = (bf16[128,16,256]{2,0,1:T(8,128)(2,1)}, bf16[128,16,256]{2,0,1:T(8,128)(2,1)S(1)}, u32[]{:S(2)}) copy-start(bf16[128,16,256]{2,0,1:T(8,128)(2,1)S(1)} %all-to-all-done.1) | copy-start | bytes 3145732
  96.8 5.7 %collective-permute-start.1 = (bf16[1,2,256]{2,1,0:T(2,128)(2,1)S(1)}, bf16[1,2,256]{2,1,0:T(2,128)(2,1)S(1)}, u32[]{:S(2)}, u32[]{:S(2)}) collective-permute-start(bf16[1,2,256]{2,1,0:T(2,128)(2,1)S(1)} %slice.122), channel_id=1, source_target_pairs={{0,16},{16,32},{32,48},{48,64},{64,80},{80,96},{96,112},{112,128},... | collective-permute-start | bytes 3080 | tf_op jit(solution)/shard_map/ppermute | solution.py:14
  103.9 7.7 %collective-permute-start.2 = (f32[16,256]{1,0:T(8,128)S(1)}, f32[16,256]{1,0:T(8,128)S(1)}, u32[]{:S(2)}, u32[]{:S(2)}) collective-permute-start(f32[16,256]{1,0:T(8,128)S(1)} %bitcast_add_fusion.1), channel_id=1, source_target_pairs={{0,16},{16,32},{32,48},{48,64},{64,80},{80,96},{96,112},{112,128},... | collective-permute-start | bytes 49160 | tf_op jit(solution)/shard_map/ppermute | solution.py:14
  108.1 4.4 %collective-permute-start.3 = (f32[16,256]{1,0:T(8,128)S(1)}, f32[16,256]{1,0:T(8,128)S(1)}, u32[]{:S(2)}, u32[]{:S(2)}) collective-permute-start(f32[16,256]{1,0:T(8,128)S(1)} %bitcast_add_fusion.1), channel_id=1, source_target_pairs={{0,32},{16,48},{32,64},{48,80},{64,96},{80,112},{96,128},{112,144}... | collective-permute-start | bytes 49160 | tf_op jit(solution)/shard_map/ppermute | solution.py:14
  112.5 4.5 %collective-permute-start.4 = (f32[16,256]{1,0:T(8,128)S(1)}, f32[16,256]{1,0:T(8,128)S(1)}, u32[]{:S(2)}, u32[]{:S(2)}) collective-permute-start(f32[16,256]{1,0:T(8,128)S(1)} %multiply_add_fusion.9), channel_id=1, source_target_pairs={{0,32},{16,48},{32,64},{48,80},{64,96},{80,112},{96,128},{112,144}... | collective-permute-start | bytes 49160 | tf_op jit(solution)/shard_map/ppermute | solution.py:14
  117.1 9.9 %collective-permute-start.5 = (f32[16,256]{1,0:T(8,128)S(1)}, f32[16,256]{1,0:T(8,128)S(1)}, u32[]{:S(2)}, u32[]{:S(2)}) collective-permute-start(f32[16,256]{1,0:T(8,128)S(1)} %multiply_add_fusion.8), channel_id=1, source_target_pairs={{0,64},{16,80},{32,96},{48,112},{64,128},{80,144},{96,160},{112,17... | collective-permute-start | bytes 49160 | tf_op jit(solution)/shard_map/ppermute | solution.py:14
  127.0 20.0 %collective-permute-start.6 = (f32[16,256]{1,0:T(8,128)S(1)}, f32[16,256]{1,0:T(8,128)S(1)}, u32[]{:S(2)}, u32[]{:S(2)}) collective-permute-start(f32[16,256]{1,0:T(8,128)S(1)} %multiply_add_fusion.7), channel_id=1, source_target_pairs={{0,128},{16,144},{32,160},{48,176},{64,192},{80,208},{96,224},{112... | collective-permute-start | bytes 49160 | tf_op jit(solution)/shard_map/ppermute | solution.py:14
  137.7 20.7 %copy-start = (bf16[32,64,256]{1,0,2:T(8,128)(2,1)S(1)}, bf16[32,64,256]{1,0,2:T(8,128)(2,1)}, u32[]{:S(2)}) copy-start(bf16[32,64,256]{1,0,2:T(8,128)(2,1)} %copy.48) | copy-start | bytes 3145732
  147.0 21.6 %collective-permute-start.7 = (f32[16,256]{1,0:T(8,128)S(1)}, f32[16,256]{1,0:T(8,128)S(1)}, u32[]{:S(2)}, u32[]{:S(2)}) collective-permute-start(f32[16,256]{1,0:T(8,128)S(1)} %multiply_add_fusion.6), channel_id=1, source_target_pairs={{0,256},{16,272},{32,288},{48,304},{64,320},{80,336},{96,352},{112... | collective-permute-start | bytes 49160 | tf_op jit(solution)/shard_map/ppermute | solution.py:14
  181.2 4.7 %copy-start.3 = (bf16[2048,256]{1,0:T(8,128)(2,1)S(1)}, bf16[2048,256]{1,0:T(8,128)(2,1)}, u32[]{:S(2)}) copy-start(bf16[2048,256]{1,0:T(8,128)(2,1)} %copy-done.2) | copy-start | bytes 3145732
  181.2 4.7 %copy-start.13 = (f32[256]{0:T(256)S(1)}, f32[256]{0:T(256)}, u32[]{:S(2)}) copy-start(f32[256]{0:T(256)} %param.9) | copy-start | bytes 3076

commit v6 on v5

--- a/solution.py
+++ b/solution.py
@@ -64,15 +64,12 @@
     end_state = jnp.exp(-decay_rate * float(block)) * starts[count - 1] + local_end[count - 1]
     end_state, passenger = lax.optimization_barrier((end_state, passenger))
     sections = lax.axis_size("seq")
-    incoming = from_behind(end_state, "seq", 1)
-    if sections > 2:
-        incoming = incoming + jnp.exp(-decay_rate * float(section)) * from_behind(end_state, "seq", 2)
-    step = 2
-    while step < sections:
-        incoming = incoming + jnp.exp(-decay_rate * float(section * step)) * from_behind(
-            incoming, "seq", step
-        )
-        step *= 2
+    here = lax.axis_index("seq")
+    later = jnp.arange(sections)
+    lag = jnp.maximum(later - 1 - here, 0).astype(jnp.float32)
+    weight = jnp.exp(-decay_rate[None, :, :] * (section * lag)[:, None, None])
+    weight = jnp.where((later > here)[:, None, None], weight, 0.0)
+    incoming = lax.psum_scatter(weight * end_state[None], "seq", scatter_dimension=0, tiled=True)[0]
     inner = jnp.einsum("ijc,kjc->kic", toeplitz, pieces, precision=lax.Precision.HIGHEST)
     block_starts = (jnp.arange(count).astype(jnp.float32) * block)[:, None, None]
     starts = starts + jnp.exp(-decay_rate[None, :, :] * block_starts) * incoming[None, :, :]

time: 209 us -> 279 us (1.33)
  waiting for transfers between devices: 24 us -> 111 us
  starting transfers between devices: 69.7 us -> 27.4 us
  between operations: 0.42 us -> 13.7 us
  local copies, waits for them, and re-layouts: 47.6 us -> 52.4 us
  blocking collectives: 15.8 us -> 19.7 us
  other arithmetic: 16.3 us -> 19.6 us
    reduce_scatter x0 -> x1, waiting for transfers between devices: none -> 90.6 us  [long_part(): lax.psum_scatter(weight * end_state[None], 'seq', scatter_dimension=0, ti...]
    ppermute x8 -> x2, starting transfers between devices: 58.2 us -> 15.8 us  [from_behind(): return lax.ppermute(block, axis, route)]
    all_to_all x1, blocking collectives: 15.8 us -> 19.7 us  [local(): lax.all_to_all(gated, 'chan', split_axis=0, concat_axis=1, tiled=True)]
    unnamed x31 -> x39, local copies, waits for them, and re-layouts: 7.43 us -> 7.43 us
  transfers between devices with their start and end apart: 10 -> 5, of which waited for: 5 -> 4; matrix products, arithmetic and copies ran while one was open for 20% -> 16% of each run, Pallas kernels for 0% -> 0%
where the time goes in v6:
time: 279 us; the launch traced here: 276 us
  waiting for transfers between devices  111 us (40%)
  local copies, waits for them, and re-layouts  52.4 us (19%)
  matrix products  31.6 us (11%)
  starting transfers between devices  27.4 us (10%)
  blocking collectives  19.7 us (7%)
  other arithmetic  19.6 us (7%)
  between operations  13.7 us (5%)
    reduce_scatter x1, waiting for transfers between devices, long_part(): lax.psum_scatter(weight * end_state[None], 'seq', scatter_dimension=0, ti...  90.6 us
    all_to_all x1, blocking collectives, local(): lax.all_to_all(gated, 'chan', split_axis=0, concat_axis=1, tiled=True)  19.7 us
    all_to_all x1, waiting for transfers between devices, arrive(): lax.all_to_all(streams, 'chan', split_axis=2, concat_axis=1, tiled=True)  16.8 us
    ppermute x2, starting transfers between devices, from_behind(): return lax.ppermute(block, axis, route)  15.8 us
    dot_general x1, matrix products, long_part(): jnp.einsum('nic,knc->kic', reading, starts, precision=lax.Precision.HIGHEST)  12.4 us
    dot_general x1, matrix products, long_part(): jnp.einsum('ijc,kjc->kic', toeplitz, pieces, precision=lax.Precision.HIGH...  10.3 us
    optimization_barrier x1, local copies, waits for them, and re-layouts, local(): lax.optimization_barrier((keys_values, features[0], toeplitz))  9.44 us
    add x5, other arithmetic, long_part(): starts + jnp.exp(-decay_rate * float(block * step)) * shifted(starts, step)  8.07 us
  transfers between devices with their start and end apart: 5, of which 4 were waited for; matrix products, arithmetic and copies ran while one was open for 16% of the time, Pallas kernels for 0%

profile of v6, /device:TPU:1, one launch (start us, length us, event | category | flops | bytes accessed | tf_op | source)
XLA Modules:
  0.0 275.7 jit_solution(15810680884925161711)
XLA Ops:
  6.5 1.6 slice-done
  8.1 3.8 %copy.72 = bf16[2,128,4096]{1,0,2:T(2,128)(2,1)} copy(bf16[2,128,4096]{2,1,0:T(8,128)(2,1)S(1)} %slice-done) | data formatting | bytes 4194304
  11.9 7.7 %all-to-all-start = ((bf16[2,128,4096]{1,0,2:T(2,128)(2,1)}), bf16[2,128,4096]{1,0,2:T(2,128)(2,1)S(1)}, u32[]{:S(2)}, u32[]{:S(2)}) async-start(bf16[2,128,4096]{1,0,2:T(2,128)(2,1)} %copy.72), calls=%async_computation | async-start | bytes 4194304 | tf_op jit(solution)/shard_map/all_to_all | solution.py:89
  21.6 0.9 constant_dynamic-slice_fusion.1
  22.5 1.6 multiply_reduce_fusion
  24.1 3.9 %fusion.12 = f32[64,64,256]{2,1,0:T(8,128)} fusion(s32[64,64]{1,0:T(8,128)S(1)} %iota_subtract_fusion, f32[64,256]{0,1:T(8,128)S(1)} %multiply_reduce_fusion), kind=kOutput, calls=%fused_computation.27 | convolution fusion | flops 805568512 | bytes 4276224 | tf_op jit(solution)/shard_map/dot_general | solution.py:36
  28.1 16.8 %all-to-all-done = bf16[2,128,4096]{1,0,2:T(2,128)(2,1)S(1)} async-done(((bf16[2,128,4096]{1,0,2:T(2,128)(2,1)}), bf16[2,128,4096]{1,0,2:T(2,128)(2,1)S(1)}, u32[]{:S(2)}, u32[]{:S(2)}) %all-to-all-start) | async-done | bytes 2097184 | tf_op jit(solution)/shard_map/all_to_all | solution.py:89
  44.9 1.3 copy-done.4
  46.2 4.7 %copy.46 = bf16[2,128,16,256]{3,1,2,0:T(8,128)(2,1)S(1)} copy(bf16[2,128,16,256]{1,0,3,2:T(2,128)(2,1)} %bitcast.70) | data formatting | bytes 4194304 | tf_op jit(solution)/shard_map/all_to_all | solution.py:89
  51.5 10.9 %collective-permute-start = (bf16[2,2,256]{2,1,0:T(2,128)(2,1)}, bf16[2,2,256]{2,1,0:T(2,128)(2,1)S(1)}, u32[]{:S(2)}, u32[]{:S(2)}) collective-permute-start(bf16[2,2,256]{2,1,0:T(2,128)(2,1)} %slice.112), channel_id=1, source_target_pairs={{0,16},{16,32},{32,48},{48,64},{64,80},{80,96},{96,112},{112,128},... | collective-permute-start | bytes 6152 | tf_op jit(solution)/shard_map/ppermute | solution.py:14
  63.0 0.7 copy.53
  63.7 0.8 copy.54
  64.5 0.7 copy.55
  65.2 0.8 copy.56
  66.0 1.5 copy.57
  68.0 1.4 add_convert_fusion
  69.8 1.0 copy-done.2
  70.7 3.8 %copy.50 = bf16[32,64,256]{1,0,2:T(8,128)(2,1)} copy(bf16[32,64,256]{2,1,0:T(8,128)(2,1)S(1)} %bitcast.67) | data formatting | bytes 2097152 | tf_op jit(solution)/shard_map/reshape | solution.py:57
  74.5 5.0 %fusion.13 = f32[32,16,256]{0,1,2:T(8,128)S(1)} fusion(bf16[32,64,256]{1,0,2:T(8,128)(2,1)} %copy.50, f32[64]{0:T(128)S(1)} %copy-done.15, f32[16,256]{0,1:T(8,128)S(1)} %copy.48), kind=kOutput, calls=%fused_computation.29 | convolution fusion | flops 100925440 | bytes 1589504 | tf_op jit(solution)/shard_map/njc,kjc->knc/dot_general | solution.py:58
  79.6 1.9 slice.121
  81.5 1.9 pad_slice_fusion
  83.4 3.1 %copy.60 = f32[1,16,256]{2,1,0:T(8,128)} copy(f32[1,16,256]{0,1,2:T(8,128)} %slice.121) | data formatting | bytes 32768 | tf_op jit(solution)/shard_map/slice | solution.py:64
  86.5 1.1 copy.79
  87.6 3.7 %all-to-all-start.1 = ((bf16[128,16,256]{2,0,1:T(8,128)(2,1)}), bf16[128,16,256]{2,0,1:T(8,128)(2,1)S(1)}, u32[]{:S(2)}, u32[]{:S(2)}) async-start(bf16[128,16,256]{2,0,1:T(8,128)(2,1)} %bitcast.74), calls=%async_computation.1 | async-start | bytes 2097152 | tf_op jit(solution)/shard_map/all_to_all | solution.py:98
  91.5 3.1 %multiply_add_fusion.4 = f32[32,16,256]{0,1,2:T(8,128)S(1)} fusion(f32[31,16,256]{0,1,2:T(8,128)} %pad_slice_fusion, f32[31,16,256]{0,1,2:T(8,128)S(1)} %bitcast.62, f32[16,256]{0,1:T(8,128)} %copy.53), kind=kLoop, calls=%fused_computation.20 | loop fusion | flops 262144 | bytes 1556480 | tf_op jit(solution)/shard_map/add | solution.py:62
  94.6 1.3 multiply_add_fusion.3
  95.9 1.3 multiply_add_fusion.2
  97.1 1.3 multiply_add_fusion.1
  98.4 1.3 multiply_add_fusion
  99.7 1.3 copy-done.1
  101.6 1.0 copy.59
  102.7 3.1 %all-to-all-done.1 = bf16[128,16,256]{2,0,1:T(8,128)(2,1)S(1)} async-done(((bf16[128,16,256]{2,0,1:T(8,128)(2,1)}), bf16[128,16,256]{2,0,1:T(8,128)(2,1)S(1)}, u32[]{:S(2)}, u32[]{:S(2)}) %all-to-all-start.1) | async-done | bytes 1048608 | tf_op jit(solution)/shard_map/all_to_all | solution.py:98
  105.8 5.0 %collective-permute-start.1 = (bf16[1,2,256]{2,1,0:T(2,128)(2,1)S(1)}, bf16[1,2,256]{2,1,0:T(2,128)(2,1)S(1)}, u32[]{:S(2)}, u32[]{:S(2)}) collective-permute-start(bf16[1,2,256]{2,1,0:T(2,128)(2,1)S(1)} %slice.122), channel_id=1, source_target_pairs={{0,16},{16,32},{32,48},{48,64},{64,80},{80,96},{96,112},{112,128},... | collective-permute-start | bytes 3080 | tf_op jit(solution)/shard_map/ppermute | solution.py:14
  110.8 0.7 collective-permute-done.1
  111.4 1.5 pad_maximum_fusion.1
  113.0 1.1 select_multiply_fusion
  114.2 2.0 copy.63
  116.2 0.9 constant_dynamic-slice_fusion.2
  117.1 9.4 %copy.51 = f32[64,64,256]{1,0,2:T(8,128)} copy(f32[64,64,256]{2,1,0:T(8,128)} %fusion.12) | data formatting | bytes 8388608 | tf_op jit(solution)/shard_map/optimization_barrier | solution.py:97
  126.5 10.3 %fusion.28 = f32[256,32,64]{2,1,0:T(8,128)} fusion(bf16[32,64,256]{1,0,2:T(8,128)(2,1)S(1)} %copy-done, f32[64,64,256]{1,0,2:T(8,128)} %copy.51), kind=kOutput, calls=%fused_computation.67 | convolution fusion | flops 402653184 | bytes 7340032 | tf_op jit(solution)/shard_map/ijc,kjc->kic/dot_general | solution.py:73
  136.8 90.6 %reduce-scatter.2.cloned.1.call-done = f32[1,16,256]{2,1,0:T(8,128)} async-done(((f32[32,16,256]{2,1,0:T(8,128)}), f32[1,16,256]{2,1,0:T(8,128)}) %reduce-scatter.2.cloned.1.call-update) | async-done | bytes 16400 | tf_op jit(solution)/shard_map/reduce_scatter | solution.py:72
  227.4 0.8 copy.64
  228.2 12.4 %add_bitcast_fusion = f32[32,64,256]{1,0,2:T(8,128)} fusion(f32[256,32,64]{2,1,0:T(8,128)} %fusion.28, f32[32,16,256]{0,1,2:T(8,128)} %copy-done.1, f32[64]{0:T(128)S(1)} %broadcast_add_fusion, f32[16,256]{0,1:T(8,128)S(1)} %copy.64, f32[32]{0:T(128)S(1)} %convert_multiply_fusion.2, f32[16,256]{0,1:T(8,128)S(1)} %copy.48, f32[16,256]{0,1:T(8,128)S(1)} %copy.47), kind=kOutput, calls=%fused_computation | convolution fusion | flops 102105088 | bytes 4768128 | tf_op jit(solution)/shard_map/nic,knc->kic/dot_general | solution.py:76
  240.7 4.6 %copy.65 = f32[32,64,256]{2,1,0:T(8,128)} copy(f32[32,64,256]{1,0,2:T(8,128)} %add_bitcast_fusion) | data formatting | bytes 4194304 | tf_op jit(solution)/shard_map/add | solution.py:77
  245.3 1.8 fusion.1
  247.1 0.9 fusion
  248.1 19.7 %all_to_all.53 = bf16[16,128,256]{2,1,0:T(8,128)(2,1)S(1)} all-to-all(bf16[16,128,256]{2,1,0:T(8,128)(2,1)S(1)} %bitcast.76), channel_id=1, replica_groups=mesh['seq'=32,'chan'=16] {'chan'}, dimensions={0} | all-to-all | bytes 2097152 | tf_op jit(solution)/shard_map/all_to_all | solution.py:112
  267.8 1.1 copy.74
  (57 shorter events, 5.1 us)
Async XLA Ops:
  6.5 1.6 slice-start
  11.9 8.3 %copy-start.11 = (f32[16,256]{1,0:T(8,128)S(1)}, f32[16,256]{1,0:T(8,128)}, u32[]{:S(2)}) copy-start(f32[16,256]{1,0:T(8,128)} %param.7) | copy-start | bytes 49156
  11.9 8.3 %copy-start.13 = (f32[16,256]{1,0:T(8,128)S(1)}, f32[16,256]{1,0:T(8,128)}, u32[]{:S(2)}) copy-start(f32[16,256]{1,0:T(8,128)} %param.8) | copy-start | bytes 49156
  11.9 33.0 %all-to-all-start = ((bf16[2,128,4096]{1,0,2:T(2,128)(2,1)}), bf16[2,128,4096]{1,0,2:T(2,128)(2,1)S(1)}, u32[]{:S(2)}, u32[]{:S(2)}) async-start(bf16[2,128,4096]{1,0,2:T(2,128)(2,1)} %copy.72), calls=%async_computation | async-start | bytes 4194304 | tf_op jit(solution)/shard_map/all_to_all | solution.py:89
  24.1 3.9 %copy-start.5 = (bf16[3,128,4096]{2,1,0:T(8,128)(2,1)S(1)}, bf16[3,128,4096]{2,1,0:T(8,128)(2,1)}, u32[]{:S(2)}) copy-start(bf16[3,128,4096]{2,1,0:T(8,128)(2,1)} %param.5) | copy-start | bytes 9437188
  44.9 1.3 copy-start.4
  51.5 16.0 %collective-permute-start = (bf16[2,2,256]{2,1,0:T(2,128)(2,1)}, bf16[2,2,256]{2,1,0:T(2,128)(2,1)S(1)}, u32[]{:S(2)}, u32[]{:S(2)}) collective-permute-start(bf16[2,2,256]{2,1,0:T(2,128)(2,1)} %slice.112), channel_id=1, source_target_pairs={{0,16},{16,32},{32,48},{48,64},{64,80},{80,96},{96,112},{112,128},... | collective-permute-start | bytes 6152 | tf_op jit(solution)/shard_map/ppermute | solution.py:14
  69.7 1.0 copy-start.2
  69.8 4.8 %copy-start.15 = (f32[64]{0:T(128)S(1)}, f32[64]{0:T(128)}, u32[]{:S(2)}) copy-start(f32[64]{0:T(128)} %broadcast_subtract_fusion) | copy-start | bytes 772
  87.6 18.1 %all-to-all-start.1 = ((bf16[128,16,256]{2,0,1:T(8,128)(2,1)}), bf16[128,16,256]{2,0,1:T(8,128)(2,1)S(1)}, u32[]{:S(2)}, u32[]{:S(2)}) async-start(bf16[128,16,256]{2,0,1:T(8,128)(2,1)} %bitcast.74), calls=%async_computation.1 | async-start | bytes 2097152 | tf_op jit(solution)/shard_map/all_to_all | solution.py:98
  91.3 136.1 %reduce-scatter.2.cloned.1.call-start = ((), (), s32[]{:S(2)}) async-start(), calls=%async_computation.4 | async-start | bytes 540672 | tf_op jit(solution)/shard_map/reduce_scatter | solution.py:72
  91.5 3.1 %copy-start.9 = (f32[16,256]{0,1:T(8,128)S(1)}, f32[16,256]{0,1:T(8,128)}, u32[]{:S(2)}) copy-start(f32[16,256]{0,1:T(8,128)} %copy.54) | copy-start | bytes 49156
  94.6 1.3 copy-start.8
  97.1 1.3 copy-start.7
  99.7 1.3 copy-start.1
  101.6 9.1 %copy-start.10 = (f32[1,16,256]{2,1,0:T(8,128)S(1)}, f32[1,16,256]{2,1,0:T(8,128)}, u32[]{:S(2)}) copy-start(f32[1,16,256]{2,1,0:T(8,128)} %copy.60) | copy-start | bytes 49156
  101.6 9.1 %copy-start.12 = (f32[16,256]{1,0:T(8,128)S(1)}, f32[16,256]{1,0:T(8,128)}, u32[]{:S(2)}) copy-start(f32[16,256]{1,0:T(8,128)} %param.7) | copy-start | bytes 49156
  101.6 11.4 %copy-start.16 = (f32[32]{0:T(128)S(1)}, f32[32]{0:T(128)}, u32[]{:S(2)}) copy-start(f32[32]{0:T(128)} %convert_multiply_fusion.1) | copy-start | bytes 388
  101.6 11.4 %copy-start.17 = (pred[32]{0:T(512)(128)(4,1)S(1)}, pred[32]{0:T(512)(128)(4,1)}, u32[]{:S(2)}) copy-start(pred[32]{0:T(512)(128)(4,1)} %iota_compare_fusion.2) | copy-start | bytes 100
  105.7 5.0 %copy-start.6 = (bf16[128,16,256]{2,0,1:T(8,128)(2,1)}, bf16[128,16,256]{2,0,1:T(8,128)(2,1)S(1)}, u32[]{:S(2)}) copy-start(bf16[128,16,256]{2,0,1:T(8,128)(2,1)S(1)} %all-to-all-done.1) | copy-start | bytes 3145732
  105.8 5.7 %collective-permute-start.1 = (bf16[1,2,256]{2,1,0:T(2,128)(2,1)S(1)}, bf16[1,2,256]{2,1,0:T(2,128)(2,1)S(1)}, u32[]{:S(2)}, u32[]{:S(2)}) collective-permute-start(bf16[1,2,256]{2,1,0:T(2,128)(2,1)S(1)} %slice.122), channel_id=1, source_target_pairs={{0,16},{16,32},{32,48},{48,64},{64,80},{80,96},{96,112},{112,128},... | collective-permute-start | bytes 3080 | tf_op jit(solution)/shard_map/ppermute | solution.py:14
  117.1 9.4 %copy-start = (bf16[32,64,256]{1,0,2:T(8,128)(2,1)S(1)}, bf16[32,64,256]{1,0,2:T(8,128)(2,1)}, u32[]{:S(2)}) copy-start(bf16[32,64,256]{1,0,2:T(8,128)(2,1)} %copy.50) | copy-start | bytes 3145732
  240.7 4.6 %copy-start.3 = (bf16[2048,256]{1,0:T(8,128)(2,1)S(1)}, bf16[2048,256]{1,0:T(8,128)(2,1)}, u32[]{:S(2)}) copy-start(bf16[2048,256]{1,0:T(8,128)(2,1)} %copy-done.2) | copy-start | bytes 3145732
  240.7 4.6 %copy-start.14 = (f32[256]{0:T(256)S(1)}, f32[256]{0:T(256)}, u32[]{:S(2)}) copy-start(f32[256]{0:T(256)} %param.9) | copy-start | bytes 3076
Sparse Core Ops, SparseCore 0:
  116.3 111.0 reduce-scatter.1

commit v7 on v6

--- a/solution.py
+++ b/solution.py
@@ -64,12 +64,20 @@
     end_state = jnp.exp(-decay_rate * float(block)) * starts[count - 1] + local_end[count - 1]
     end_state, passenger = lax.optimization_barrier((end_state, passenger))
     sections = lax.axis_size("seq")
-    here = lax.axis_index("seq")
-    later = jnp.arange(sections)
-    lag = jnp.maximum(later - 1 - here, 0).astype(jnp.float32)
-    weight = jnp.exp(-decay_rate[None, :, :] * (section * lag)[:, None, None])
-    weight = jnp.where((later > here)[:, None, None], weight, 0.0)
-    incoming = lax.psum_scatter(weight * end_state[None], "seq", scatter_dimension=0, tiled=True)[0]
+    radix = 4
+    incoming = jnp.zeros_like(end_state)
+    for distance in range(1, min(radix, sections - 1) + 1):
+        weight = jnp.exp(-decay_rate * float(section * (distance - 1)))
+        incoming = incoming + weight * from_behind(end_state, "seq", distance)
+    span = radix
+    while span < sections:
+        total = incoming
+        for multiple in range(1, radix):
+            if span * multiple < sections:
+                weight = jnp.exp(-decay_rate * float(section * span * multiple))
+                total = total + weight * from_behind(incoming, "seq", span * multiple)
+        incoming = total
+        span *= radix
     inner = jnp.einsum("ijc,kjc->kic", toeplitz, pieces, precision=lax.Precision.HIGHEST)
     block_starts = (jnp.arange(count).astype(jnp.float32) * block)[:, None, None]
     starts = starts + jnp.exp(-decay_rate[None, :, :] * block_starts) * incoming[None, :, :]

time: 279 us -> 206 us (0.74)
  waiting for transfers between devices: 111 us -> 21.8 us
  starting transfers between devices: 27.4 us -> 64.5 us
  between operations: 13.7 us -> 0.46 us
  blocking collectives: 19.7 us -> 16.7 us
    reduce_scatter x1 -> x0, waiting for transfers between devices: 90.6 us -> none  [long_part(): lax.psum_scatter(weight * end_state[None], 'seq', scatter_dimension=0, ti...]
    ppermute x2 -> x10, starting transfers between devices: 15.8 us -> 52.9 us  [from_behind(): return lax.ppermute(block, axis, route)]
    all_to_all x1, blocking collectives: 19.7 us -> 16.7 us  [local(): lax.all_to_all(gated, 'chan', split_axis=0, concat_axis=1, tiled=True)]
  transfers between devices with their start and end apart: 5 -> 12, of which waited for: 4 -> 4; matrix products, arithmetic and copies ran while one was open for 16% -> 21% of each run, Pallas kernels for 0% -> 0%
where the time goes in v7:
time: 206 us; the launch traced here: 204 us
  starting transfers between devices  64.5 us (31%)
  local copies, waits for them, and re-layouts  50.2 us (24%)
  matrix products  31.6 us (15%)
  waiting for transfers between devices  21.8 us (11%)
  other arithmetic  18.2 us (9%)
  blocking collectives  16.7 us (8%)
    ppermute x10, starting transfers between devices, from_behind(): return lax.ppermute(block, axis, route)  52.9 us
    all_to_all x1, blocking collectives, local(): lax.all_to_all(gated, 'chan', split_axis=0, concat_axis=1, tiled=True)  16.7 us
    all_to_all x1, waiting for transfers between devices, arrive(): lax.all_to_all(streams, 'chan', split_axis=2, concat_axis=1, tiled=True)  16.5 us
    dot_general x1, matrix products, long_part(): jnp.einsum('nic,knc->kic', reading, starts, precision=lax.Precision.HIGHEST)  12.5 us
    dot_general x1, matrix products, long_part(): jnp.einsum('ijc,kjc->kic', toeplitz, pieces, precision=lax.Precision.HIGH...  10.3 us
    optimization_barrier x1, local copies, waits for them, and re-layouts, local(): lax.optimization_barrier((keys_values, features[0], toeplitz))  9.32 us
    add x5, other arithmetic, long_part(): starts + jnp.exp(-decay_rate * float(block * step)) * shifted(starts, step)  8.07 us
    all_to_all x1, starting transfers between devices, arrive(): lax.all_to_all(streams, 'chan', split_axis=2, concat_axis=1, tiled=True)  7.7 us
  transfers between devices with their start and end apart: 12, of which 4 were waited for; matrix products, arithmetic and copies ran while one was open for 21% of the time, Pallas kernels for 0%

profile of v7, /device:TPU:1, one launch (start us, length us, event | category | flops | bytes accessed | tf_op | source)
XLA Modules:
  0.0 203.5 jit_solution(17142382949549706285)
XLA Ops:
  0.0 1.6 slice-done
  1.6 3.8 %copy.68 = bf16[2,128,4096]{1,0,2:T(2,128)(2,1)} copy(bf16[2,128,4096]{2,1,0:T(8,128)(2,1)S(1)} %slice-done) | data formatting | bytes 4194304
  5.4 7.7 %all-to-all-start = ((bf16[2,128,4096]{1,0,2:T(2,128)(2,1)}), bf16[2,128,4096]{1,0,2:T(2,128)(2,1)S(1)}, u32[]{:S(2)}, u32[]{:S(2)}) async-start(bf16[2,128,4096]{1,0,2:T(2,128)(2,1)} %copy.68), calls=%async_computation | async-start | bytes 4194304 | tf_op jit(solution)/shard_map/all_to_all | solution.py:97
  13.7 1.5 constant_dynamic-slice_fusion.2
  16.3 1.6 multiply_reduce_fusion
  17.9 3.8 %fusion.12 = f32[64,64,256]{2,1,0:T(8,128)} fusion(s32[64,64]{1,0:T(8,128)S(1)} %iota_subtract_fusion, f32[64,256]{0,1:T(8,128)S(1)} %multiply_reduce_fusion), kind=kOutput, calls=%fused_computation.26 | convolution fusion | flops 805568512 | bytes 4276224 | tf_op jit(solution)/shard_map/dot_general | solution.py:36
  21.9 16.5 %all-to-all-done = bf16[2,128,4096]{1,0,2:T(2,128)(2,1)S(1)} async-done(((bf16[2,128,4096]{1,0,2:T(2,128)(2,1)}), bf16[2,128,4096]{1,0,2:T(2,128)(2,1)S(1)}, u32[]{:S(2)}, u32[]{:S(2)}) %all-to-all-start) | async-done | bytes 2097184 | tf_op jit(solution)/shard_map/all_to_all | solution.py:97
  38.4 1.3 copy-done.4
  39.7 4.7 %copy.44 = bf16[2,128,16,256]{3,1,2,0:T(8,128)(2,1)S(1)} copy(bf16[2,128,16,256]{1,0,3,2:T(2,128)(2,1)} %bitcast.69) | data formatting | bytes 4194304 | tf_op jit(solution)/shard_map/all_to_all | solution.py:97
  45.0 10.9 %collective-permute-start = (bf16[2,2,256]{2,1,0:T(2,128)(2,1)}, bf16[2,2,256]{2,1,0:T(2,128)(2,1)}, u32[]{:S(2)}, u32[]{:S(2)}) collective-permute-start(bf16[2,2,256]{2,1,0:T(2,128)(2,1)} %slice.112), channel_id=1, source_target_pairs={{0,16},{16,32},{32,48},{48,64},{64,80},{80,96},{96,112},{112,128},... | collective-permute-start | bytes 6152 | tf_op jit(solution)/shard_map/ppermute | solution.py:14
  59.6 1.5 copy.55
  61.0 1.2 pad_maximum_fusion
  62.3 1.4 add_convert_fusion
  64.0 1.0 copy-done.2
  65.0 3.8 %copy.48 = bf16[32,64,256]{1,0,2:T(8,128)(2,1)} copy(bf16[32,64,256]{2,1,0:T(8,128)(2,1)S(1)} %bitcast.66) | data formatting | bytes 2097152 | tf_op jit(solution)/shard_map/reshape | solution.py:57
  68.8 5.0 %fusion.13 = f32[32,16,256]{0,1,2:T(8,128)S(1)} fusion(bf16[32,64,256]{1,0,2:T(8,128)(2,1)} %copy.48, f32[64]{0:T(128)S(1)} %copy-done.17, f32[16,256]{0,1:T(8,128)S(1)} %copy.46), kind=kOutput, calls=%fused_computation.28 | convolution fusion | flops 100925440 | bytes 1589504 | tf_op jit(solution)/shard_map/njc,kjc->knc/dot_general | solution.py:58
  73.8 1.9 slice.121
  75.7 2.0 pad_slice_fusion
  77.7 3.1 %copy.58 = f32[1,16,256]{2,1,0:T(8,128)} copy(f32[1,16,256]{0,1,2:T(8,128)} %slice.121) | data formatting | bytes 32768 | tf_op jit(solution)/shard_map/slice | solution.py:64
  80.8 1.1 copy.75
  81.9 3.8 %all-to-all-start.1 = ((bf16[128,16,256]{2,0,1:T(8,128)(2,1)}), bf16[128,16,256]{2,0,1:T(8,128)(2,1)S(1)}, u32[]{:S(2)}, u32[]{:S(2)}) async-start(bf16[128,16,256]{2,0,1:T(8,128)(2,1)} %bitcast.73), calls=%async_computation.1 | async-start | bytes 2097152 | tf_op jit(solution)/shard_map/all_to_all | solution.py:106
  85.8 3.1 %multiply_add_fusion.4 = f32[32,16,256]{0,1,2:T(8,128)S(1)} fusion(f32[31,16,256]{0,1,2:T(8,128)} %pad_slice_fusion, f32[31,16,256]{0,1,2:T(8,128)S(1)} %bitcast.61, f32[16,256]{0,1:T(8,128)} %copy.51), kind=kLoop, calls=%fused_computation.19 | loop fusion | flops 262144 | bytes 1556480 | tf_op jit(solution)/shard_map/add | solution.py:62
  88.8 1.3 multiply_add_fusion.3
  90.1 1.3 multiply_add_fusion.2
  91.4 1.3 multiply_add_fusion.1
  92.7 1.3 multiply_add_fusion
  93.9 1.3 copy-done.1
  95.8 1.0 copy.57
  96.9 3.7 %all-to-all-done.1 = bf16[128,16,256]{2,0,1:T(8,128)(2,1)S(1)} async-done(((bf16[128,16,256]{2,0,1:T(8,128)(2,1)}), bf16[128,16,256]{2,0,1:T(8,128)(2,1)S(1)}, u32[]{:S(2)}, u32[]{:S(2)}) %all-to-all-start.1) | async-done | bytes 1048608 | tf_op jit(solution)/shard_map/all_to_all | solution.py:106
  100.6 4.4 %collective-permute-start.1 = (bf16[1,2,256]{2,1,0:T(2,128)(2,1)S(1)}, bf16[1,2,256]{2,1,0:T(2,128)(2,1)S(1)}, u32[]{:S(2)}, u32[]{:S(2)}) collective-permute-start(bf16[1,2,256]{2,1,0:T(2,128)(2,1)S(1)} %slice.122), channel_id=1, source_target_pairs={{0,16},{16,32},{32,48},{48,64},{64,80},{80,96},{96,112},{112,128},... | collective-permute-start | bytes 3080 | tf_op jit(solution)/shard_map/ppermute | solution.py:14
  105.7 1.5 pad_maximum_fusion.1
  107.2 4.4 %collective-permute-start.5 = (f32[16,256]{1,0:T(8,128)S(1)}, f32[16,256]{1,0:T(8,128)S(1)}, u32[]{:S(2)}, u32[]{:S(2)}) collective-permute-start(f32[16,256]{1,0:T(8,128)S(1)} %bitcast_add_fusion.1), channel_id=1, source_target_pairs={{0,64},{16,80},{32,96},{48,112},{64,128},{80,144},{96,160},{112,17... | collective-permute-start | bytes 49160 | tf_op jit(solution)/shard_map/ppermute | solution.py:14
  111.6 8.7 %collective-permute-start.4 = (f32[16,256]{1,0:T(8,128)S(1)}, f32[16,256]{1,0:T(8,128)S(1)}, u32[]{:S(2)}, u32[]{:S(2)}) collective-permute-start(f32[16,256]{1,0:T(8,128)S(1)} %bitcast_add_fusion.1), channel_id=1, source_target_pairs={{0,48},{16,64},{32,80},{48,96},{64,112},{80,128},{96,144},{112,160... | collective-permute-start | bytes 49160 | tf_op jit(solution)/shard_map/ppermute | solution.py:14
  120.3 2.3 %collective-permute-start.3 = (f32[16,256]{1,0:T(8,128)S(1)}, f32[16,256]{1,0:T(8,128)S(1)}, u32[]{:S(2)}, u32[]{:S(2)}) collective-permute-start(f32[16,256]{1,0:T(8,128)S(1)} %bitcast_add_fusion.1), channel_id=1, source_target_pairs={{0,32},{16,48},{32,64},{48,80},{64,96},{80,112},{96,128},{112,144}... | collective-permute-start | bytes 49160 | tf_op jit(solution)/shard_map/ppermute | solution.py:14
  122.7 2.1 %collective-permute-start.2 = (f32[16,256]{1,0:T(8,128)S(1)}, f32[16,256]{1,0:T(8,128)S(1)}, u32[]{:S(2)}, u32[]{:S(2)}) collective-permute-start(f32[16,256]{1,0:T(8,128)S(1)} %bitcast_add_fusion.1), channel_id=1, source_target_pairs={{0,16},{16,32},{32,48},{48,64},{64,80},{80,96},{96,112},{112,128},... | collective-permute-start | bytes 49160 | tf_op jit(solution)/shard_map/ppermute | solution.py:14
  124.8 1.0 collective-permute-done.2
  125.8 12.1 %collective-permute-start.8 = (f32[16,256]{1,0:T(8,128)S(1)}, f32[16,256]{1,0:T(8,128)S(1)}, u32[]{:S(2)}, u32[]{:S(2)}) collective-permute-start(f32[16,256]{1,0:T(8,128)S(1)} %multiply_add_fusion.7), channel_id=1, source_target_pairs={{0,192},{16,208},{32,224},{48,240},{64,256},{80,272},{96,288},{112... | collective-permute-start | bytes 49160 | tf_op jit(solution)/shard_map/ppermute | solution.py:14
  137.9 3.5 %collective-permute-start.7 = (f32[16,256]{1,0:T(8,128)S(1)}, f32[16,256]{1,0:T(8,128)S(1)}, u32[]{:S(2)}, u32[]{:S(2)}) collective-permute-start(f32[16,256]{1,0:T(8,128)S(1)} %multiply_add_fusion.7), channel_id=1, source_target_pairs={{0,128},{16,144},{32,160},{48,176},{64,192},{80,208},{96,224},{112... | collective-permute-start | bytes 49160 | tf_op jit(solution)/shard_map/ppermute | solution.py:14
  141.4 2.0 collective-permute-start.6
  143.5 9.3 %copy.49 = f32[64,64,256]{1,0,2:T(8,128)} copy(f32[64,64,256]{2,1,0:T(8,128)} %fusion.12) | data formatting | bytes 8388608 | tf_op jit(solution)/shard_map/optimization_barrier | solution.py:105
  152.8 2.5 %collective-permute-start.9 = (f32[16,256]{1,0:T(8,128)S(1)}, f32[16,256]{1,0:T(8,128)S(1)}, u32[]{:S(2)}, u32[]{:S(2)}) collective-permute-start(f32[16,256]{1,0:T(8,128)S(1)} %multiply_add_fusion.6), channel_id=1, source_target_pairs={{0,256},{16,272},{32,288},{48,304},{64,320},{80,336},{96,352},{112... | collective-permute-start | bytes 49160 | tf_op jit(solution)/shard_map/ppermute | solution.py:14
  155.4 10.3 %fusion.28 = f32[256,32,64]{2,1,0:T(8,128)} fusion(bf16[32,64,256]{1,0,2:T(8,128)(2,1)S(1)} %copy-done, f32[64,64,256]{1,0,2:T(8,128)} %copy.49), kind=kOutput, calls=%fused_computation.67 | convolution fusion | flops 402653184 | bytes 7340032 | tf_op jit(solution)/shard_map/ijc,kjc->kic/dot_general | solution.py:81
  165.8 12.5 %add_bitcast_fusion = f32[32,64,256]{1,0,2:T(8,128)} fusion(f32[256,32,64]{2,1,0:T(8,128)} %fusion.28, f32[32,16,256]{0,1,2:T(8,128)} %copy-done.1, f32[64]{0:T(128)S(1)} %broadcast_add_fusion, f32[16,256]{0,1:T(8,128)S(1)} %copy.60, f32[32]{0:T(128)S(1)} %convert_multiply_fusion.1, f32[16,256]{0,1:T(8,128)S(1)} %copy.46, f32[16,256]{0,1:T(8,128)S(1)} %copy.45), kind=kOutput, calls=%fused_computation | convolution fusion | flops 102105088 | bytes 4768128 | tf_op jit(solution)/shard_map/nic,knc->kic/dot_general | solution.py:84
  178.3 4.7 %copy.61 = f32[32,64,256]{2,1,0:T(8,128)} copy(f32[32,64,256]{1,0,2:T(8,128)} %add_bitcast_fusion) | data formatting | bytes 4194304 | tf_op jit(solution)/shard_map/add | solution.py:85
  183.0 1.8 fusion.1
  184.8 0.9 fusion
  185.7 16.7 %all_to_all.53 = bf16[16,128,256]{2,1,0:T(8,128)(2,1)S(1)} all-to-all(bf16[16,128,256]{2,1,0:T(8,128)(2,1)S(1)} %bitcast.75), channel_id=1, replica_groups=mesh['seq'=32,'chan'=16] {'chan'}, dimensions={0} | all-to-all | bytes 2097152 | tf_op jit(solution)/shard_map/all_to_all | solution.py:120
  202.5 1.1 copy.70
  (68 shorter events, 7.9 us)
Async XLA Ops:
  0.0 1.6 slice-start
  5.4 7.7 %copy-start.10 = (f32[16,256]{1,0:T(8,128)S(1)}, f32[16,256]{1,0:T(8,128)}, u32[]{:S(2)}) copy-start(f32[16,256]{1,0:T(8,128)} %param.7) | copy-start | bytes 49156
  5.4 7.7 %copy-start.13 = (f32[16,256]{1,0:T(8,128)S(1)}, f32[16,256]{1,0:T(8,128)}, u32[]{:S(2)}) copy-start(f32[16,256]{1,0:T(8,128)} %param.8) | copy-start | bytes 49156
  5.4 33.0 %all-to-all-start = ((bf16[2,128,4096]{1,0,2:T(2,128)(2,1)}), bf16[2,128,4096]{1,0,2:T(2,128)(2,1)S(1)}, u32[]{:S(2)}, u32[]{:S(2)}) async-start(bf16[2,128,4096]{1,0,2:T(2,128)(2,1)} %copy.68), calls=%async_computation | async-start | bytes 4194304 | tf_op jit(solution)/shard_map/all_to_all | solution.py:97
  17.9 3.8 %copy-start.5 = (bf16[3,128,4096]{2,1,0:T(8,128)(2,1)S(1)}, bf16[3,128,4096]{2,1,0:T(8,128)(2,1)}, u32[]{:S(2)}) copy-start(bf16[3,128,4096]{2,1,0:T(8,128)(2,1)} %param.5) | copy-start | bytes 9437188
  38.4 1.3 copy-start.4
  45.0 16.0 %collective-permute-start = (bf16[2,2,256]{2,1,0:T(2,128)(2,1)}, bf16[2,2,256]{2,1,0:T(2,128)(2,1)}, u32[]{:S(2)}, u32[]{:S(2)}) collective-permute-start(bf16[2,2,256]{2,1,0:T(2,128)(2,1)} %slice.112), channel_id=1, source_target_pairs={{0,16},{16,32},{32,48},{48,64},{64,80},{80,96},{96,112},{112,128},... | collective-permute-start | bytes 6152 | tf_op jit(solution)/shard_map/ppermute | solution.py:14
  64.0 1.0 copy-start.2
  64.0 4.8 %copy-start.17 = (f32[64]{0:T(128)S(1)}, f32[64]{0:T(128)}, u32[]{:S(2)}) copy-start(f32[64]{0:T(128)} %broadcast_subtract_fusion) | copy-start | bytes 772
  81.9 18.7 %all-to-all-start.1 = ((bf16[128,16,256]{2,0,1:T(8,128)(2,1)}), bf16[128,16,256]{2,0,1:T(8,128)(2,1)S(1)}, u32[]{:S(2)}, u32[]{:S(2)}) async-start(bf16[128,16,256]{2,0,1:T(8,128)(2,1)} %bitcast.73), calls=%async_computation.1 | async-start | bytes 2097152 | tf_op jit(solution)/shard_map/all_to_all | solution.py:106
  85.7 3.1 %copy-start.9 = (f32[16,256]{0,1:T(8,128)S(1)}, f32[16,256]{0,1:T(8,128)}, u32[]{:S(2)}) copy-start(f32[16,256]{0,1:T(8,128)} %copy.52) | copy-start | bytes 49156
  88.8 1.3 copy-start.8
  91.4 1.3 copy-start.7
  93.9 1.3 copy-start.1
  95.8 9.2 %copy-start.11 = (f32[16,256]{1,0:T(8,128)S(1)}, f32[16,256]{1,0:T(8,128)}, u32[]{:S(2)}) copy-start(f32[16,256]{1,0:T(8,128)} %param.7) | copy-start | bytes 49156
  95.8 9.2 %copy-start.12 = (f32[1,16,256]{2,1,0:T(8,128)S(1)}, f32[1,16,256]{2,1,0:T(8,128)}, u32[]{:S(2)}) copy-start(f32[1,16,256]{2,1,0:T(8,128)} %copy.58) | copy-start | bytes 49156
  100.6 4.5 %copy-start.6 = (bf16[128,16,256]{2,0,1:T(8,128)(2,1)}, bf16[128,16,256]{2,0,1:T(8,128)(2,1)S(1)}, u32[]{:S(2)}) copy-start(bf16[128,16,256]{2,0,1:T(8,128)(2,1)S(1)} %all-to-all-done.1) | copy-start | bytes 3145732
  100.6 5.1 %collective-permute-start.1 = (bf16[1,2,256]{2,1,0:T(2,128)(2,1)S(1)}, bf16[1,2,256]{2,1,0:T(2,128)(2,1)S(1)}, u32[]{:S(2)}, u32[]{:S(2)}) collective-permute-start(bf16[1,2,256]{2,1,0:T(2,128)(2,1)S(1)} %slice.122), channel_id=1, source_target_pairs={{0,16},{16,32},{32,48},{48,64},{64,80},{80,96},{96,112},{112,128},... | collective-permute-start | bytes 3080 | tf_op jit(solution)/shard_map/ppermute | solution.py:14
  107.2 17.6 %collective-permute-start.5 = (f32[16,256]{1,0:T(8,128)S(1)}, f32[16,256]{1,0:T(8,128)S(1)}, u32[]{:S(2)}, u32[]{:S(2)}) collective-permute-start(f32[16,256]{1,0:T(8,128)S(1)} %bitcast_add_fusion.1), channel_id=1, source_target_pairs={{0,64},{16,80},{32,96},{48,112},{64,128},{80,144},{96,160},{112,17... | collective-permute-start | bytes 49160 | tf_op jit(solution)/shard_map/ppermute | solution.py:14
  111.6 13.1 %collective-permute-start.4 = (f32[16,256]{1,0:T(8,128)S(1)}, f32[16,256]{1,0:T(8,128)S(1)}, u32[]{:S(2)}, u32[]{:S(2)}) collective-permute-start(f32[16,256]{1,0:T(8,128)S(1)} %bitcast_add_fusion.1), channel_id=1, source_target_pairs={{0,48},{16,64},{32,80},{48,96},{64,112},{80,128},{96,144},{112,160... | collective-permute-start | bytes 49160 | tf_op jit(solution)/shard_map/ppermute | solution.py:14
  120.3 4.4 %collective-permute-start.3 = (f32[16,256]{1,0:T(8,128)S(1)}, f32[16,256]{1,0:T(8,128)S(1)}, u32[]{:S(2)}, u32[]{:S(2)}) collective-permute-start(f32[16,256]{1,0:T(8,128)S(1)} %bitcast_add_fusion.1), channel_id=1, source_target_pairs={{0,32},{16,48},{32,64},{48,80},{64,96},{80,112},{96,128},{112,144}... | collective-permute-start | bytes 49160 | tf_op jit(solution)/shard_map/ppermute | solution.py:14
  122.7 3.1 %collective-permute-start.2 = (f32[16,256]{1,0:T(8,128)S(1)}, f32[16,256]{1,0:T(8,128)S(1)}, u32[]{:S(2)}, u32[]{:S(2)}) collective-permute-start(f32[16,256]{1,0:T(8,128)S(1)} %bitcast_add_fusion.1), channel_id=1, source_target_pairs={{0,16},{16,32},{32,48},{48,64},{64,80},{80,96},{96,112},{112,128},... | collective-permute-start | bytes 49160 | tf_op jit(solution)/shard_map/ppermute | solution.py:14
  125.8 27.0 %collective-permute-start.8 = (f32[16,256]{1,0:T(8,128)S(1)}, f32[16,256]{1,0:T(8,128)S(1)}, u32[]{:S(2)}, u32[]{:S(2)}) collective-permute-start(f32[16,256]{1,0:T(8,128)S(1)} %multiply_add_fusion.7), channel_id=1, source_target_pairs={{0,192},{16,208},{32,224},{48,240},{64,256},{80,272},{96,288},{112... | collective-permute-start | bytes 49160 | tf_op jit(solution)/shard_map/ppermute | solution.py:14
  137.9 14.9 %collective-permute-start.7 = (f32[16,256]{1,0:T(8,128)S(1)}, f32[16,256]{1,0:T(8,128)S(1)}, u32[]{:S(2)}, u32[]{:S(2)}) collective-permute-start(f32[16,256]{1,0:T(8,128)S(1)} %multiply_add_fusion.7), channel_id=1, source_target_pairs={{0,128},{16,144},{32,160},{48,176},{64,192},{80,208},{96,224},{112... | collective-permute-start | bytes 49160 | tf_op jit(solution)/shard_map/ppermute | solution.py:14
  141.4 11.4 %collective-permute-start.6 = (f32[16,256]{1,0:T(8,128)S(1)}, f32[16,256]{1,0:T(8,128)S(1)}, u32[]{:S(2)}, u32[]{:S(2)}) collective-permute-start(f32[16,256]{1,0:T(8,128)S(1)} %multiply_add_fusion.7), channel_id=1, source_target_pairs={{0,64},{16,80},{32,96},{48,112},{64,128},{80,144},{96,160},{112,17... | collective-permute-start | bytes 49160 | tf_op jit(solution)/shard_map/ppermute | solution.py:14
  143.5 11.9 %copy-start = (bf16[32,64,256]{1,0,2:T(8,128)(2,1)S(1)}, bf16[32,64,256]{1,0,2:T(8,128)(2,1)}, u32[]{:S(2)}) copy-start(bf16[32,64,256]{1,0,2:T(8,128)(2,1)} %copy.48) | copy-start | bytes 3145732
  152.8 12.8 %collective-permute-start.9 = (f32[16,256]{1,0:T(8,128)S(1)}, f32[16,256]{1,0:T(8,128)S(1)}, u32[]{:S(2)}, u32[]{:S(2)}) collective-permute-start(f32[16,256]{1,0:T(8,128)S(1)} %multiply_add_fusion.6), channel_id=1, source_target_pairs={{0,256},{16,272},{32,288},{48,304},{64,320},{80,336},{96,352},{112... | collective-permute-start | bytes 49160 | tf_op jit(solution)/shard_map/ppermute | solution.py:14
  178.3 4.7 %copy-start.3 = (bf16[2048,256]{1,0:T(8,128)(2,1)S(1)}, bf16[2048,256]{1,0:T(8,128)(2,1)}, u32[]{:S(2)}) copy-start(bf16[2048,256]{1,0:T(8,128)(2,1)} %copy-done.2) | copy-start | bytes 3145732
  178.3 4.7 %copy-start.16 = (f32[256]{0:T(256)S(1)}, f32[256]{0:T(256)}, u32[]{:S(2)}) copy-start(f32[256]{0:T(256)} %param.9) | copy-start | bytes 3076
  182.9 1.9 copy-start.14
  182.9 1.9 copy-start.15

commit v8 on v7

--- a/solution.py
+++ b/solution.py
@@ -78,11 +78,12 @@
                 total = total + weight * from_behind(incoming, "seq", span * multiple)
         incoming = total
         span *= radix
-    inner = jnp.einsum("ijc,kjc->kic", toeplitz, pieces, precision=lax.Precision.HIGHEST)
     block_starts = (jnp.arange(count).astype(jnp.float32) * block)[:, None, None]
     starts = starts + jnp.exp(-decay_rate[None, :, :] * block_starts) * incoming[None, :, :]
-    carried = jnp.einsum("nic,knc->kic", reading, starts, precision=lax.Precision.HIGHEST)
-    longconv = (inner + carried).reshape(signal.shape)
+    operands = jnp.concatenate([pieces, starts], axis=1)
+    longconv = jnp.einsum(
+        "cij,kjc->kic", toeplitz, operands, precision=lax.Precision.HIGHEST
+    ).reshape(signal.shape)
     return (longconv + skip_gain[None, :] * signal).astype(jnp.bfloat16), passenger
 
 
@@ -100,7 +101,10 @@
 
     scaled = residue * jnp.sqrt(1.0 - jnp.exp(-2.0 * decay_rate))
     section = features.shape[1] * lax.axis_size("chan")
-    toeplitz = modal_tables(decay_rate, scaled, math.gcd(section, block_len))[0]
+    toeplitz, unused_ending, reading = modal_tables(decay_rate, scaled, math.gcd(section, block_len))
+    toeplitz = jnp.concatenate(
+        [jnp.transpose(toeplitz, (2, 0, 1)), jnp.transpose(reading, (2, 1, 0))], axis=2
+    )
     keys_values = arrive(features[1:])
     keys_values, queries, toeplitz = lax.optimization_barrier((keys_values, features[0], toeplitz))
     queries = lax.all_to_all(queries, "chan", split_axis=1, concat_axis=0, tiled=True)

time: 206 us -> 214 us (1.039)
  the two profiles are of different devices: /device:TPU:1 before, /device:TPU:32 now
where the time goes in v8:
time: 214 us; the launch traced here: 212 us
  local copies, waits for them, and re-layouts  56.6 us (26%)
  starting transfers between devices  56.3 us (26%)
  waiting for transfers between devices  32.1 us (15%)
  matrix products  26.1 us (12%)
  other arithmetic  22.1 us (10%)
  blocking collectives  18.8 us (9%)
    ppermute x10, starting transfers between devices, from_behind(): return lax.ppermute(block, axis, route)  44.6 us
    all_to_all x1, waiting for transfers between devices, arrive(): lax.all_to_all(streams, 'chan', split_axis=2, concat_axis=1, tiled=True)  21.7 us
    all_to_all x1, blocking collectives, local(): lax.all_to_all(gated, 'chan', split_axis=0, concat_axis=1, tiled=True)  18.8 us
    dot_general x1, matrix products, long_part(): jnp.einsum('cij,kjc->kic', toeplitz, operands, precision=lax.Precision.HI...  18.2 us
    add x5, other arithmetic, long_part(): starts + jnp.exp(-decay_rate * float(block * step)) * shifted(starts, step)  8.07 us
    optimization_barrier x1, local copies, waits for them, and re-layouts, local(): lax.optimization_barrier((keys_values, features[0], toeplitz))  7.93 us
    reshape x2, local copies, waits for them, and re-layouts, long_part(): pieces = signal.reshape(count, block, signal.shape[1])  7.67 us
    all_to_all x1, starting transfers between devices, arrive(): lax.all_to_all(streams, 'chan', split_axis=2, concat_axis=1, tiled=True)  7.17 us
  transfers between devices with their start and end apart: 12, of which 5 were waited for; matrix products, arithmetic and copies ran while one was open for 18% of the time, Pallas kernels for 0%

profile of v8, /device:TPU:32, one launch (start us, length us, event | category | flops | bytes accessed | tf_op | source)
XLA Modules:
  0.0 212.5 jit_solution(7381163029316255104)
XLA Ops:
  0.0 1.6 slice-done
  1.6 3.8 %copy.73 = bf16[2,128,4096]{1,0,2:T(2,128)(2,1)} copy(bf16[2,128,4096]{2,1,0:T(8,128)(2,1)S(1)} %slice-done) | data formatting | bytes 4194304
  5.4 7.2 %all-to-all-start = ((bf16[2,128,4096]{1,0,2:T(2,128)(2,1)}), bf16[2,128,4096]{1,0,2:T(2,128)(2,1)S(1)}, u32[]{:S(2)}, u32[]{:S(2)}) async-start(bf16[2,128,4096]{1,0,2:T(2,128)(2,1)} %copy.73), calls=%async_computation | async-start | bytes 4194304 | tf_op jit(solution)/shard_map/all_to_all | solution.py:98
  13.7 1.6 multiply_reduce_fusion
  15.6 2.9 %fusion.12 = f32[256,64,64]{0,2,1:T(8,128)S(1)} fusion(s32[64,64]{1,0:T(8,128)S(1)} %iota_subtract_fusion, f32[64,256]{0,1:T(8,128)S(1)} %multiply_reduce_fusion), kind=kOutput, calls=%fused_computation.25 | convolution fusion | flops 805568512 | bytes 4276224 | tf_op jit(solution)/shard_map/dot_general | solution.py:36
  18.5 2.9 %pad_maximum_fusion = f32[256,64,80]{0,2,1:T(8,128)} fusion(f32[256,64,16]{0,2,1:T(8,128)S(1)} %exponential_multiply_fusion, f32[256,64,64]{0,2,1:T(8,128)S(1)} %fusion.12), kind=kLoop, calls=%fused_computation | loop fusion | flops 1310720 | bytes 10485760 | tf_op jit(solution)/shard_map/concatenate | solution.py:105
  21.5 1.1 slice_bitcast_fusion
  22.6 21.7 %all-to-all-done = bf16[2,128,4096]{1,0,2:T(2,128)(2,1)S(1)} async-done(((bf16[2,128,4096]{1,0,2:T(2,128)(2,1)}), bf16[2,128,4096]{1,0,2:T(2,128)(2,1)S(1)}, u32[]{:S(2)}, u32[]{:S(2)}) %all-to-all-start) | async-done | bytes 2097184 | tf_op jit(solution)/shard_map/all_to_all | solution.py:98
  44.3 1.3 copy-done.1
  45.6 4.7 %copy.48 = bf16[2,128,16,256]{3,1,2,0:T(8,128)(2,1)S(1)} copy(bf16[2,128,16,256]{1,0,3,2:T(2,128)(2,1)} %bitcast.74) | data formatting | bytes 4194304 | tf_op jit(solution)/shard_map/all_to_all | solution.py:98
  50.4 1.9 collective-permute-start
  55.8 1.4 add_convert_fusion
  57.6 3.8 %copy.52 = bf16[32,64,256]{1,0,2:T(8,128)(2,1)} copy(bf16[32,64,256]{2,1,0:T(8,128)(2,1)S(1)} %bitcast.70) | data formatting | bytes 2097152 | tf_op jit(solution)/shard_map/reshape | solution.py:57
  61.4 5.0 %fusion.13 = f32[32,16,256]{0,1,2:T(8,128)S(1)} fusion(bf16[32,64,256]{1,0,2:T(8,128)(2,1)} %copy.52, f32[64]{0:T(128)} %broadcast_subtract_fusion, f32[16,256]{0,1:T(8,128)S(1)} %copy.50), kind=kOutput, calls=%fused_computation.27 | convolution fusion | flops 100925440 | bytes 1589504 | tf_op jit(solution)/shard_map/njc,kjc->knc/dot_general | solution.py:58
  66.4 1.9 slice.121
  68.3 1.9 pad_slice_fusion
  70.2 3.1 %copy.60 = f32[1,16,256]{2,1,0:T(8,128)} copy(f32[1,16,256]{0,1,2:T(8,128)} %slice.121) | data formatting | bytes 32768 | tf_op jit(solution)/shard_map/slice | solution.py:64
  73.4 2.3 %copy.80 = bf16[16,16,8,256]{3,2,0,1:T(8,128)(2,1)} copy(bf16[16,16,8,256]{3,2,1,0:T(8,128)(2,1)} %bitcast.75) | data formatting | bytes 2097152 | tf_op jit(solution)/shard_map/all_to_all | solution.py:110
  75.6 4.5 %all-to-all-start.1 = ((bf16[128,16,256]{2,0,1:T(8,128)(2,1)}), bf16[128,16,256]{2,0,1:T(8,128)(2,1)}, u32[]{:S(2)}, u32[]{:S(2)}) async-start(bf16[128,16,256]{2,0,1:T(8,128)(2,1)} %bitcast.76), calls=%async_computation.1 | async-start | bytes 2097152 | tf_op jit(solution)/shard_map/all_to_all | solution.py:110
  80.2 3.1 %multiply_add_fusion.5 = f32[32,16,256]{0,1,2:T(8,128)S(1)} fusion(f32[31,16,256]{0,1,2:T(8,128)} %pad_slice_fusion, f32[31,16,256]{0,1,2:T(8,128)S(1)} %bitcast.65, f32[16,256]{0,1:T(8,128)} %copy.53), kind=kLoop, calls=%fused_computation.18 | loop fusion | flops 262144 | bytes 1556480 | tf_op jit(solution)/shard_map/add | solution.py:62
  83.3 1.3 multiply_add_fusion.4
  84.5 1.3 multiply_add_fusion.3
  85.8 1.3 multiply_add_fusion.2
  87.1 1.3 multiply_add_fusion.1
  88.3 1.9 slice.120
  90.3 2.5 %copy.59 = f32[1,16,256]{2,1,0:T(8,128)S(1)} copy(f32[1,16,256]{0,1,2:T(8,128)} %slice.120) | data formatting | bytes 32768 | tf_op jit(solution)/shard_map/slice | solution.py:64
  92.8 5.0 %all-to-all-done.1 = bf16[128,16,256]{2,0,1:T(8,128)(2,1)} async-done(((bf16[128,16,256]{2,0,1:T(8,128)(2,1)}), bf16[128,16,256]{2,0,1:T(8,128)(2,1)}, u32[]{:S(2)}, u32[]{:S(2)}) %all-to-all-start.1) | async-done | bytes 1048608 | tf_op jit(solution)/shard_map/all_to_all | solution.py:110
  98.4 3.0 %collective-permute-start.1 = (bf16[1,2,256]{2,1,0:T(2,128)(2,1)S(1)}, bf16[1,2,256]{2,1,0:T(2,128)(2,1)S(1)}, u32[]{:S(2)}, u32[]{:S(2)}) collective-permute-start(bf16[1,2,256]{2,1,0:T(2,128)(2,1)S(1)} %slice.122), channel_id=1, source_target_pairs={{0,16},{16,32},{32,48},{48,64},{64,80},{80,96},{96,112},{112,128},... | collective-permute-start | bytes 3080 | tf_op jit(solution)/shard_map/ppermute | solution.py:14
  101.5 1.8 collective-permute-done.1
  103.3 2.5 %pad_maximum_fusion.2 = bf16[1,2050,256]{2,1,0:T(8,128)(2,1)} fusion(bf16[1,2048,256]{2,1,0:T(8,128)(2,1)} %bitcast.15, bf16[1,2,256]{2,1,0:T(2,128)(2,1)S(1)} %collective-permute-done.1), kind=kLoop, calls=%fused_computation.28 | loop fusion | flops 2099200 | bytes 2099200 | tf_op jit(solution)/shard_map/concatenate | solution.py:113
  105.8 4.3 %collective-permute-start.5 = (f32[16,256]{1,0:T(8,128)S(1)}, f32[16,256]{1,0:T(8,128)S(1)}, u32[]{:S(2)}, u32[]{:S(2)}) collective-permute-start(f32[16,256]{1,0:T(8,128)S(1)} %bitcast_add_fusion.1), channel_id=1, source_target_pairs={{0,64},{16,80},{32,96},{48,112},{64,128},{80,144},{96,160},{112,17... | collective-permute-start | bytes 49160 | tf_op jit(solution)/shard_map/ppermute | solution.py:14
  110.1 7.9 %collective-permute-start.4 = (f32[16,256]{1,0:T(8,128)S(1)}, f32[16,256]{1,0:T(8,128)S(1)}, u32[]{:S(2)}, u32[]{:S(2)}) collective-permute-start(f32[16,256]{1,0:T(8,128)S(1)} %bitcast_add_fusion.1), channel_id=1, source_target_pairs={{0,48},{16,64},{32,80},{48,96},{64,112},{80,128},{96,144},{112,160... | collective-permute-start | bytes 49160 | tf_op jit(solution)/shard_map/ppermute | solution.py:14
  117.9 5.6 %collective-permute-start.3 = (f32[16,256]{1,0:T(8,128)S(1)}, f32[16,256]{1,0:T(8,128)S(1)}, u32[]{:S(2)}, u32[]{:S(2)}) collective-permute-start(f32[16,256]{1,0:T(8,128)S(1)} %bitcast_add_fusion.1), channel_id=1, source_target_pairs={{0,32},{16,48},{32,64},{48,80},{64,96},{80,112},{96,128},{112,144}... | collective-permute-start | bytes 49160 | tf_op jit(solution)/shard_map/ppermute | solution.py:14
  123.6 1.9 collective-permute-start.2
  125.6 3.1 %collective-permute-done.2 = f32[16,256]{1,0:T(8,128)S(1)} collective-permute-done((f32[16,256]{1,0:T(8,128)S(1)}, f32[16,256]{1,0:T(8,128)S(1)}, u32[]{:S(2)}, u32[]{:S(2)}) %collective-permute-start.2) | collective-permute-done | bytes 16416 | tf_op jit(solution)/shard_map/ppermute | solution.py:14
  128.7 7.8 %collective-permute-start.8 = (f32[16,256]{1,0:T(8,128)S(1)}, f32[16,256]{1,0:T(8,128)S(1)}, u32[]{:S(2)}, u32[]{:S(2)}) collective-permute-start(f32[16,256]{1,0:T(8,128)S(1)} %multiply_add_fusion.8), channel_id=1, source_target_pairs={{0,192},{16,208},{32,224},{48,240},{64,256},{80,272},{96,288},{112... | collective-permute-start | bytes 49160 | tf_op jit(solution)/shard_map/ppermute | solution.py:14
  136.4 4.1 %collective-permute-start.7 = (f32[16,256]{1,0:T(8,128)S(1)}, f32[16,256]{1,0:T(8,128)S(1)}, u32[]{:S(2)}, u32[]{:S(2)}) collective-permute-start(f32[16,256]{1,0:T(8,128)S(1)} %multiply_add_fusion.8), channel_id=1, source_target_pairs={{0,128},{16,144},{32,160},{48,176},{64,192},{80,208},{96,224},{112... | collective-permute-start | bytes 49160 | tf_op jit(solution)/shard_map/ppermute | solution.py:14
  140.6 1.4 collective-permute-start.6
  143.4 6.7 %collective-permute-start.9 = (f32[16,256]{1,0:T(8,128)S(1)}, f32[16,256]{1,0:T(8,128)S(1)}, u32[]{:S(2)}, u32[]{:S(2)}) collective-permute-start(f32[16,256]{1,0:T(8,128)S(1)} %multiply_add_fusion.7), channel_id=1, source_target_pairs={{0,256},{16,272},{32,288},{48,304},{64,320},{80,336},{96,352},{112... | collective-permute-start | bytes 49160 | tf_op jit(solution)/shard_map/ppermute | solution.py:14
  150.1 3.9 %copy.63 = f32[32,64,256]{1,0,2:T(8,128)} copy(bf16[32,64,256]{2,1,0:T(8,128)(2,1)S(1)} %bitcast.71) | data formatting | bytes 3145728 | tf_op jit(solution)/shard_map/reshape | solution.py:57
  154.0 7.9 %copy.65 = f32[256,64,80]{2,1,0:T(8,128)} copy(f32[256,64,80]{0,2,1:T(8,128)} %pad_maximum_fusion) | data formatting | bytes 10485760 | tf_op jit(solution)/shard_map/optimization_barrier | solution.py:109
  162.0 2.8 %multiply_add_fusion = f32[32,16,256]{0,1,2:T(8,128)} fusion(f32[32,16,256]{0,1,2:T(8,128)S(1)} %multiply_add_fusion.1, f32[16,256]{0,1:T(8,128)S(1)} %copy.62, f32[32]{0:T(128)S(1)} %convert_multiply_fusion.1, f32[16,256]{0,1:T(8,128)S(1)} %copy.50), kind=kLoop, calls=%fused_computation.13 | loop fusion | flops 393216 | bytes 1081472 | tf_op jit(solution)/shard_map/add | solution.py:82
  164.8 3.8 %copy.64 = f32[32,16,256]{1,0,2:T(8,128)} copy(f32[32,16,256]{0,1,2:T(8,128)} %multiply_add_fusion) | data formatting | bytes 1048576 | tf_op jit(solution)/shard_map/add | solution.py:82
  168.7 18.2 %fusion.4 = f32[32,64,256]{1,0,2:T(8,128)} fusion(f32[256,64,80]{2,1,0:T(8,128)} %copy.65, f32[32,16,256]{1,0,2:T(8,128)} %copy.64, f32[32,64,256]{1,0,2:T(8,128)} %copy.63), kind=kOutput, calls=%fused_computation.6 | convolution fusion | flops 503971840 | bytes 9961472 | tf_op jit(solution)/shard_map/cij,kjc->kic/dot_general | solution.py:84
  186.9 3.6 %copy.66 = f32[32,64,256]{2,1,0:T(8,128)S(1)} copy(f32[32,64,256]{1,0,2:T(8,128)} %fusion.4) | data formatting | bytes 4194304 | tf_op jit(solution)/shard_map/cij,kjc->kic/transpose | solution.py:84
  190.7 1.0 copy-done
  192.6 18.8 %all_to_all.53 = bf16[16,128,256]{2,1,0:T(8,128)(2,1)S(1)} all-to-all(bf16[16,128,256]{2,1,0:T(8,128)(2,1)S(1)} %bitcast.78), channel_id=1, replica_groups=mesh['seq'=32,'chan'=16] {'chan'}, dimensions={0} | all-to-all | bytes 2097152 | tf_op jit(solution)/shard_map/all_to_all | solution.py:124
  211.4 1.1 copy.75
  (54 shorter events, 8.8 us)
Async XLA Ops:
  0.0 1.6 slice-start
  5.4 7.2 %copy-start.5 = (f32[16,256]{1,0:T(8,128)S(1)}, f32[16,256]{1,0:T(8,128)}, u32[]{:S(2)}) copy-start(f32[16,256]{1,0:T(8,128)} %param.7) | copy-start | bytes 49156
  5.4 7.2 %copy-start.7 = (f32[16,256]{1,0:T(8,128)S(1)}, f32[16,256]{1,0:T(8,128)}, u32[]{:S(2)}) copy-start(f32[16,256]{1,0:T(8,128)} %param.8) | copy-start | bytes 49156
  5.4 38.9 %all-to-all-start = ((bf16[2,128,4096]{1,0,2:T(2,128)(2,1)}), bf16[2,128,4096]{1,0,2:T(2,128)(2,1)S(1)}, u32[]{:S(2)}, u32[]{:S(2)}) async-start(bf16[2,128,4096]{1,0,2:T(2,128)(2,1)} %copy.73), calls=%async_computation | async-start | bytes 4194304 | tf_op jit(solution)/shard_map/all_to_all | solution.py:98
  18.5 3.0 %copy-start.2 = (bf16[3,128,4096]{2,1,0:T(8,128)(2,1)S(1)}, bf16[3,128,4096]{2,1,0:T(8,128)(2,1)}, u32[]{:S(2)}) copy-start(bf16[3,128,4096]{2,1,0:T(8,128)(2,1)} %param.5) | copy-start | bytes 9437188
  44.3 1.3 copy-start.1
  50.4 4.9 %collective-permute-start = (bf16[2,2,256]{2,1,0:T(2,128)(2,1)S(1)}, bf16[2,2,256]{2,1,0:T(2,128)(2,1)S(1)}, u32[]{:S(2)}, u32[]{:S(2)}) collective-permute-start(bf16[2,2,256]{2,1,0:T(2,128)(2,1)S(1)} %slice.112), channel_id=1, source_target_pairs={{0,16},{16,32},{32,48},{48,64},{64,80},{80,96},{96,112},{112,128},... | collective-permute-start | bytes 6152 | tf_op jit(solution)/shard_map/ppermute | solution.py:14
  75.6 22.1 %all-to-all-start.1 = ((bf16[128,16,256]{2,0,1:T(8,128)(2,1)}), bf16[128,16,256]{2,0,1:T(8,128)(2,1)}, u32[]{:S(2)}, u32[]{:S(2)}) async-start(bf16[128,16,256]{2,0,1:T(8,128)(2,1)} %bitcast.76), calls=%async_computation.1 | async-start | bytes 2097152 | tf_op jit(solution)/shard_map/all_to_all | solution.py:110
  80.2 3.1 %copy-start.4 = (f32[16,256]{0,1:T(8,128)S(1)}, f32[16,256]{0,1:T(8,128)}, u32[]{:S(2)}) copy-start(f32[16,256]{0,1:T(8,128)} %copy.54) | copy-start | bytes 49156
  83.3 1.3 copy-start.3
  90.3 11.2 %copy-start.6 = (f32[1,16,256]{2,1,0:T(8,128)S(1)}, f32[1,16,256]{2,1,0:T(8,128)}, u32[]{:S(2)}) copy-start(f32[1,16,256]{2,1,0:T(8,128)} %copy.60) | copy-start | bytes 49156
  98.4 4.9 %collective-permute-start.1 = (bf16[1,2,256]{2,1,0:T(2,128)(2,1)S(1)}, bf16[1,2,256]{2,1,0:T(2,128)(2,1)S(1)}, u32[]{:S(2)}, u32[]{:S(2)}) collective-permute-start(bf16[1,2,256]{2,1,0:T(2,128)(2,1)S(1)} %slice.122), channel_id=1, source_target_pairs={{0,16},{16,32},{32,48},{48,64},{64,80},{80,96},{96,112},{112,128},... | collective-permute-start | bytes 3080 | tf_op jit(solution)/shard_map/ppermute | solution.py:14
  105.8 19.8 %collective-permute-start.5 = (f32[16,256]{1,0:T(8,128)S(1)}, f32[16,256]{1,0:T(8,128)S(1)}, u32[]{:S(2)}, u32[]{:S(2)}) collective-permute-start(f32[16,256]{1,0:T(8,128)S(1)} %bitcast_add_fusion.1), channel_id=1, source_target_pairs={{0,64},{16,80},{32,96},{48,112},{64,128},{80,144},{96,160},{112,17... | collective-permute-start | bytes 49160 | tf_op jit(solution)/shard_map/ppermute | solution.py:14
  110.1 15.5 %collective-permute-start.4 = (f32[16,256]{1,0:T(8,128)S(1)}, f32[16,256]{1,0:T(8,128)S(1)}, u32[]{:S(2)}, u32[]{:S(2)}) collective-permute-start(f32[16,256]{1,0:T(8,128)S(1)} %bitcast_add_fusion.1), channel_id=1, source_target_pairs={{0,48},{16,64},{32,80},{48,96},{64,112},{80,128},{96,144},{112,160... | collective-permute-start | bytes 49160 | tf_op jit(solution)/shard_map/ppermute | solution.py:14
  117.9 7.6 %collective-permute-start.3 = (f32[16,256]{1,0:T(8,128)S(1)}, f32[16,256]{1,0:T(8,128)S(1)}, u32[]{:S(2)}, u32[]{:S(2)}) collective-permute-start(f32[16,256]{1,0:T(8,128)S(1)} %bitcast_add_fusion.1), channel_id=1, source_target_pairs={{0,32},{16,48},{32,64},{48,80},{64,96},{80,112},{96,128},{112,144}... | collective-permute-start | bytes 49160 | tf_op jit(solution)/shard_map/ppermute | solution.py:14
  123.6 5.1 %collective-permute-start.2 = (f32[16,256]{1,0:T(8,128)S(1)}, f32[16,256]{1,0:T(8,128)S(1)}, u32[]{:S(2)}, u32[]{:S(2)}) collective-permute-start(f32[16,256]{1,0:T(8,128)S(1)} %bitcast_add_fusion.1), channel_id=1, source_target_pairs={{0,16},{16,32},{32,48},{48,64},{64,80},{80,96},{96,112},{112,128},... | collective-permute-start | bytes 49160 | tf_op jit(solution)/shard_map/ppermute | solution.py:14
  128.7 14.2 %collective-permute-start.8 = (f32[16,256]{1,0:T(8,128)S(1)}, f32[16,256]{1,0:T(8,128)S(1)}, u32[]{:S(2)}, u32[]{:S(2)}) collective-permute-start(f32[16,256]{1,0:T(8,128)S(1)} %multiply_add_fusion.8), channel_id=1, source_target_pairs={{0,192},{16,208},{32,224},{48,240},{64,256},{80,272},{96,288},{112... | collective-permute-start | bytes 49160 | tf_op jit(solution)/shard_map/ppermute | solution.py:14
  136.4 6.4 %collective-permute-start.7 = (f32[16,256]{1,0:T(8,128)S(1)}, f32[16,256]{1,0:T(8,128)S(1)}, u32[]{:S(2)}, u32[]{:S(2)}) collective-permute-start(f32[16,256]{1,0:T(8,128)S(1)} %multiply_add_fusion.8), channel_id=1, source_target_pairs={{0,128},{16,144},{32,160},{48,176},{64,192},{80,208},{96,224},{112... | collective-permute-start | bytes 49160 | tf_op jit(solution)/shard_map/ppermute | solution.py:14
  140.6 2.8 %collective-permute-start.6 = (f32[16,256]{1,0:T(8,128)S(1)}, f32[16,256]{1,0:T(8,128)S(1)}, u32[]{:S(2)}, u32[]{:S(2)}) collective-permute-start(f32[16,256]{1,0:T(8,128)S(1)} %multiply_add_fusion.8), channel_id=1, source_target_pairs={{0,64},{16,80},{32,96},{48,112},{64,128},{80,144},{96,160},{112,17... | collective-permute-start | bytes 49160 | tf_op jit(solution)/shard_map/ppermute | solution.py:14
  143.4 18.5 %collective-permute-start.9 = (f32[16,256]{1,0:T(8,128)S(1)}, f32[16,256]{1,0:T(8,128)S(1)}, u32[]{:S(2)}, u32[]{:S(2)}) collective-permute-start(f32[16,256]{1,0:T(8,128)S(1)} %multiply_add_fusion.7), channel_id=1, source_target_pairs={{0,256},{16,272},{32,288},{48,304},{64,320},{80,336},{96,352},{112... | collective-permute-start | bytes 49160 | tf_op jit(solution)/shard_map/ppermute | solution.py:14
  186.9 3.6 %copy-start.8 = (f32[256]{0:T(256)S(1)}, f32[256]{0:T(256)}, u32[]{:S(2)}) copy-start(f32[256]{0:T(256)} %param.9) | copy-start | bytes 3076
  190.4 1.2 copy-start

commit v9 on v7

--- a/solution.py
+++ b/solution.py
@@ -5,7 +5,7 @@
 from jax import lax
 from jax.sharding import PartitionSpec as P
 
-block_len = 64
+block_len = 32
 
 
 def from_behind(block, axis, distance):

time: 206 us -> 198 us (0.961)
  matrix products: 31.6 us -> 23.9 us
    dot_general x1, matrix products: 10.3 us -> 6.32 us  [long_part(): jnp.einsum('ijc,kjc->kic', toeplitz, pieces, precision=lax.Precision.HIGH...]
    optimization_barrier x1, local copies, waits for them, and re-layouts: 9.32 us -> 5.52 us  [local(): lax.optimization_barrier((keys_values, features[0], toeplitz))]
    all_to_all x1, waiting for transfers between devices: 16.5 us -> 18.9 us  [arrive(): lax.all_to_all(streams, 'chan', split_axis=2, concat_axis=1, tiled=True)]
    dot_general x1, matrix products: 3.83 us -> 1.59 us  [modal_tables(): jnp.dot(one_hot.reshape(block * block, block), kernel, precision=lax.Prec...]
    add x5 -> x6, other arithmetic: 8.07 us -> 9.32 us  [long_part(): starts + jnp.exp(-decay_rate * float(block * step)) * shifted(starts, step)]
    exp x5 -> x6, local copies, waits for them, and re-layouts: 4.54 us -> 5.34 us  [long_part(): jnp.exp(-decay_rate * float(block * step)) * shifted(starts, step)]
    all_to_all x1 -> x2, local copies, waits for them, and re-layouts: 4.72 us -> 4.48 us  [arrive(): lax.all_to_all(streams, 'chan', split_axis=2, concat_axis=1, tiled=True)]
    unnamed x39 -> x34, local copies, waits for them, and re-layouts: 7.43 us -> 7.43 us
  transfers between devices with their start and end apart: 12 -> 12, of which waited for: 4 -> 4; matrix products, arithmetic and copies ran while one was open for 21% -> 19% of each run, Pallas kernels for 0% -> 0%
where the time goes in v9:
time: 198 us; the launch traced here: 194 us
  starting transfers between devices  64.6 us (33%)
  local copies, waits for them, and re-layouts  48.4 us (24%)
  matrix products  23.9 us (12%)
  waiting for transfers between devices  22.9 us (12%)
  other arithmetic  18.2 us (9%)
  blocking collectives  15.9 us (8%)
    ppermute x10, starting transfers between devices, from_behind(): return lax.ppermute(block, axis, route)  53 us
    all_to_all x1, waiting for transfers between devices, arrive(): lax.all_to_all(streams, 'chan', split_axis=2, concat_axis=1, tiled=True)  18.9 us
    all_to_all x1, blocking collectives, local(): lax.all_to_all(gated, 'chan', split_axis=0, concat_axis=1, tiled=True)  15.9 us
    dot_general x1, matrix products, long_part(): jnp.einsum('nic,knc->kic', reading, starts, precision=lax.Precision.HIGHEST)  12.5 us
    add x6, other arithmetic, long_part(): starts + jnp.exp(-decay_rate * float(block * step)) * shifted(starts, step)  9.32 us
    all_to_all x1, starting transfers between devices, arrive(): lax.all_to_all(streams, 'chan', split_axis=2, concat_axis=1, tiled=True)  7.7 us
    unnamed x34, local copies, waits for them, and re-layouts  7.43 us
    dot_general x1, matrix products, long_part(): jnp.einsum('ijc,kjc->kic', toeplitz, pieces, precision=lax.Precision.HIGH...  6.32 us
  transfers between devices with their start and end apart: 12, of which 4 were waited for; matrix products, arithmetic and copies ran while one was open for 19% of the time, Pallas kernels for 0%

profile of v9, /device:TPU:1, one launch (start us, length us, event | category | flops | bytes accessed | tf_op | source)
XLA Modules:
  0.0 194.3 jit_solution(9639320503622799961)
XLA Ops:
  0.0 1.6 slice-done
  1.6 3.8 %copy.70 = bf16[2,128,4096]{1,0,2:T(2,128)(2,1)} copy(bf16[2,128,4096]{2,1,0:T(8,128)(2,1)S(1)} %slice-done) | data formatting | bytes 4194304
  5.4 7.7 %all-to-all-start = ((bf16[2,128,4096]{1,0,2:T(2,128)(2,1)}), bf16[2,128,4096]{1,0,2:T(2,128)(2,1)S(1)}, u32[]{:S(2)}, u32[]{:S(2)}) async-start(bf16[2,128,4096]{1,0,2:T(2,128)(2,1)} %copy.70), calls=%async_computation | async-start | bytes 4194304 | tf_op jit(solution)/shard_map/all_to_all | solution.py:97
  13.9 1.5 constant_dynamic-slice_fusion.2
  16.3 1.6 multiply_reduce_fusion
  17.9 1.6 fusion.25
  19.5 18.9 %all-to-all-done = bf16[2,128,4096]{1,0,2:T(2,128)(2,1)S(1)} async-done(((bf16[2,128,4096]{1,0,2:T(2,128)(2,1)}), bf16[2,128,4096]{1,0,2:T(2,128)(2,1)S(1)}, u32[]{:S(2)}, u32[]{:S(2)}) %all-to-all-start) | async-done | bytes 2097184 | tf_op jit(solution)/shard_map/all_to_all | solution.py:97
  38.4 1.6 copy.42
  40.0 2.9 %copy.43 = bf16[2,16,128,256]{3,2,1,0:T(8,128)(2,1)S(1)} copy(bf16[2,16,128,256]{2,3,1,0:T(8,128)(2,1)} %bitcast.65) | data formatting | bytes 4194304 | tf_op jit(solution)/shard_map/all_to_all | solution.py:97
  43.4 10.9 %collective-permute-start = (bf16[2,2,256]{2,1,0:T(2,128)(2,1)}, bf16[2,2,256]{2,1,0:T(2,128)(2,1)}, u32[]{:S(2)}, u32[]{:S(2)}) collective-permute-start(bf16[2,2,256]{2,1,0:T(2,128)(2,1)} %slice.116), channel_id=1, source_target_pairs={{0,16},{16,32},{32,48},{48,64},{64,80},{80,96},{96,112},{112,128},... | collective-permute-start | bytes 6152 | tf_op jit(solution)/shard_map/ppermute | solution.py:14
  54.9 1.3 copy.71
  60.0 1.5 copy.56
  61.5 1.2 pad_maximum_fusion
  62.8 1.4 add_convert_fusion
  64.5 1.0 copy-done.2
  65.5 4.4 %copy.48 = bf16[64,32,256]{0,1,2:T(8,128)(2,1)} copy(bf16[64,32,256]{2,1,0:T(8,128)(2,1)S(1)} %bitcast.62) | data formatting | bytes 2097152 | tf_op jit(solution)/shard_map/reshape | solution.py:57
  69.9 3.5 %fusion.12 = f32[64,16,256]{0,1,2:T(8,128)S(1)} fusion(bf16[64,32,256]{0,1,2:T(8,128)(2,1)} %copy.48, f32[32]{0:T(128)S(1)} %copy-done.14, f32[16,256]{0,1:T(8,128)S(1)} %copy.46), kind=kOutput, calls=%fused_computation.27 | convolution fusion | flops 100794368 | bytes 2113664 | tf_op jit(solution)/shard_map/njc,kjc->knc/dot_general | solution.py:58
  73.4 1.9 slice.126
  75.3 2.0 %pad_slice_fusion = f32[63,16,256]{0,1,2:T(8,128)} fusion(f32[63,16,256]{0,1,2:T(8,128)S(1)} %bitcast.55), kind=kLoop, calls=%fused_computation.26 | loop fusion | bytes 2064384 | tf_op jit(solution)/shard_map/slice | solution.py:48
  77.3 3.1 %copy.59 = f32[1,16,256]{2,1,0:T(8,128)} copy(f32[1,16,256]{0,1,2:T(8,128)} %slice.126) | data formatting | bytes 32768 | tf_op jit(solution)/shard_map/slice | solution.py:64
  80.4 3.8 %all-to-all-start.1 = ((bf16[128,16,256]{0,2,1:T(8,128)(2,1)}), bf16[128,16,256]{0,2,1:T(8,128)(2,1)S(1)}, u32[]{:S(2)}, u32[]{:S(2)}) async-start(bf16[128,16,256]{0,2,1:T(8,128)(2,1)} %bitcast.11), calls=%async_computation.1 | async-start | bytes 2097152 | tf_op jit(solution)/shard_map/all_to_all | solution.py:106
  84.3 3.1 %multiply_add_fusion.5 = f32[64,16,256]{0,1,2:T(8,128)S(1)} fusion(f32[63,16,256]{0,1,2:T(8,128)} %pad_slice_fusion, f32[63,16,256]{0,1,2:T(8,128)S(1)} %bitcast.56, f32[16,256]{0,1:T(8,128)} %copy.51), kind=kLoop, calls=%fused_computation.20 | loop fusion | flops 524288 | bytes 3129344 | tf_op jit(solution)/shard_map/add | solution.py:62
  87.3 1.3 multiply_add_fusion.4
  88.6 1.3 multiply_add_fusion.3
  89.9 1.3 multiply_add_fusion.2
  91.2 1.3 multiply_add_fusion.1
  92.4 1.3 multiply_add_fusion
  93.7 1.4 copy-done.1
  95.7 1.0 copy.58
  96.7 2.4 %all-to-all-done.1 = bf16[128,16,256]{0,2,1:T(8,128)(2,1)S(1)} async-done(((bf16[128,16,256]{0,2,1:T(8,128)(2,1)}), bf16[128,16,256]{0,2,1:T(8,128)(2,1)S(1)}, u32[]{:S(2)}, u32[]{:S(2)}) %all-to-all-start.1) | async-done | bytes 1048608 | tf_op jit(solution)/shard_map/all_to_all | solution.py:106
  99.6 4.4 %collective-permute-start.1 = (bf16[1,2,256]{2,1,0:T(2,128)(2,1)S(1)}, bf16[1,2,256]{2,1,0:T(2,128)(2,1)S(1)}, u32[]{:S(2)}, u32[]{:S(2)}) collective-permute-start(bf16[1,2,256]{2,1,0:T(2,128)(2,1)S(1)} %slice.127), channel_id=1, source_target_pairs={{0,16},{16,32},{32,48},{48,64},{64,80},{80,96},{96,112},{112,128},... | collective-permute-start | bytes 3080 | tf_op jit(solution)/shard_map/ppermute | solution.py:14
  105.0 4.4 %collective-permute-start.5 = (f32[16,256]{1,0:T(8,128)S(1)}, f32[16,256]{1,0:T(8,128)S(1)}, u32[]{:S(2)}, u32[]{:S(2)}) collective-permute-start(f32[16,256]{1,0:T(8,128)S(1)} %bitcast_add_fusion.1), channel_id=1, source_target_pairs={{0,64},{16,80},{32,96},{48,112},{64,128},{80,144},{96,160},{112,17... | collective-permute-start | bytes 49160 | tf_op jit(solution)/shard_map/ppermute | solution.py:14
  109.5 8.7 %collective-permute-start.4 = (f32[16,256]{1,0:T(8,128)S(1)}, f32[16,256]{1,0:T(8,128)S(1)}, u32[]{:S(2)}, u32[]{:S(2)}) collective-permute-start(f32[16,256]{1,0:T(8,128)S(1)} %bitcast_add_fusion.1), channel_id=1, source_target_pairs={{0,48},{16,64},{32,80},{48,96},{64,112},{80,128},{96,144},{112,160... | collective-permute-start | bytes 49160 | tf_op jit(solution)/shard_map/ppermute | solution.py:14
  118.2 2.3 %collective-permute-start.3 = (f32[16,256]{1,0:T(8,128)S(1)}, f32[16,256]{1,0:T(8,128)S(1)}, u32[]{:S(2)}, u32[]{:S(2)}) collective-permute-start(f32[16,256]{1,0:T(8,128)S(1)} %bitcast_add_fusion.1), channel_id=1, source_target_pairs={{0,32},{16,48},{32,64},{48,80},{64,96},{80,112},{96,128},{112,144}... | collective-permute-start | bytes 49160 | tf_op jit(solution)/shard_map/ppermute | solution.py:14
  120.5 2.1 %collective-permute-start.2 = (f32[16,256]{1,0:T(8,128)S(1)}, f32[16,256]{1,0:T(8,128)S(1)}, u32[]{:S(2)}, u32[]{:S(2)}) collective-permute-start(f32[16,256]{1,0:T(8,128)S(1)} %bitcast_add_fusion.1), channel_id=1, source_target_pairs={{0,16},{16,32},{32,48},{48,64},{64,80},{80,96},{96,112},{112,128},... | collective-permute-start | bytes 49160 | tf_op jit(solution)/shard_map/ppermute | solution.py:14
  122.6 1.0 collective-permute-done.2
  123.6 12.1 %collective-permute-start.8 = (f32[16,256]{1,0:T(8,128)S(1)}, f32[16,256]{1,0:T(8,128)S(1)}, u32[]{:S(2)}, u32[]{:S(2)}) collective-permute-start(f32[16,256]{1,0:T(8,128)S(1)} %multiply_add_fusion.8), channel_id=1, source_target_pairs={{0,192},{16,208},{32,224},{48,240},{64,256},{80,272},{96,288},{112... | collective-permute-start | bytes 49160 | tf_op jit(solution)/shard_map/ppermute | solution.py:14
  135.7 3.5 %collective-permute-start.7 = (f32[16,256]{1,0:T(8,128)S(1)}, f32[16,256]{1,0:T(8,128)S(1)}, u32[]{:S(2)}, u32[]{:S(2)}) collective-permute-start(f32[16,256]{1,0:T(8,128)S(1)} %multiply_add_fusion.8), channel_id=1, source_target_pairs={{0,128},{16,144},{32,160},{48,176},{64,192},{80,208},{96,224},{112... | collective-permute-start | bytes 49160 | tf_op jit(solution)/shard_map/ppermute | solution.py:14
  139.2 2.0 %collective-permute-start.6 = (f32[16,256]{1,0:T(8,128)S(1)}, f32[16,256]{1,0:T(8,128)S(1)}, u32[]{:S(2)}, u32[]{:S(2)}) collective-permute-start(f32[16,256]{1,0:T(8,128)S(1)} %multiply_add_fusion.8), channel_id=1, source_target_pairs={{0,64},{16,80},{32,96},{48,112},{64,128},{80,144},{96,160},{112,17... | collective-permute-start | bytes 49160 | tf_op jit(solution)/shard_map/ppermute | solution.py:14
  141.3 5.5 %copy.49 = f32[32,32,256]{1,0,2:T(8,128)} copy(f32[32,32,256]{2,1,0:T(8,128)} %fusion.25) | data formatting | bytes 2097152 | tf_op jit(solution)/shard_map/optimization_barrier | solution.py:105
  146.9 2.6 %collective-permute-start.9 = (f32[16,256]{1,0:T(8,128)S(1)}, f32[16,256]{1,0:T(8,128)S(1)}, u32[]{:S(2)}, u32[]{:S(2)}) collective-permute-start(f32[16,256]{1,0:T(8,128)S(1)} %multiply_add_fusion.7), channel_id=1, source_target_pairs={{0,256},{16,272},{32,288},{48,304},{64,320},{80,336},{96,352},{112... | collective-permute-start | bytes 49160 | tf_op jit(solution)/shard_map/ppermute | solution.py:14
  149.5 6.3 %fusion.28 = f32[256,64,32]{1,2,0:T(8,128)} fusion(bf16[64,32,256]{0,1,2:T(8,128)(2,1)S(1)} %copy-done, f32[32,32,256]{1,0,2:T(8,128)} %copy.49), kind=kOutput, calls=%fused_computation.67 | convolution fusion | flops 201326592 | bytes 4194304 | tf_op jit(solution)/shard_map/ijc,kjc->kic/dot_general | solution.py:81
  155.9 12.5 %add_bitcast_fusion = f32[64,32,256]{0,1,2:T(8,128)} fusion(f32[256,64,32]{1,2,0:T(8,128)} %fusion.28, f32[64,16,256]{0,1,2:T(8,128)} %copy-done.1, f32[32]{0:T(128)S(1)} %broadcast_add_fusion, f32[16,256]{0,1:T(8,128)S(1)} %copy.61, f32[64]{0:T(128)S(1)} %convert_multiply_fusion.1, f32[16,256]{0,1:T(8,128)S(1)} %copy.46, f32[16,256]{0,1:T(8,128)S(1)} %copy.45), kind=kOutput, calls=%fused_computation | convolution fusion | flops 102236160 | bytes 5292416 | tf_op jit(solution)/shard_map/nic,knc->kic/dot_general | solution.py:84
  168.4 5.3 %copy.62 = f32[64,32,256]{2,1,0:T(8,128)} copy(f32[64,32,256]{0,1,2:T(8,128)} %add_bitcast_fusion) | data formatting | bytes 4194304 | tf_op jit(solution)/shard_map/add | solution.py:85
  173.6 1.8 fusion.1
  175.5 0.9 fusion
  176.4 15.9 %all_to_all.53 = bf16[16,128,256]{2,1,0:T(8,128)(2,1)S(1)} all-to-all(bf16[16,128,256]{2,1,0:T(8,128)(2,1)S(1)} %bitcast.71), channel_id=1, replica_groups=mesh['seq'=32,'chan'=16] {'chan'}, dimensions={0} | all-to-all | bytes 2097152 | tf_op jit(solution)/shard_map/all_to_all | solution.py:120
  193.0 1.3 copy.64
  (68 shorter events, 10.0 us)
Async XLA Ops:
  0.0 1.6 slice-start
  5.4 7.7 %copy-start.8 = (f32[16,256]{1,0:T(8,128)S(1)}, f32[16,256]{1,0:T(8,128)}, u32[]{:S(2)}) copy-start(f32[16,256]{1,0:T(8,128)} %param.7) | copy-start | bytes 49156
  5.4 7.7 %copy-start.11 = (f32[16,256]{1,0:T(8,128)S(1)}, f32[16,256]{1,0:T(8,128)}, u32[]{:S(2)}) copy-start(f32[16,256]{1,0:T(8,128)} %param.8) | copy-start | bytes 49156
  5.4 33.0 %all-to-all-start = ((bf16[2,128,4096]{1,0,2:T(2,128)(2,1)}), bf16[2,128,4096]{1,0,2:T(2,128)(2,1)S(1)}, u32[]{:S(2)}, u32[]{:S(2)}) async-start(bf16[2,128,4096]{1,0,2:T(2,128)(2,1)} %copy.70), calls=%async_computation | async-start | bytes 4194304 | tf_op jit(solution)/shard_map/all_to_all | solution.py:97
  42.9 12.0 %slice-start.1 = ((bf16[3,128,4096]{2,1,0:T(8,128)(2,1)}), bf16[1,128,4096]{2,1,0:T(8,128)(2,1)S(1)}, s32[]{:S(2)}) async-start(bf16[3,128,4096]{2,1,0:T(8,128)(2,1)} %param.5), calls=%async_computation.4 | async-start | bytes 2097152 | tf_op jit(solution)/shard_map/slice | solution.py:105
  43.4 18.1 %collective-permute-start = (bf16[2,2,256]{2,1,0:T(2,128)(2,1)}, bf16[2,2,256]{2,1,0:T(2,128)(2,1)}, u32[]{:S(2)}, u32[]{:S(2)}) collective-permute-start(bf16[2,2,256]{2,1,0:T(2,128)(2,1)} %slice.116), channel_id=1, source_target_pairs={{0,16},{16,32},{32,48},{48,64},{64,80},{80,96},{96,112},{112,128},... | collective-permute-start | bytes 6152 | tf_op jit(solution)/shard_map/ppermute | solution.py:14
  64.5 1.0 copy-start.2
  64.5 5.4 %copy-start.14 = (f32[32]{0:T(128)S(1)}, f32[32]{0:T(128)}, u32[]{:S(2)}) copy-start(f32[32]{0:T(128)} %broadcast_subtract_fusion) | copy-start | bytes 388
  80.4 18.7 %all-to-all-start.1 = ((bf16[128,16,256]{0,2,1:T(8,128)(2,1)}), bf16[128,16,256]{0,2,1:T(8,128)(2,1)S(1)}, u32[]{:S(2)}, u32[]{:S(2)}) async-start(bf16[128,16,256]{0,2,1:T(8,128)(2,1)} %bitcast.11), calls=%async_computation.1 | async-start | bytes 2097152 | tf_op jit(solution)/shard_map/all_to_all | solution.py:106
  84.2 3.1 %copy-start.7 = (f32[16,256]{0,1:T(8,128)S(1)}, f32[16,256]{0,1:T(8,128)}, u32[]{:S(2)}) copy-start(f32[16,256]{0,1:T(8,128)} %copy.52) | copy-start | bytes 49156
  87.3 1.3 copy-start.6
  88.6 1.3 copy-start.5
  91.1 1.3 copy-start.4
  93.7 1.4 copy-start.1
  95.7 8.4 %copy-start.9 = (f32[16,256]{1,0:T(8,128)S(1)}, f32[16,256]{1,0:T(8,128)}, u32[]{:S(2)}) copy-start(f32[16,256]{1,0:T(8,128)} %param.7) | copy-start | bytes 49156
  95.7 8.4 %copy-start.10 = (f32[1,16,256]{2,1,0:T(8,128)S(1)}, f32[1,16,256]{2,1,0:T(8,128)}, u32[]{:S(2)}) copy-start(f32[1,16,256]{2,1,0:T(8,128)} %copy.59) | copy-start | bytes 49156
  99.6 5.1 %collective-permute-start.1 = (bf16[1,2,256]{2,1,0:T(2,128)(2,1)S(1)}, bf16[1,2,256]{2,1,0:T(2,128)(2,1)S(1)}, u32[]{:S(2)}, u32[]{:S(2)}) collective-permute-start(bf16[1,2,256]{2,1,0:T(2,128)(2,1)S(1)} %slice.127), channel_id=1, source_target_pairs={{0,16},{16,32},{32,48},{48,64},{64,80},{80,96},{96,112},{112,128},... | collective-permute-start | bytes 3080 | tf_op jit(solution)/shard_map/ppermute | solution.py:14
  105.0 17.6 %collective-permute-start.5 = (f32[16,256]{1,0:T(8,128)S(1)}, f32[16,256]{1,0:T(8,128)S(1)}, u32[]{:S(2)}, u32[]{:S(2)}) collective-permute-start(f32[16,256]{1,0:T(8,128)S(1)} %bitcast_add_fusion.1), channel_id=1, source_target_pairs={{0,64},{16,80},{32,96},{48,112},{64,128},{80,144},{96,160},{112,17... | collective-permute-start | bytes 49160 | tf_op jit(solution)/shard_map/ppermute | solution.py:14
  109.5 13.1 %collective-permute-start.4 = (f32[16,256]{1,0:T(8,128)S(1)}, f32[16,256]{1,0:T(8,128)S(1)}, u32[]{:S(2)}, u32[]{:S(2)}) collective-permute-start(f32[16,256]{1,0:T(8,128)S(1)} %bitcast_add_fusion.1), channel_id=1, source_target_pairs={{0,48},{16,64},{32,80},{48,96},{64,112},{80,128},{96,144},{112,160... | collective-permute-start | bytes 49160 | tf_op jit(solution)/shard_map/ppermute | solution.py:14
  118.2 4.4 %collective-permute-start.3 = (f32[16,256]{1,0:T(8,128)S(1)}, f32[16,256]{1,0:T(8,128)S(1)}, u32[]{:S(2)}, u32[]{:S(2)}) collective-permute-start(f32[16,256]{1,0:T(8,128)S(1)} %bitcast_add_fusion.1), channel_id=1, source_target_pairs={{0,32},{16,48},{32,64},{48,80},{64,96},{80,112},{96,128},{112,144}... | collective-permute-start | bytes 49160 | tf_op jit(solution)/shard_map/ppermute | solution.py:14
  120.5 3.1 %collective-permute-start.2 = (f32[16,256]{1,0:T(8,128)S(1)}, f32[16,256]{1,0:T(8,128)S(1)}, u32[]{:S(2)}, u32[]{:S(2)}) collective-permute-start(f32[16,256]{1,0:T(8,128)S(1)} %bitcast_add_fusion.1), channel_id=1, source_target_pairs={{0,16},{16,32},{32,48},{48,64},{64,80},{80,96},{96,112},{112,128},... | collective-permute-start | bytes 49160 | tf_op jit(solution)/shard_map/ppermute | solution.py:14
  123.6 23.2 %collective-permute-start.8 = (f32[16,256]{1,0:T(8,128)S(1)}, f32[16,256]{1,0:T(8,128)S(1)}, u32[]{:S(2)}, u32[]{:S(2)}) collective-permute-start(f32[16,256]{1,0:T(8,128)S(1)} %multiply_add_fusion.8), channel_id=1, source_target_pairs={{0,192},{16,208},{32,224},{48,240},{64,256},{80,272},{96,288},{112... | collective-permute-start | bytes 49160 | tf_op jit(solution)/shard_map/ppermute | solution.py:14
  135.7 11.1 %collective-permute-start.7 = (f32[16,256]{1,0:T(8,128)S(1)}, f32[16,256]{1,0:T(8,128)S(1)}, u32[]{:S(2)}, u32[]{:S(2)}) collective-permute-start(f32[16,256]{1,0:T(8,128)S(1)} %multiply_add_fusion.8), channel_id=1, source_target_pairs={{0,128},{16,144},{32,160},{48,176},{64,192},{80,208},{96,224},{112... | collective-permute-start | bytes 49160 | tf_op jit(solution)/shard_map/ppermute | solution.py:14
  139.2 7.6 %collective-permute-start.6 = (f32[16,256]{1,0:T(8,128)S(1)}, f32[16,256]{1,0:T(8,128)S(1)}, u32[]{:S(2)}, u32[]{:S(2)}) collective-permute-start(f32[16,256]{1,0:T(8,128)S(1)} %multiply_add_fusion.8), channel_id=1, source_target_pairs={{0,64},{16,80},{32,96},{48,112},{64,128},{80,144},{96,160},{112,17... | collective-permute-start | bytes 49160 | tf_op jit(solution)/shard_map/ppermute | solution.py:14
  141.3 8.1 %copy-start = (bf16[64,32,256]{0,1,2:T(8,128)(2,1)S(1)}, bf16[64,32,256]{0,1,2:T(8,128)(2,1)}, u32[]{:S(2)}) copy-start(bf16[64,32,256]{0,1,2:T(8,128)(2,1)} %copy.48) | copy-start | bytes 3145732
  146.9 8.9 %collective-permute-start.9 = (f32[16,256]{1,0:T(8,128)S(1)}, f32[16,256]{1,0:T(8,128)S(1)}, u32[]{:S(2)}, u32[]{:S(2)}) collective-permute-start(f32[16,256]{1,0:T(8,128)S(1)} %multiply_add_fusion.7), channel_id=1, source_target_pairs={{0,256},{16,272},{32,288},{48,304},{64,320},{80,336},{96,352},{112... | collective-permute-start | bytes 49160 | tf_op jit(solution)/shard_map/ppermute | solution.py:14
  168.4 5.3 %copy-start.3 = (bf16[2048,256]{1,0:T(8,128)(2,1)S(1)}, bf16[2048,256]{1,0:T(8,128)(2,1)}, u32[]{:S(2)}) copy-start(bf16[2048,256]{1,0:T(8,128)(2,1)} %copy-done.2) | copy-start | bytes 3145732
  168.4 5.3 %copy-start.13 = (f32[256]{0:T(256)S(1)}, f32[256]{0:T(256)}, u32[]{:S(2)}) copy-start(f32[256]{0:T(256)} %param.9) | copy-start | bytes 3076
  173.6 1.8 copy-start.12

commit v10 on v9

--- a/solution.py
+++ b/solution.py
@@ -5,7 +5,7 @@
 from jax import lax
 from jax.sharding import PartitionSpec as P
 
-block_len = 32
+block_len = 16
 
 
 def from_behind(block, axis, distance):

time: 198 us -> 195 us (0.985)
  matrix products: 23.9 us -> 13.3 us
  other arithmetic: 18.2 us -> 20.6 us
  blocking collectives: 15.9 us -> 17.9 us
    dot_general x1, matrix products: 12.5 us -> 5.45 us  [long_part(): jnp.einsum('nic,knc->kic', reading, starts, precision=lax.Precision.HIGHEST)]
    all_to_all x1, waiting for transfers between devices: 18.9 us -> 22.4 us  [arrive(): lax.all_to_all(streams, 'chan', split_axis=2, concat_axis=1, tiled=True)]
    exp x0 -> x1, local copies, waits for them, and re-layouts: none -> 3.46 us  [modal_tables(): jnp.exp(-decay_rate[:, None, :] * (block - 1.0 - positions)[None, :, None])]
    mul x1, local copies, waits for them, and re-layouts: 0.1 us -> 3.49 us  [modal_tables(): scaled_residue[:, None, :]]
    optimization_barrier x1, local copies, waits for them, and re-layouts: 5.52 us -> 2.47 us  [local(): lax.optimization_barrier((keys_values, features[0], toeplitz))]
    slice x2, local copies, waits for them, and re-layouts: 1.64 us -> 4.46 us  [long_part(): starts[count - 1]]
    reshape x1, local copies, waits for them, and re-layouts: 4.42 us -> 1.63 us  [long_part(): pieces = signal.reshape(count, block, signal.shape[1])]
    all_to_all x1, waiting for transfers between devices: 2.35 us -> 0.01 us  [local(): lax.all_to_all(queries, 'chan', split_axis=1, concat_axis=0, tiled=True)]
  transfers between devices with their start and end apart: 12 -> 12, of which waited for: 4 -> 2; matrix products, arithmetic and copies ran while one was open for 19% -> 22% of each run, Pallas kernels for 0% -> 0%
where the time goes in v10:
time: 195 us; the launch traced here: 192 us
  starting transfers between devices  66.5 us (34%)
  local copies, waits for them, and re-layouts  49.3 us (25%)
  waiting for transfers between devices  23.5 us (12%)
  other arithmetic  20.6 us (11%)
  blocking collectives  17.9 us (9%)
  matrix products  13.3 us (7%)
    ppermute x10, starting transfers between devices, from_behind(): return lax.ppermute(block, axis, route)  54.9 us
    all_to_all x1, waiting for transfers between devices, arrive(): lax.all_to_all(streams, 'chan', split_axis=2, concat_axis=1, tiled=True)  22.4 us
    all_to_all x1, blocking collectives, local(): lax.all_to_all(gated, 'chan', split_axis=0, concat_axis=1, tiled=True)  17.9 us
    add x7, other arithmetic, long_part(): starts + jnp.exp(-decay_rate * float(block * step)) * shifted(starts, step)  10.6 us
    all_to_all x1, starting transfers between devices, arrive(): lax.all_to_all(streams, 'chan', split_axis=2, concat_axis=1, tiled=True)  7.7 us
    unnamed x42, local copies, waits for them, and re-layouts  7.15 us
    dot_general x1, matrix products, long_part(): jnp.einsum('nic,knc->kic', reading, starts, precision=lax.Precision.HIGHEST)  5.45 us
    exp x7, local copies, waits for them, and re-layouts, long_part(): jnp.exp(-decay_rate * float(block * step)) * shifted(starts, step)  4.63 us
  transfers between devices with their start and end apart: 12, of which 2 were waited for; matrix products, arithmetic and copies ran while one was open for 22% of the time, Pallas kernels for 0%

profile of v10, /device:TPU:1, one launch (start us, length us, event | category | flops | bytes accessed | tf_op | source)
XLA Modules:
  0.0 191.5 jit_solution(17508875955149489068)
XLA Ops:
  0.0 1.6 slice-done
  1.6 3.8 %copy.103 = bf16[2,128,4096]{1,0,2:T(2,128)(2,1)} copy(bf16[2,128,4096]{2,1,0:T(8,128)(2,1)S(1)} %slice-done) | data formatting | bytes 4194304
  5.4 7.7 %all-to-all-start = ((bf16[2,128,4096]{1,0,2:T(2,128)(2,1)}), bf16[2,128,4096]{1,0,2:T(2,128)(2,1)S(1)}, u32[]{:S(2)}, u32[]{:S(2)}) async-start(bf16[2,128,4096]{1,0,2:T(2,128)(2,1)} %copy.103), calls=%async_computation | async-start | bytes 4194304 | tf_op jit(solution)/shard_map/all_to_all | solution.py:97
  14.7 1.0 exponential_multiply_fusion
  16.0 22.4 %all-to-all-done = bf16[2,128,4096]{1,0,2:T(2,128)(2,1)S(1)} async-done(((bf16[2,128,4096]{1,0,2:T(2,128)(2,1)}), bf16[2,128,4096]{1,0,2:T(2,128)(2,1)S(1)}, u32[]{:S(2)}, u32[]{:S(2)}) %all-to-all-start) | async-done | bytes 2097184 | tf_op jit(solution)/shard_map/all_to_all | solution.py:97
  38.4 1.6 copy.72
  40.0 2.9 %copy.73 = bf16[2,16,128,256]{3,2,1,0:T(8,128)(2,1)S(1)} copy(bf16[2,16,128,256]{2,3,1,0:T(8,128)(2,1)} %bitcast.70) | data formatting | bytes 4194304 | tf_op jit(solution)/shard_map/all_to_all | solution.py:97
  42.9 11.0 %collective-permute-start = (bf16[2,2,256]{2,1,0:T(2,128)(2,1)S(1)}, bf16[2,2,256]{2,1,0:T(2,128)(2,1)S(1)}, u32[]{:S(2)}, u32[]{:S(2)}) collective-permute-start(bf16[2,2,256]{2,1,0:T(2,128)(2,1)S(1)} %slice.120), channel_id=1, source_target_pairs={{0,16},{16,32},{32,48},{48,64},{64,80},{80,96},{96,112},{112,128},... | collective-permute-start | bytes 6152 | tf_op jit(solution)/shard_map/ppermute | solution.py:14
  53.9 1.3 copy.104
  55.3 3.5 %copy.80 = f32[16,16,256]{1,0,2:T(8,128)} copy(f32[16,16,256]{2,1,0:T(8,128)} %get-tuple-element.36) | data formatting | bytes 524288 | tf_op jit(solution)/shard_map/exp | solution.py:39
  63.9 1.4 add_convert_fusion
  65.6 1.0 copy-done
  66.6 1.6 copy.77
  68.3 3.1 %convolution_bitcast_fusion = f32[128,16,256]{0,1,2:T(8,128)S(1)} fusion(bf16[128,16,256]{0,1,2:T(8,128)(2,1)S(1)} %copy.77, f32[16,16,256]{1,0,2:T(8,128)} %copy.80), kind=kOutput, calls=%fused_computation.22 | convolution fusion | flops 100663296 | bytes 3407872 | tf_op jit(solution)/shard_map/njc,kjc->knc/dot_general | solution.py:58
  71.4 2.0 %slice.131 = f32[1,16,256]{0,1,2:T(8,128)} slice(f32[128,16,256]{0,1,2:T(8,128)S(1)} %convolution_bitcast_fusion), slice={[127:128], [0:16], [0:256]} | slice | bytes 32768 | tf_op jit(solution)/shard_map/slice | solution.py:64
  73.3 1.9 %pad_slice_fusion = f32[127,16,256]{0,1,2:T(8,128)} fusion(f32[127,16,256]{0,1,2:T(8,128)S(1)} %bitcast.59), kind=kLoop, calls=%fused_computation.21 | loop fusion | bytes 4161536 | tf_op jit(solution)/shard_map/slice | solution.py:48
  75.3 3.8 %all-to-all-start.1 = ((bf16[128,16,256]{0,2,1:T(8,128)(2,1)}), bf16[128,16,256]{0,2,1:T(8,128)(2,1)S(1)}, u32[]{:S(2)}, u32[]{:S(2)}) async-start(bf16[128,16,256]{0,2,1:T(8,128)(2,1)} %bitcast.11), calls=%async_computation.1 | async-start | bytes 2097152 | tf_op jit(solution)/shard_map/all_to_all | solution.py:106
  79.1 3.1 %multiply_add_fusion.6 = f32[128,16,256]{0,1,2:T(8,128)S(1)} fusion(f32[127,16,256]{0,1,2:T(8,128)} %pad_slice_fusion, f32[127,16,256]{0,1,2:T(8,128)S(1)} %bitcast.60, f32[16,256]{0,1:T(8,128)} %copy.81), kind=kLoop, calls=%fused_computation.19 | loop fusion | flops 1048576 | bytes 6275072 | tf_op jit(solution)/shard_map/add | solution.py:62
  82.2 1.3 multiply_add_fusion.5
  83.5 1.3 multiply_add_fusion.4
  84.8 1.3 multiply_add_fusion.3
  86.0 1.3 multiply_add_fusion.2
  87.3 1.3 multiply_add_fusion.1
  88.6 1.3 multiply_add_fusion
  89.9 1.9 %slice.130 = f32[1,16,256]{0,1,2:T(8,128)} slice(f32[128,16,256]{0,1,2:T(8,128)S(1)} %multiply_add_fusion), slice={[127:128], [0:16], [0:256]} | slice | bytes 32768 | tf_op jit(solution)/shard_map/slice | solution.py:64
  91.8 2.5 %copy.89 = f32[1,16,256]{2,1,0:T(8,128)S(1)} copy(f32[1,16,256]{0,1,2:T(8,128)} %slice.130) | data formatting | bytes 32768 | tf_op jit(solution)/shard_map/slice | solution.py:64
  94.3 2.5 %copy.90 = f32[1,16,256]{2,1,0:T(8,128)S(1)} copy(f32[1,16,256]{0,1,2:T(8,128)} %slice.131) | data formatting | bytes 32768 | tf_op jit(solution)/shard_map/slice | solution.py:64
  96.8 1.0 copy-done.4
  97.8 1.5 copy.91
  99.3 1.9 %collective-permute-start.1 = (bf16[1,2,256]{2,1,0:T(2,128)(2,1)S(1)}, bf16[1,2,256]{2,1,0:T(2,128)(2,1)S(1)}, u32[]{:S(2)}, u32[]{:S(2)}) collective-permute-start(bf16[1,2,256]{2,1,0:T(2,128)(2,1)S(1)} %slice.132), channel_id=1, source_target_pairs={{0,16},{16,32},{32,48},{48,64},{64,80},{80,96},{96,112},{112,128},... | collective-permute-start | bytes 3080 | tf_op jit(solution)/shard_map/ppermute | solution.py:14
  101.3 1.1 collective-permute-done.1
  102.4 1.5 pad_maximum_fusion.1
  103.9 3.8 %collective-permute-start.2 = (f32[16,256]{1,0:T(8,128)S(1)}, f32[16,256]{1,0:T(8,128)S(1)}, u32[]{:S(2)}, u32[]{:S(2)}) collective-permute-start(f32[16,256]{1,0:T(8,128)S(1)} %bitcast_add_fusion.1), channel_id=1, source_target_pairs={{0,16},{16,32},{32,48},{48,64},{64,80},{80,96},{96,112},{112,128},... | collective-permute-start | bytes 49160 | tf_op jit(solution)/shard_map/ppermute | solution.py:14
  107.6 3.5 %collective-permute-start.3 = (f32[16,256]{1,0:T(8,128)S(1)}, f32[16,256]{1,0:T(8,128)S(1)}, u32[]{:S(2)}, u32[]{:S(2)}) collective-permute-start(f32[16,256]{1,0:T(8,128)S(1)} %bitcast_add_fusion.1), channel_id=1, source_target_pairs={{0,32},{16,48},{32,64},{48,80},{64,96},{80,112},{96,128},{112,144}... | collective-permute-start | bytes 49160 | tf_op jit(solution)/shard_map/ppermute | solution.py:14
  111.2 4.9 %collective-permute-start.4 = (f32[16,256]{1,0:T(8,128)S(1)}, f32[16,256]{1,0:T(8,128)S(1)}, u32[]{:S(2)}, u32[]{:S(2)}) collective-permute-start(f32[16,256]{1,0:T(8,128)S(1)} %bitcast_add_fusion.1), channel_id=1, source_target_pairs={{0,48},{16,64},{32,80},{48,96},{64,112},{80,128},{96,144},{112,160... | collective-permute-start | bytes 49160 | tf_op jit(solution)/shard_map/ppermute | solution.py:14
  116.1 4.9 %collective-permute-start.5 = (f32[16,256]{1,0:T(8,128)S(1)}, f32[16,256]{1,0:T(8,128)S(1)}, u32[]{:S(2)}, u32[]{:S(2)}) collective-permute-start(f32[16,256]{1,0:T(8,128)S(1)} %bitcast_add_fusion.1), channel_id=1, source_target_pairs={{0,64},{16,80},{32,96},{48,112},{64,128},{80,144},{96,160},{112,17... | collective-permute-start | bytes 49160 | tf_op jit(solution)/shard_map/ppermute | solution.py:14
  122.6 9.1 %collective-permute-start.6 = (f32[16,256]{1,0:T(8,128)}, f32[16,256]{1,0:T(8,128)}, u32[]{:S(2)}, u32[]{:S(2)}) collective-permute-start(f32[16,256]{1,0:T(8,128)} %multiply_add_fusion.9), channel_id=1, source_target_pairs={{0,64},{16,80},{32,96},{48,112},{64,128},{80,144},{96,160},{112,17... | collective-permute-start | bytes 49160 | tf_op jit(solution)/shard_map/ppermute | solution.py:14
  131.7 7.1 %collective-permute-start.7 = (f32[16,256]{1,0:T(8,128)}, f32[16,256]{1,0:T(8,128)}, u32[]{:S(2)}, u32[]{:S(2)}) collective-permute-start(f32[16,256]{1,0:T(8,128)} %multiply_add_fusion.9), channel_id=1, source_target_pairs={{0,128},{16,144},{32,160},{48,176},{64,192},{80,208},{96,224},{112... | collective-permute-start | bytes 49160 | tf_op jit(solution)/shard_map/ppermute | solution.py:14
  138.8 4.9 %collective-permute-start.8 = (f32[16,256]{1,0:T(8,128)}, f32[16,256]{1,0:T(8,128)}, u32[]{:S(2)}, u32[]{:S(2)}) collective-permute-start(f32[16,256]{1,0:T(8,128)} %multiply_add_fusion.9), channel_id=1, source_target_pairs={{0,192},{16,208},{32,224},{48,240},{64,256},{80,272},{96,288},{112... | collective-permute-start | bytes 49160 | tf_op jit(solution)/shard_map/ppermute | solution.py:14
  145.0 3.5 %copy.93 = f32[16,16,256]{0,1,2:T(8,128)} copy(f32[16,16,256]{2,1,0:T(8,128)} %get-tuple-element.25) | data formatting | bytes 524288 | tf_op jit(solution)/shard_map/mul | solution.py:40
  148.5 2.5 %copy.78 = f32[16,16,256]{1,0,2:T(8,128)} copy(f32[16,16,256]{2,1,0:T(8,128)S(1)} %fusion.14) | data formatting | bytes 524288 | tf_op jit(solution)/shard_map/optimization_barrier | solution.py:105
  151.8 3.7 %collective-permute-start.9 = (f32[16,256]{1,0:T(8,128)S(1)}, f32[16,256]{1,0:T(8,128)S(1)}, u32[]{:S(2)}, u32[]{:S(2)}) collective-permute-start(f32[16,256]{1,0:T(8,128)S(1)} %multiply_add_fusion.8), channel_id=1, source_target_pairs={{0,256},{16,272},{32,288},{48,304},{64,320},{80,336},{96,352},{112... | collective-permute-start | bytes 49160 | tf_op jit(solution)/shard_map/ppermute | solution.py:14
  155.6 4.4 %fusion.17 = f32[256,128,16]{1,2,0:T(8,128)} fusion(bf16[128,16,256]{0,1,2:T(8,128)(2,1)} %copy-done.2, f32[16,16,256]{1,0,2:T(8,128)} %copy.78), kind=kOutput, calls=%fused_computation.61 | convolution fusion | flops 100663296 | bytes 3407872 | tf_op jit(solution)/shard_map/ijc,kjc->kic/dot_general | solution.py:81
  160.1 5.5 %add_bitcast_fusion = f32[128,16,256]{0,1,2:T(8,128)} fusion(f32[256,128,16]{1,2,0:T(8,128)} %fusion.17, f32[16,16,256]{0,1,2:T(8,128)} %copy.93, f32[128,16,256]{0,1,2:T(8,128)S(1)} %multiply_add_fusion, f32[16,256]{0,1:T(8,128)S(1)} %copy.92, f32[128]{0:T(128)S(1)} %copy-done.18, f32[16,256]{0,1:T(8,128)S(1)} %copy.88), kind=kOutput, calls=%fused_computation.7 | convolution fusion | flops 102760448 | bytes 6586880 | tf_op jit(solution)/shard_map/nic,knc->kic/dot_general | solution.py:84
  165.6 3.3 %copy.94 = f32[128,16,256]{2,1,0:T(8,128)} copy(f32[128,16,256]{0,1,2:T(8,128)} %add_bitcast_fusion) | data formatting | bytes 4194304 | tf_op jit(solution)/shard_map/add | solution.py:85
  168.9 1.8 fusion.1
  171.7 17.9 %all_to_all.53 = bf16[16,128,256]{2,1,0:T(8,128)(2,1)S(1)} all-to-all(bf16[16,128,256]{2,1,0:T(8,128)(2,1)S(1)} %bitcast.76), channel_id=1, replica_groups=mesh['seq'=32,'chan'=16] {'chan'}, dimensions={0} | all-to-all | bytes 2097152 | tf_op jit(solution)/shard_map/all_to_all | solution.py:120
  190.2 1.3 copy.96
  (78 shorter events, 12.8 us)
Async XLA Ops:
  0.0 1.6 slice-start
  5.4 8.6 %copy-start.10 = (f32[16,256]{1,0:T(8,128)S(1)}, f32[16,256]{1,0:T(8,128)}, u32[]{:S(2)}) copy-start(f32[16,256]{1,0:T(8,128)} %param.7) | copy-start | bytes 49156
  5.4 8.7 %copy-start.16 = (f32[16,256]{1,0:T(8,128)S(1)}, f32[16,256]{1,0:T(8,128)}, u32[]{:S(2)}) copy-start(f32[16,256]{1,0:T(8,128)} %param.8) | copy-start | bytes 49156
  5.4 33.0 %all-to-all-start = ((bf16[2,128,4096]{1,0,2:T(2,128)(2,1)}), bf16[2,128,4096]{1,0,2:T(2,128)(2,1)S(1)}, u32[]{:S(2)}, u32[]{:S(2)}) async-start(bf16[2,128,4096]{1,0,2:T(2,128)(2,1)} %copy.103), calls=%async_computation | async-start | bytes 4194304 | tf_op jit(solution)/shard_map/all_to_all | solution.py:97
  14.7 1.0 copy-start.13
  42.9 11.1 %slice-start.1 = ((bf16[3,128,4096]{2,1,0:T(8,128)(2,1)}), bf16[1,128,4096]{2,1,0:T(8,128)(2,1)S(1)}, s32[]{:S(2)}) async-start(bf16[3,128,4096]{2,1,0:T(8,128)(2,1)} %param.5), calls=%async_computation.4 | async-start | bytes 2097152 | tf_op jit(solution)/shard_map/slice | solution.py:105
  42.9 20.5 %collective-permute-start = (bf16[2,2,256]{2,1,0:T(2,128)(2,1)S(1)}, bf16[2,2,256]{2,1,0:T(2,128)(2,1)S(1)}, u32[]{:S(2)}, u32[]{:S(2)}) collective-permute-start(bf16[2,2,256]{2,1,0:T(2,128)(2,1)S(1)} %slice.120), channel_id=1, source_target_pairs={{0,16},{16,32},{32,48},{48,64},{64,80},{80,96},{96,112},{112,128},... | collective-permute-start | bytes 6152 | tf_op jit(solution)/shard_map/ppermute | solution.py:14
  55.3 7.2 %copy-start.15 = (f32[16,256]{1,0:T(8,128)S(1)}, f32[16,256]{1,0:T(8,128)}, u32[]{:S(2)}) copy-start(f32[16,256]{1,0:T(8,128)} %get-tuple-element.33) | copy-start | bytes 49156
  55.3 7.3 %copy-start.14 = (f32[16,256]{1,0:T(8,128)S(1)}, f32[16,256]{1,0:T(8,128)}, u32[]{:S(2)}) copy-start(f32[16,256]{1,0:T(8,128)} %get-tuple-element.27) | copy-start | bytes 49156
  65.6 1.0 copy-start
  68.3 3.1 %copy-start.2 = (bf16[128,16,256]{0,1,2:T(8,128)(2,1)}, bf16[128,16,256]{0,1,2:T(8,128)(2,1)S(1)}, u32[]{:S(2)}) copy-start(bf16[128,16,256]{0,1,2:T(8,128)(2,1)S(1)} %copy.77) | copy-start | bytes 3145732
  75.3 21.6 %all-to-all-start.1 = ((bf16[128,16,256]{0,2,1:T(8,128)(2,1)}), bf16[128,16,256]{0,2,1:T(8,128)(2,1)S(1)}, u32[]{:S(2)}, u32[]{:S(2)}) async-start(bf16[128,16,256]{0,2,1:T(8,128)(2,1)} %bitcast.11), calls=%async_computation.1 | async-start | bytes 2097152 | tf_op jit(solution)/shard_map/all_to_all | solution.py:106
  79.1 3.1 %copy-start.9 = (f32[16,256]{0,1:T(8,128)S(1)}, f32[16,256]{0,1:T(8,128)}, u32[]{:S(2)}) copy-start(f32[16,256]{0,1:T(8,128)} %copy.82) | copy-start | bytes 49156
  82.2 1.3 copy-start.8
  83.5 1.3 copy-start.7
  84.8 1.3 copy-start.6
  87.3 1.3 copy-start.5
  94.3 7.0 %copy-start.11 = (f32[16,256]{1,0:T(8,128)S(1)}, f32[16,256]{1,0:T(8,128)}, u32[]{:S(2)}) copy-start(f32[16,256]{1,0:T(8,128)} %param.7) | copy-start | bytes 49156
  96.8 1.0 copy-start.4
  99.3 2.0 %copy-start.3 = (bf16[16,128,256]{2,1,0:T(8,128)(2,1)}, bf16[16,128,256]{2,1,0:T(8,128)(2,1)S(1)}, u32[]{:S(2)}) copy-start(bf16[16,128,256]{2,1,0:T(8,128)(2,1)S(1)} %copy.91) | copy-start | bytes 3145732
  99.3 3.1 %collective-permute-start.1 = (bf16[1,2,256]{2,1,0:T(2,128)(2,1)S(1)}, bf16[1,2,256]{2,1,0:T(2,128)(2,1)S(1)}, u32[]{:S(2)}, u32[]{:S(2)}) collective-permute-start(bf16[1,2,256]{2,1,0:T(2,128)(2,1)S(1)} %slice.132), channel_id=1, source_target_pairs={{0,16},{16,32},{32,48},{48,64},{64,80},{80,96},{96,112},{112,128},... | collective-permute-start | bytes 3080 | tf_op jit(solution)/shard_map/ppermute | solution.py:14
  103.9 18.1 %collective-permute-start.2 = (f32[16,256]{1,0:T(8,128)S(1)}, f32[16,256]{1,0:T(8,128)S(1)}, u32[]{:S(2)}, u32[]{:S(2)}) collective-permute-start(f32[16,256]{1,0:T(8,128)S(1)} %bitcast_add_fusion.1), channel_id=1, source_target_pairs={{0,16},{16,32},{32,48},{48,64},{64,80},{80,96},{96,112},{112,128},... | collective-permute-start | bytes 49160 | tf_op jit(solution)/shard_map/ppermute | solution.py:14
  107.6 14.3 %collective-permute-start.3 = (f32[16,256]{1,0:T(8,128)S(1)}, f32[16,256]{1,0:T(8,128)S(1)}, u32[]{:S(2)}, u32[]{:S(2)}) collective-permute-start(f32[16,256]{1,0:T(8,128)S(1)} %bitcast_add_fusion.1), channel_id=1, source_target_pairs={{0,32},{16,48},{32,64},{48,80},{64,96},{80,112},{96,128},{112,144}... | collective-permute-start | bytes 49160 | tf_op jit(solution)/shard_map/ppermute | solution.py:14
  111.2 10.7 %collective-permute-start.4 = (f32[16,256]{1,0:T(8,128)S(1)}, f32[16,256]{1,0:T(8,128)S(1)}, u32[]{:S(2)}, u32[]{:S(2)}) collective-permute-start(f32[16,256]{1,0:T(8,128)S(1)} %bitcast_add_fusion.1), channel_id=1, source_target_pairs={{0,48},{16,64},{32,80},{48,96},{64,112},{80,128},{96,144},{112,160... | collective-permute-start | bytes 49160 | tf_op jit(solution)/shard_map/ppermute | solution.py:14
  116.1 5.8 %collective-permute-start.5 = (f32[16,256]{1,0:T(8,128)S(1)}, f32[16,256]{1,0:T(8,128)S(1)}, u32[]{:S(2)}, u32[]{:S(2)}) collective-permute-start(f32[16,256]{1,0:T(8,128)S(1)} %bitcast_add_fusion.1), channel_id=1, source_target_pairs={{0,64},{16,80},{32,96},{48,112},{64,128},{80,144},{96,160},{112,17... | collective-permute-start | bytes 49160 | tf_op jit(solution)/shard_map/ppermute | solution.py:14
  122.6 28.4 %collective-permute-start.6 = (f32[16,256]{1,0:T(8,128)}, f32[16,256]{1,0:T(8,128)}, u32[]{:S(2)}, u32[]{:S(2)}) collective-permute-start(f32[16,256]{1,0:T(8,128)} %multiply_add_fusion.9), channel_id=1, source_target_pairs={{0,64},{16,80},{32,96},{48,112},{64,128},{80,144},{96,160},{112,17... | collective-permute-start | bytes 49160 | tf_op jit(solution)/shard_map/ppermute | solution.py:14
  131.7 19.3 %collective-permute-start.7 = (f32[16,256]{1,0:T(8,128)}, f32[16,256]{1,0:T(8,128)}, u32[]{:S(2)}, u32[]{:S(2)}) collective-permute-start(f32[16,256]{1,0:T(8,128)} %multiply_add_fusion.9), channel_id=1, source_target_pairs={{0,128},{16,144},{32,160},{48,176},{64,192},{80,208},{96,224},{112... | collective-permute-start | bytes 49160 | tf_op jit(solution)/shard_map/ppermute | solution.py:14
  138.8 12.2 %collective-permute-start.8 = (f32[16,256]{1,0:T(8,128)}, f32[16,256]{1,0:T(8,128)}, u32[]{:S(2)}, u32[]{:S(2)}) collective-permute-start(f32[16,256]{1,0:T(8,128)} %multiply_add_fusion.9), channel_id=1, source_target_pairs={{0,192},{16,208},{32,224},{48,240},{64,256},{80,272},{96,288},{112... | collective-permute-start | bytes 49160 | tf_op jit(solution)/shard_map/ppermute | solution.py:14
  151.8 8.2 %copy-start.12 = (f32[16,256]{1,0:T(8,128)S(1)}, f32[16,256]{1,0:T(8,128)}, u32[]{:S(2)}) copy-start(f32[16,256]{1,0:T(8,128)} %param.7) | copy-start | bytes 49156
  151.8 8.3 %copy-start.18 = (f32[128]{0:T(128)S(1)}, f32[128]{0:T(128)}, u32[]{:S(2)}) copy-start(f32[128]{0:T(128)} %convert_multiply_fusion.1) | copy-start | bytes 1540
  151.8 8.2 %collective-permute-start.9 = (f32[16,256]{1,0:T(8,128)S(1)}, f32[16,256]{1,0:T(8,128)S(1)}, u32[]{:S(2)}, u32[]{:S(2)}) collective-permute-start(f32[16,256]{1,0:T(8,128)S(1)} %multiply_add_fusion.8), channel_id=1, source_target_pairs={{0,256},{16,272},{32,288},{48,304},{64,320},{80,336},{96,352},{112... | collective-permute-start | bytes 49160 | tf_op jit(solution)/shard_map/ppermute | solution.py:14
  165.6 3.3 %copy-start.1 = (bf16[2048,256]{1,0:T(8,128)(2,1)S(1)}, bf16[2048,256]{1,0:T(8,128)(2,1)}, u32[]{:S(2)}) copy-start(bf16[2048,256]{1,0:T(8,128)(2,1)} %copy-done) | copy-start | bytes 3145732
  165.6 3.3 %copy-start.17 = (f32[256]{0:T(256)S(1)}, f32[256]{0:T(256)}, u32[]{:S(2)}) copy-start(f32[256]{0:T(256)} %param.9) | copy-start | bytes 3076

commit v11 on v10

--- a/solution.py
+++ b/solution.py
@@ -5,7 +5,7 @@
 from jax import lax
 from jax.sharding import PartitionSpec as P
 
-block_len = 16
+block_len = 8
 
 
 def from_behind(block, axis, distance):

time: 195 us -> 203 us (1.041)
  other arithmetic: 20.6 us -> 27.3 us
  starting transfers between devices: 66.5 us -> 69.3 us
  local copies, waits for them, and re-layouts: 49.3 us -> 47 us
  blocking collectives: 17.9 us -> 20.1 us
    add x7 -> x8, other arithmetic: 10.6 us -> 17.2 us  [long_part(): starts + jnp.exp(-decay_rate * float(block * step)) * shifted(starts, step)]
    exp x1 -> x0, local copies, waits for them, and re-layouts: 3.46 us -> none  [modal_tables(): jnp.exp(-decay_rate[:, None, :] * (block - 1.0 - positions)[None, :, None])]
    mul x1, local copies, waits for them, and re-layouts: 3.49 us -> 0.1 us  [local(): scaled = residue * jnp.sqrt(1.0 - jnp.exp(-2.0 * decay_rate))]
    ppermute x10, starting transfers between devices: 54.9 us -> 57.9 us  [from_behind(): return lax.ppermute(block, axis, route)]
    exp x7 -> x8, local copies, waits for them, and re-layouts: 4.63 us -> 6.84 us  [long_part(): jnp.exp(-decay_rate * float(block * step)) * shifted(starts, step)]
    all_to_all x1, blocking collectives: 17.9 us -> 20.1 us  [local(): lax.all_to_all(gated, 'chan', split_axis=0, concat_axis=1, tiled=True)]
  transfers between devices with their start and end apart: 12 -> 12, of which waited for: 2 -> 3; matrix products, arithmetic and copies ran while one was open for 22% -> 23% of each run, Pallas kernels for 0% -> 0%
where the time goes in v11:
time: 203 us; the launch traced here: 200 us
  starting transfers between devices  69.3 us (34%)
  local copies, waits for them, and re-layouts  47 us (23%)
  other arithmetic  27.3 us (13%)
  waiting for transfers between devices  22.7 us (11%)
  blocking collectives  20.1 us (10%)
  matrix products  13.1 us (6%)
    ppermute x10, starting transfers between devices, from_behind(): return lax.ppermute(block, axis, route)  57.9 us
    all_to_all x1, waiting for transfers between devices, arrive(): lax.all_to_all(streams, 'chan', split_axis=2, concat_axis=1, tiled=True)  20.8 us
    all_to_all x1, blocking collectives, local(): lax.all_to_all(gated, 'chan', split_axis=0, concat_axis=1, tiled=True)  20.1 us
    add x8, other arithmetic, long_part(): starts + jnp.exp(-decay_rate * float(block * step)) * shifted(starts, step)  17.2 us
    unnamed x42, local copies, waits for them, and re-layouts  9 us
    all_to_all x1, starting transfers between devices, arrive(): lax.all_to_all(streams, 'chan', split_axis=2, concat_axis=1, tiled=True)  7.57 us
    exp x8, local copies, waits for them, and re-layouts, long_part(): jnp.exp(-decay_rate * float(block * step)) * shifted(starts, step)  6.84 us
    dot_general x1, matrix products, long_part(): jnp.einsum('nic,knc->kic', reading, starts, precision=lax.Precision.HIGHEST)  6.53 us
  transfers between devices with their start and end apart: 12, of which 3 were waited for; matrix products, arithmetic and copies ran while one was open for 23% of the time, Pallas kernels for 0%

profile of v11, /device:TPU:1, one launch (start us, length us, event | category | flops | bytes accessed | tf_op | source)
XLA Modules:
  0.0 199.9 jit_solution(16438466808769133873)
XLA Ops:
  0.0 1.6 slice-done
  1.6 3.8 %copy.74 = bf16[2,128,4096]{1,0,2:T(2,128)(2,1)} copy(bf16[2,128,4096]{2,1,0:T(8,128)(2,1)S(1)} %slice-done) | data formatting | bytes 4194304
  5.4 7.6 %all-to-all-start = ((bf16[2,128,4096]{1,0,2:T(2,128)(2,1)}), bf16[2,128,4096]{1,0,2:T(2,128)(2,1)S(1)}, u32[]{:S(2)}, u32[]{:S(2)}) async-start(bf16[2,128,4096]{1,0,2:T(2,128)(2,1)} %copy.74), calls=%async_computation | async-start | bytes 4194304 | tf_op jit(solution)/shard_map/all_to_all | solution.py:97
  13.8 1.4 constant_dynamic-slice_fusion.2
  17.5 20.8 %all-to-all-done = bf16[2,128,4096]{1,0,2:T(2,128)(2,1)S(1)} async-done(((bf16[2,128,4096]{1,0,2:T(2,128)(2,1)}), bf16[2,128,4096]{1,0,2:T(2,128)(2,1)S(1)}, u32[]{:S(2)}, u32[]{:S(2)}) %all-to-all-start) | async-done | bytes 2097184 | tf_op jit(solution)/shard_map/all_to_all | solution.py:97
  38.2 1.6 copy.44
  39.9 2.9 %copy.45 = bf16[2,16,128,256]{3,2,1,0:T(8,128)(2,1)S(1)} copy(bf16[2,16,128,256]{2,3,1,0:T(8,128)(2,1)} %bitcast.67) | data formatting | bytes 4194304 | tf_op jit(solution)/shard_map/all_to_all | solution.py:97
  43.4 10.9 %collective-permute-start = (bf16[2,2,256]{2,1,0:T(2,128)(2,1)}, bf16[2,2,256]{2,1,0:T(2,128)(2,1)}, u32[]{:S(2)}, u32[]{:S(2)}) collective-permute-start(bf16[2,2,256]{2,1,0:T(2,128)(2,1)} %slice.124), channel_id=1, source_target_pairs={{0,16},{16,32},{32,48},{48,64},{64,80},{80,96},{96,112},{112,128},... | collective-permute-start | bytes 6152 | tf_op jit(solution)/shard_map/ppermute | solution.py:14
  54.9 1.3 copy.75
  61.5 1.5 copy.60
  63.0 1.2 pad_maximum_fusion
  64.2 1.4 add_convert_fusion
  65.9 1.3 copy.50
  67.2 2.1 %convolution_bitcast_fusion = f32[256,16,256]{0,1,2:T(8,128)S(1)} fusion(bf16[256,8,256]{0,1,2:T(8,128)(2,1)S(1)} %copy.50, f32[8]{0:T(128)S(1)} %copy-done.17, f32[16,256]{0,1:T(8,128)S(1)} %copy.48), kind=kOutput, calls=%fused_computation.15 | convolution fusion | flops 100696064 | bytes 5259296 | tf_op jit(solution)/shard_map/njc,kjc->knc/dot_general | solution.py:58
  69.3 3.3 %pad_slice_fusion = f32[255,16,256]{0,1,2:T(8,128)} fusion(f32[255,16,256]{0,1,2:T(8,128)S(1)} %bitcast.56), kind=kLoop, calls=%fused_computation.14 | loop fusion | bytes 8355840 | tf_op jit(solution)/shard_map/slice | solution.py:48
  72.6 3.8 %all-to-all-start.1 = ((bf16[128,16,256]{0,2,1:T(8,128)(2,1)}), bf16[128,16,256]{0,2,1:T(8,128)(2,1)S(1)}, u32[]{:S(2)}, u32[]{:S(2)}) async-start(bf16[128,16,256]{0,2,1:T(8,128)(2,1)} %bitcast.11), calls=%async_computation.1 | async-start | bytes 2097152 | tf_op jit(solution)/shard_map/all_to_all | solution.py:106
  76.4 5.1 %multiply_add_fusion.7 = f32[256,16,256]{0,1,2:T(8,128)S(1)} fusion(f32[255,16,256]{0,1,2:T(8,128)} %pad_slice_fusion, f32[255,16,256]{0,1,2:T(8,128)} %bitcast.57, f32[16,256]{0,1:T(8,128)} %copy.53), kind=kLoop, calls=%fused_computation.12 | loop fusion | flops 2097152 | bytes 12566528 | tf_op jit(solution)/shard_map/add | solution.py:62
  81.6 1.9 multiply_add_fusion.6
  83.5 1.9 multiply_add_fusion.5
  85.4 1.9 multiply_add_fusion.4
  87.4 1.9 multiply_add_fusion.3
  89.3 1.9 multiply_add_fusion.2
  91.5 2.0 slice.136
  93.4 1.9 multiply_add_fusion.1
  97.0 2.0 copy-done.2
  99.0 2.0 %slice.135 = f32[1,16,256]{0,1,2:T(8,128)} slice(f32[256,16,256]{0,1,2:T(8,128)S(1)} %multiply_add_fusion), slice={[255:256], [0:16], [0:256]} | slice | bytes 32768 | tf_op jit(solution)/shard_map/slice | solution.py:64
  101.0 2.5 %copy.62 = f32[1,16,256]{2,1,0:T(8,128)S(1)} copy(f32[1,16,256]{0,1,2:T(8,128)} %slice.135) | data formatting | bytes 32768 | tf_op jit(solution)/shard_map/slice | solution.py:64
  103.5 2.5 %copy.63 = f32[1,16,256]{2,1,0:T(8,128)S(1)} copy(f32[1,16,256]{0,1,2:T(8,128)} %slice.136) | data formatting | bytes 32768 | tf_op jit(solution)/shard_map/slice | solution.py:64
  106.0 1.0 copy-done.4
  107.0 1.5 copy.64
  108.5 1.9 collective-permute-start.1
  110.5 1.1 collective-permute-done.1
  111.6 1.5 pad_maximum_fusion.1
  113.0 3.8 %collective-permute-start.2 = (f32[16,256]{1,0:T(8,128)S(1)}, f32[16,256]{1,0:T(8,128)S(1)}, u32[]{:S(2)}, u32[]{:S(2)}) collective-permute-start(f32[16,256]{1,0:T(8,128)S(1)} %bitcast_add_fusion.1), channel_id=1, source_target_pairs={{0,16},{16,32},{32,48},{48,64},{64,80},{80,96},{96,112},{112,128},... | collective-permute-start | bytes 49160 | tf_op jit(solution)/shard_map/ppermute | solution.py:14
  116.8 3.5 %collective-permute-start.3 = (f32[16,256]{1,0:T(8,128)S(1)}, f32[16,256]{1,0:T(8,128)S(1)}, u32[]{:S(2)}, u32[]{:S(2)}) collective-permute-start(f32[16,256]{1,0:T(8,128)S(1)} %bitcast_add_fusion.1), channel_id=1, source_target_pairs={{0,32},{16,48},{32,64},{48,80},{64,96},{80,112},{96,128},{112,144}... | collective-permute-start | bytes 49160 | tf_op jit(solution)/shard_map/ppermute | solution.py:14
  120.4 4.9 %collective-permute-start.4 = (f32[16,256]{1,0:T(8,128)S(1)}, f32[16,256]{1,0:T(8,128)S(1)}, u32[]{:S(2)}, u32[]{:S(2)}) collective-permute-start(f32[16,256]{1,0:T(8,128)S(1)} %bitcast_add_fusion.1), channel_id=1, source_target_pairs={{0,48},{16,64},{32,80},{48,96},{64,112},{80,128},{96,144},{112,160... | collective-permute-start | bytes 49160 | tf_op jit(solution)/shard_map/ppermute | solution.py:14
  125.3 4.9 %collective-permute-start.5 = (f32[16,256]{1,0:T(8,128)S(1)}, f32[16,256]{1,0:T(8,128)S(1)}, u32[]{:S(2)}, u32[]{:S(2)}) collective-permute-start(f32[16,256]{1,0:T(8,128)S(1)} %bitcast_add_fusion.1), channel_id=1, source_target_pairs={{0,64},{16,80},{32,96},{48,112},{64,128},{80,144},{96,160},{112,17... | collective-permute-start | bytes 49160 | tf_op jit(solution)/shard_map/ppermute | solution.py:14
  131.1 6.1 %collective-permute-start.6 = (f32[16,256]{1,0:T(8,128)S(1)}, f32[16,256]{1,0:T(8,128)S(1)}, u32[]{:S(2)}, u32[]{:S(2)}) collective-permute-start(f32[16,256]{1,0:T(8,128)S(1)} %multiply_add_fusion.10), channel_id=1, source_target_pairs={{0,64},{16,80},{32,96},{48,112},{64,128},{80,144},{96,160},{112,17... | collective-permute-start | bytes 49160 | tf_op jit(solution)/shard_map/ppermute | solution.py:14
  137.2 6.7 %collective-permute-start.7 = (f32[16,256]{1,0:T(8,128)S(1)}, f32[16,256]{1,0:T(8,128)S(1)}, u32[]{:S(2)}, u32[]{:S(2)}) collective-permute-start(f32[16,256]{1,0:T(8,128)S(1)} %multiply_add_fusion.10), channel_id=1, source_target_pairs={{0,128},{16,144},{32,160},{48,176},{64,192},{80,208},{96,224},{112... | collective-permute-start | bytes 49160 | tf_op jit(solution)/shard_map/ppermute | solution.py:14
  144.0 6.2 %collective-permute-start.8 = (f32[16,256]{1,0:T(8,128)S(1)}, f32[16,256]{1,0:T(8,128)}, u32[]{:S(2)}, u32[]{:S(2)}) collective-permute-start(f32[16,256]{1,0:T(8,128)S(1)} %multiply_add_fusion.10), channel_id=1, source_target_pairs={{0,192},{16,208},{32,224},{48,240},{64,256},{80,272},{96,288},{112... | collective-permute-start | bytes 49160 | tf_op jit(solution)/shard_map/ppermute | solution.py:14
  150.7 1.3 copy.51
  152.7 9.0 %collective-permute-start.9 = (f32[16,256]{1,0:T(8,128)S(1)}, f32[16,256]{1,0:T(8,128)S(1)}, u32[]{:S(2)}, u32[]{:S(2)}) collective-permute-start(f32[16,256]{1,0:T(8,128)S(1)} %multiply_add_fusion.9), channel_id=1, source_target_pairs={{0,256},{16,272},{32,288},{48,304},{64,320},{80,336},{96,352},{112... | collective-permute-start | bytes 49160 | tf_op jit(solution)/shard_map/ppermute | solution.py:14
  161.7 3.6 %fusion.27 = f32[256,256,8]{1,2,0:T(8,128)} fusion(bf16[256,8,256]{0,1,2:T(8,128)(2,1)S(1)} %copy.50, f32[8,8,256]{1,0,2:T(8,128)} %copy.51), kind=kOutput, calls=%fused_computation.71 | convolution fusion | flops 50331648 | bytes 3211264 | tf_op jit(solution)/shard_map/ijc,kjc->kic/dot_general | solution.py:81
  165.4 6.5 %add_bitcast_fusion = f32[256,8,256]{0,1,2:T(8,128)} fusion(f32[256,256,8]{1,2,0:T(8,128)} %fusion.27, f32[256,16,256]{0,1,2:T(8,128)} %copy-done.2, f32[16,256]{0,1:T(8,128)S(1)} %copy.65, f32[256]{0:T(256)S(1)} %convert_multiply_fusion.1, f32[16,256]{0,1:T(8,128)S(1)} %copy.48, f32[8]{0:T(128)S(1)} %copy-done.18, f32[16,256]{0,1:T(8,128)S(1)} %copy.47), kind=kOutput, calls=%fused_computation.22 | convolution fusion | flops 104398848 | bytes 8438816 | tf_op jit(solution)/shard_map/nic,knc->kic/dot_general | solution.py:84
  172.0 3.1 %copy.66 = f32[256,8,256]{2,1,0:T(8,128)} copy(f32[256,8,256]{0,1,2:T(8,128)} %add_bitcast_fusion) | data formatting | bytes 4194304 | tf_op jit(solution)/shard_map/add | solution.py:85
  175.1 1.8 fusion.6
  177.9 20.1 %all_to_all.53 = bf16[16,128,256]{2,1,0:T(8,128)(2,1)S(1)} all-to-all(bf16[16,128,256]{2,1,0:T(8,128)(2,1)S(1)} %bitcast.73), channel_id=1, replica_groups=mesh['seq'=32,'chan'=16] {'chan'}, dimensions={0} | all-to-all | bytes 2097152 | tf_op jit(solution)/shard_map/all_to_all | solution.py:120
  198.6 1.3 copy.68
  (81 shorter events, 15.7 us)
Async XLA Ops:
  0.0 1.6 slice-start
  1.6 11.4 %copy-start.11 = (f32[16,256]{1,0:T(8,128)S(1)}, f32[16,256]{1,0:T(8,128)}, u32[]{:S(2)}) copy-start(f32[16,256]{1,0:T(8,128)} %param.7) | copy-start | bytes 49156
  1.6 11.4 %copy-start.14 = (f32[16,256]{1,0:T(8,128)S(1)}, f32[16,256]{1,0:T(8,128)}, u32[]{:S(2)}) copy-start(f32[16,256]{1,0:T(8,128)} %param.8) | copy-start | bytes 49156
  5.4 32.9 %all-to-all-start = ((bf16[2,128,4096]{1,0,2:T(2,128)(2,1)}), bf16[2,128,4096]{1,0,2:T(2,128)(2,1)S(1)}, u32[]{:S(2)}, u32[]{:S(2)}) async-start(bf16[2,128,4096]{1,0,2:T(2,128)(2,1)} %copy.74), calls=%async_computation | async-start | bytes 4194304 | tf_op jit(solution)/shard_map/all_to_all | solution.py:97
  39.9 15.0 %slice-start.1 = ((bf16[3,128,4096]{2,1,0:T(8,128)(2,1)}), bf16[1,128,4096]{2,1,0:T(8,128)(2,1)S(1)}, s32[]{:S(2)}) async-start(bf16[3,128,4096]{2,1,0:T(8,128)(2,1)} %param.5), calls=%async_computation.4 | async-start | bytes 2097152 | tf_op jit(solution)/shard_map/slice | solution.py:105
  43.4 19.6 %collective-permute-start = (bf16[2,2,256]{2,1,0:T(2,128)(2,1)}, bf16[2,2,256]{2,1,0:T(2,128)(2,1)}, u32[]{:S(2)}, u32[]{:S(2)}) collective-permute-start(bf16[2,2,256]{2,1,0:T(2,128)(2,1)} %slice.124), channel_id=1, source_target_pairs={{0,16},{16,32},{32,48},{48,64},{64,80},{80,96},{96,112},{112,128},... | collective-permute-start | bytes 6152 | tf_op jit(solution)/shard_map/ppermute | solution.py:14
  65.6 1.6 copy-start.17
  69.3 3.3 %copy-start = (f32[256,16,256]{0,1,2:T(8,128)}, f32[256,16,256]{0,1,2:T(8,128)S(1)}, u32[]{:S(2)}) copy-start(f32[256,16,256]{0,1,2:T(8,128)S(1)} %convolution_bitcast_fusion) | copy-start | bytes 12582916
  72.6 33.5 %all-to-all-start.1 = ((bf16[128,16,256]{0,2,1:T(8,128)(2,1)}), bf16[128,16,256]{0,2,1:T(8,128)(2,1)S(1)}, u32[]{:S(2)}, u32[]{:S(2)}) async-start(bf16[128,16,256]{0,2,1:T(8,128)(2,1)} %bitcast.11), calls=%async_computation.1 | async-start | bytes 2097152 | tf_op jit(solution)/shard_map/all_to_all | solution.py:106
  76.4 5.2 %copy-start.9 = (f32[16,256]{0,1:T(8,128)S(1)}, f32[16,256]{0,1:T(8,128)}, u32[]{:S(2)}) copy-start(f32[16,256]{0,1:T(8,128)} %copy.54) | copy-start | bytes 49156
  81.6 1.9 copy-start.8
  83.5 1.9 copy-start.7
  85.4 1.9 copy-start.6
  87.3 1.9 copy-start.5
  89.3 2.2 %copy-start.1 = (f32[256,16,256]{0,1,2:T(8,128)S(1)}, f32[256,16,256]{0,1,2:T(8,128)}, u32[]{:S(2)}) copy-start(f32[256,16,256]{0,1,2:T(8,128)} %copy-done) | copy-start | bytes 12582916
  95.3 0.9 copy-start.10
  97.0 2.0 copy-start.2
  101.0 9.5 %copy-start.12 = (f32[16,256]{1,0:T(8,128)S(1)}, f32[16,256]{1,0:T(8,128)}, u32[]{:S(2)}) copy-start(f32[16,256]{1,0:T(8,128)} %param.7) | copy-start | bytes 49156
  101.0 49.7 %copy-start.13 = (f32[8,8,256]{2,1,0:T(8,128)S(1)}, f32[8,8,256]{2,1,0:T(8,128)}, u32[]{:S(2)}) copy-start(f32[8,8,256]{2,1,0:T(8,128)} %fusion.24) | copy-start | bytes 196612
  106.0 1.0 copy-start.4
  108.5 2.0 copy-start.3
  108.5 3.1 %collective-permute-start.1 = (bf16[1,2,256]{2,1,0:T(2,128)(2,1)S(1)}, bf16[1,2,256]{2,1,0:T(2,128)(2,1)S(1)}, u32[]{:S(2)}, u32[]{:S(2)}) collective-permute-start(bf16[1,2,256]{2,1,0:T(2,128)(2,1)S(1)} %slice.137), channel_id=1, source_target_pairs={{0,16},{16,32},{32,48},{48,64},{64,80},{80,96},{96,112},{112,128},... | collective-permute-start | bytes 3080 | tf_op jit(solution)/shard_map/ppermute | solution.py:14
  113.0 17.2 %collective-permute-start.2 = (f32[16,256]{1,0:T(8,128)S(1)}, f32[16,256]{1,0:T(8,128)S(1)}, u32[]{:S(2)}, u32[]{:S(2)}) collective-permute-start(f32[16,256]{1,0:T(8,128)S(1)} %bitcast_add_fusion.1), channel_id=1, source_target_pairs={{0,16},{16,32},{32,48},{48,64},{64,80},{80,96},{96,112},{112,128},... | collective-permute-start | bytes 49160 | tf_op jit(solution)/shard_map/ppermute | solution.py:14
  116.8 13.4 %collective-permute-start.3 = (f32[16,256]{1,0:T(8,128)S(1)}, f32[16,256]{1,0:T(8,128)S(1)}, u32[]{:S(2)}, u32[]{:S(2)}) collective-permute-start(f32[16,256]{1,0:T(8,128)S(1)} %bitcast_add_fusion.1), channel_id=1, source_target_pairs={{0,32},{16,48},{32,64},{48,80},{64,96},{80,112},{96,128},{112,144}... | collective-permute-start | bytes 49160 | tf_op jit(solution)/shard_map/ppermute | solution.py:14
  120.4 9.9 %collective-permute-start.4 = (f32[16,256]{1,0:T(8,128)S(1)}, f32[16,256]{1,0:T(8,128)S(1)}, u32[]{:S(2)}, u32[]{:S(2)}) collective-permute-start(f32[16,256]{1,0:T(8,128)S(1)} %bitcast_add_fusion.1), channel_id=1, source_target_pairs={{0,48},{16,64},{32,80},{48,96},{64,112},{80,128},{96,144},{112,160... | collective-permute-start | bytes 49160 | tf_op jit(solution)/shard_map/ppermute | solution.py:14
  125.3 5.8 %collective-permute-start.5 = (f32[16,256]{1,0:T(8,128)S(1)}, f32[16,256]{1,0:T(8,128)S(1)}, u32[]{:S(2)}, u32[]{:S(2)}) collective-permute-start(f32[16,256]{1,0:T(8,128)S(1)} %bitcast_add_fusion.1), channel_id=1, source_target_pairs={{0,64},{16,80},{32,96},{48,112},{64,128},{80,144},{96,160},{112,17... | collective-permute-start | bytes 49160 | tf_op jit(solution)/shard_map/ppermute | solution.py:14
  131.1 20.9 %collective-permute-start.6 = (f32[16,256]{1,0:T(8,128)S(1)}, f32[16,256]{1,0:T(8,128)S(1)}, u32[]{:S(2)}, u32[]{:S(2)}) collective-permute-start(f32[16,256]{1,0:T(8,128)S(1)} %multiply_add_fusion.10), channel_id=1, source_target_pairs={{0,64},{16,80},{32,96},{48,112},{64,128},{80,144},{96,160},{112,17... | collective-permute-start | bytes 49160 | tf_op jit(solution)/shard_map/ppermute | solution.py:14
  137.2 14.8 %collective-permute-start.7 = (f32[16,256]{1,0:T(8,128)S(1)}, f32[16,256]{1,0:T(8,128)S(1)}, u32[]{:S(2)}, u32[]{:S(2)}) collective-permute-start(f32[16,256]{1,0:T(8,128)S(1)} %multiply_add_fusion.10), channel_id=1, source_target_pairs={{0,128},{16,144},{32,160},{48,176},{64,192},{80,208},{96,224},{112... | collective-permute-start | bytes 49160 | tf_op jit(solution)/shard_map/ppermute | solution.py:14
  144.0 8.0 %collective-permute-start.8 = (f32[16,256]{1,0:T(8,128)S(1)}, f32[16,256]{1,0:T(8,128)}, u32[]{:S(2)}, u32[]{:S(2)}) collective-permute-start(f32[16,256]{1,0:T(8,128)S(1)} %multiply_add_fusion.10), channel_id=1, source_target_pairs={{0,192},{16,208},{32,224},{48,240},{64,256},{80,272},{96,288},{112... | collective-permute-start | bytes 49160 | tf_op jit(solution)/shard_map/ppermute | solution.py:14
  152.0 13.5 %copy-start.18 = (f32[8]{0:T(128)S(1)}, f32[8]{0:T(128)}, u32[]{:S(2)}) copy-start(f32[8]{0:T(128)} %broadcast_add_fusion) | copy-start | bytes 100
  152.7 12.6 %collective-permute-start.9 = (f32[16,256]{1,0:T(8,128)S(1)}, f32[16,256]{1,0:T(8,128)S(1)}, u32[]{:S(2)}, u32[]{:S(2)}) collective-permute-start(f32[16,256]{1,0:T(8,128)S(1)} %multiply_add_fusion.9), channel_id=1, source_target_pairs={{0,256},{16,272},{32,288},{48,304},{64,320},{80,336},{96,352},{112... | collective-permute-start | bytes 49160 | tf_op jit(solution)/shard_map/ppermute | solution.py:14
  172.0 3.1 %copy-start.16 = (f32[256]{0:T(256)S(1)}, f32[256]{0:T(256)}, u32[]{:S(2)}) copy-start(f32[256]{0:T(256)} %param.9) | copy-start | bytes 3076
  172.0 5.0 %copy-start.15 = (f32[1,1,256]{2,1,0:T(1,128)S(1)}, f32[1,1,256]{2,1,0:T(1,128)}, u32[]{:S(2)}) copy-start(f32[1,1,256]{2,1,0:T(1,128)} %get-tuple-element.21) | copy-start | bytes 3076

commit v12 on v6

--- a/solution.py
+++ b/solution.py
@@ -5,7 +5,7 @@
 from jax import lax
 from jax.sharding import PartitionSpec as P
 
-block_len = 64
+block_len = 16
 
 
 def from_behind(block, axis, distance):
@@ -64,12 +64,13 @@
     end_state = jnp.exp(-decay_rate * float(block)) * starts[count - 1] + local_end[count - 1]
     end_state, passenger = lax.optimization_barrier((end_state, passenger))
     sections = lax.axis_size("seq")
+    gathered = lax.all_gather(end_state, "seq")
     here = lax.axis_index("seq")
-    later = jnp.arange(sections)
-    lag = jnp.maximum(later - 1 - here, 0).astype(jnp.float32)
+    earlier = jnp.arange(sections)
+    lag = jnp.maximum(here - 1 - earlier, 0).astype(jnp.float32)
     weight = jnp.exp(-decay_rate[None, :, :] * (section * lag)[:, None, None])
-    weight = jnp.where((later > here)[:, None, None], weight, 0.0)
-    incoming = lax.psum_scatter(weight * end_state[None], "seq", scatter_dimension=0, tiled=True)[0]
+    weight = jnp.where((earlier < here)[:, None, None], weight, 0.0)
+    incoming = jnp.sum(weight * gathered, axis=0)
     inner = jnp.einsum("ijc,kjc->kic", toeplitz, pieces, precision=lax.Precision.HIGHEST)
     block_starts = (jnp.arange(count).astype(jnp.float32) * block)[:, None, None]
     starts = starts + jnp.exp(-decay_rate[None, :, :] * block_starts) * incoming[None, :, :]

time: 279 us -> 192 us (0.69)
  waiting for transfers between devices: 111 us -> 19.8 us
  blocking collectives: 19.7 us -> 61 us
  matrix products: 31.6 us -> 12.5 us
  between operations: 13.7 us -> 0.5 us
    reduce_scatter x1 -> x0, waiting for transfers between devices: 90.6 us -> none  [long_part(): lax.psum_scatter(weight * end_state[None], 'seq', scatter_dimension=0, ti...]
    all_gather x0 -> x1, blocking collectives: none -> 38.1 us  [long_part(): gathered = lax.all_gather(end_state, 'seq')]
    dot_general x1, matrix products: 12.4 us -> 5.44 us  [long_part(): jnp.einsum('nic,knc->kic', reading, starts, precision=lax.Precision.HIGHEST)]
    optimization_barrier x1, local copies, waits for them, and re-layouts: 9.44 us -> 2.5 us  [local(): lax.optimization_barrier((keys_values, features[0], toeplitz))]
    dot_general x1, matrix products: 10.3 us -> 4.04 us  [long_part(): jnp.einsum('ijc,kjc->kic', toeplitz, pieces, precision=lax.Precision.HIGH...]
    dot_general x1, matrix products: 3.86 us -> 0.31 us  [modal_tables(): jnp.dot(one_hot.reshape(block * block, block), kernel, precision=lax.Prec...]
    slice x2, local copies, waits for them, and re-layouts: 1.64 us -> 5.09 us  [long_part(): starts[count - 1]]
    exp x0 -> x1, local copies, waits for them, and re-layouts: none -> 3.41 us  [modal_tables(): jnp.exp(-decay_rate[:, None, :] * (block - 1.0 - positions)[None, :, None])]
  transfers between devices with their start and end apart: 5 -> 4, of which waited for: 4 -> 2; matrix products, arithmetic and copies ran while one was open for 16% -> 24% of each run, Pallas kernels for 0% -> 0%
where the time goes in v12:
time: 192 us; the launch traced here: 191 us
  blocking collectives  61 us (32%)
  local copies, waits for them, and re-layouts  51.5 us (27%)
  starting transfers between devices  25 us (13%)
  other arithmetic  21.2 us (11%)
  waiting for transfers between devices  19.8 us (10%)
  matrix products  12.5 us (7%)
    all_gather x1, blocking collectives, long_part(): gathered = lax.all_gather(end_state, 'seq')  38.1 us
    all_to_all x1, blocking collectives, local(): lax.all_to_all(gated, 'chan', split_axis=0, concat_axis=1, tiled=True)  22.9 us
    all_to_all x1, waiting for transfers between devices, arrive(): lax.all_to_all(streams, 'chan', split_axis=2, concat_axis=1, tiled=True)  18.8 us
    ppermute x2, starting transfers between devices, from_behind(): return lax.ppermute(block, axis, route)  12.8 us
    add x7, other arithmetic, long_part(): starts + jnp.exp(-decay_rate * float(block * step)) * shifted(starts, step)  10.6 us
    all_to_all x1, starting transfers between devices, arrive(): lax.all_to_all(streams, 'chan', split_axis=2, concat_axis=1, tiled=True)  7.7 us
    unnamed x66, local copies, waits for them, and re-layouts  7.51 us
    dot_general x1, matrix products, long_part(): jnp.einsum('nic,knc->kic', reading, starts, precision=lax.Precision.HIGHEST)  5.44 us
  transfers between devices with their start and end apart: 4, of which 2 were waited for; matrix products, arithmetic and copies ran while one was open for 24% of the time, Pallas kernels for 0%

profile of v12, /device:TPU:1, one launch (start us, length us, event | category | flops | bytes accessed | tf_op | source)
XLA Modules:
  0.0 191.5 jit_solution(17607341510637734510)
XLA Ops:
  0.0 1.6 slice-done
  1.6 3.8 %copy.104 = bf16[2,128,4096]{1,0,2:T(2,128)(2,1)} copy(bf16[2,128,4096]{2,1,0:T(8,128)(2,1)S(1)} %slice-done) | data formatting | bytes 4194304
  5.4 7.7 %all-to-all-start = ((bf16[2,128,4096]{1,0,2:T(2,128)(2,1)}), bf16[2,128,4096]{1,0,2:T(2,128)(2,1)S(1)}, u32[]{:S(2)}, u32[]{:S(2)}) async-start(bf16[2,128,4096]{1,0,2:T(2,128)(2,1)} %copy.104), calls=%async_computation | async-start | bytes 4194304 | tf_op jit(solution)/shard_map/all_to_all | solution.py:90
  14.2 1.4 constant_dynamic-slice_fusion.2
  15.7 1.4 constant_dynamic-slice_fusion.1
  18.3 1.0 exponential_multiply_fusion
  19.6 18.8 %all-to-all-done = bf16[2,128,4096]{1,0,2:T(2,128)(2,1)S(1)} async-done(((bf16[2,128,4096]{1,0,2:T(2,128)(2,1)}), bf16[2,128,4096]{1,0,2:T(2,128)(2,1)S(1)}, u32[]{:S(2)}, u32[]{:S(2)}) %all-to-all-start) | async-done | bytes 2097184 | tf_op jit(solution)/shard_map/all_to_all | solution.py:90
  38.4 1.6 copy.73
  40.0 2.9 %copy.74 = bf16[2,16,128,256]{3,2,1,0:T(8,128)(2,1)S(1)} copy(bf16[2,16,128,256]{2,3,1,0:T(8,128)(2,1)} %bitcast.71) | data formatting | bytes 4194304 | tf_op jit(solution)/shard_map/all_to_all | solution.py:90
  43.5 10.9 %collective-permute-start = (bf16[2,2,256]{2,1,0:T(2,128)(2,1)}, bf16[2,2,256]{2,1,0:T(2,128)(2,1)}, u32[]{:S(2)}, u32[]{:S(2)}) collective-permute-start(bf16[2,2,256]{2,1,0:T(2,128)(2,1)} %slice.120), channel_id=1, source_target_pairs={{0,16},{16,32},{32,48},{48,64},{64,80},{80,96},{96,112},{112,128},... | collective-permute-start | bytes 6152 | tf_op jit(solution)/shard_map/ppermute | solution.py:14
  55.0 1.3 copy.105
  57.1 3.4 %copy.81 = f32[16,16,256]{1,0,2:T(8,128)} copy(f32[16,16,256]{2,1,0:T(8,128)} %get-tuple-element.36) | data formatting | bytes 524288 | tf_op jit(solution)/shard_map/exp | solution.py:39
  61.2 0.8 copy.83
  63.5 0.8 copy.86
  64.3 0.8 copy.87
  65.0 0.8 copy.88
  65.8 2.5 %copy.94 = f32[16,16,256]{0,1,2:T(8,128)} copy(f32[16,16,256]{2,1,0:T(8,128)S(1)} %copy-done.3) | data formatting | bytes 524288 | tf_op jit(solution)/shard_map/mul | solution.py:40
  68.3 1.2 pad_maximum_fusion
  69.5 1.4 add_convert_fusion
  71.3 1.0 copy-done
  72.2 1.6 copy.78
  73.9 2.7 %convolution_bitcast_fusion = f32[128,16,256]{0,1,2:T(8,128)S(1)} fusion(bf16[128,16,256]{0,1,2:T(8,128)(2,1)S(1)} %copy.78, f32[16,16,256]{1,0,2:T(8,128)} %copy.81), kind=kOutput, calls=%fused_computation.22 | convolution fusion | flops 100663296 | bytes 3407872 | tf_op jit(solution)/shard_map/njc,kjc->knc/dot_general | solution.py:58
  76.6 1.9 %slice.131 = f32[1,16,256]{0,1,2:T(8,128)} slice(f32[128,16,256]{0,1,2:T(8,128)S(1)} %convolution_bitcast_fusion), slice={[127:128], [0:16], [0:256]} | slice | bytes 32768 | tf_op jit(solution)/shard_map/slice | solution.py:64
  78.5 2.0 %pad_slice_fusion = f32[127,16,256]{0,1,2:T(8,128)} fusion(f32[127,16,256]{0,1,2:T(8,128)S(1)} %bitcast.60), kind=kLoop, calls=%fused_computation.21 | loop fusion | bytes 4161536 | tf_op jit(solution)/shard_map/slice | solution.py:48
  80.5 4.5 %all-to-all-start.1 = ((bf16[128,16,256]{0,2,1:T(8,128)(2,1)}), bf16[128,16,256]{0,2,1:T(8,128)(2,1)}, u32[]{:S(2)}, u32[]{:S(2)}) async-start(bf16[128,16,256]{0,2,1:T(8,128)(2,1)} %bitcast.74), calls=%async_computation.1 | async-start | bytes 2097152 | tf_op jit(solution)/shard_map/all_to_all | solution.py:99
  85.1 3.1 %multiply_add_fusion.6 = f32[128,16,256]{0,1,2:T(8,128)S(1)} fusion(f32[127,16,256]{0,1,2:T(8,128)} %pad_slice_fusion, f32[127,16,256]{0,1,2:T(8,128)S(1)} %bitcast.61, f32[16,256]{0,1:T(8,128)} %copy.82), kind=kLoop, calls=%fused_computation.19 | loop fusion | flops 1048576 | bytes 6275072 | tf_op jit(solution)/shard_map/add | solution.py:62
  88.1 1.3 multiply_add_fusion.5
  89.4 1.3 multiply_add_fusion.4
  90.7 1.3 multiply_add_fusion.3
  92.0 1.3 multiply_add_fusion.2
  93.3 1.3 multiply_add_fusion.1
  94.5 1.3 multiply_add_fusion
  95.8 2.0 %slice.130 = f32[1,16,256]{0,1,2:T(8,128)} slice(f32[128,16,256]{0,1,2:T(8,128)S(1)} %multiply_add_fusion), slice={[127:128], [0:16], [0:256]} | slice | bytes 32768 | tf_op jit(solution)/shard_map/slice | solution.py:64
  97.8 3.1 %copy.90 = f32[1,16,256]{2,1,0:T(8,128)} copy(f32[1,16,256]{0,1,2:T(8,128)} %slice.130) | data formatting | bytes 32768 | tf_op jit(solution)/shard_map/slice | solution.py:64
  100.9 3.1 %copy.91 = f32[1,16,256]{2,1,0:T(8,128)} copy(f32[1,16,256]{0,1,2:T(8,128)} %slice.131) | data formatting | bytes 32768 | tf_op jit(solution)/shard_map/slice | solution.py:64
  104.0 2.5 %copy.79 = f32[16,16,256]{1,0,2:T(8,128)} copy(f32[16,16,256]{2,1,0:T(8,128)S(1)} %fusion.14) | data formatting | bytes 524288 | tf_op jit(solution)/shard_map/optimization_barrier | solution.py:98
  106.5 4.0 %fusion.17 = f32[256,128,16]{1,2,0:T(8,128)} fusion(bf16[128,16,256]{0,1,2:T(8,128)(2,1)S(1)} %copy.78, f32[16,16,256]{1,0,2:T(8,128)} %copy.79), kind=kOutput, calls=%fused_computation.61 | convolution fusion | flops 100663296 | bytes 3407872 | tf_op jit(solution)/shard_map/ijc,kjc->kic/dot_general | solution.py:74
  110.6 1.5 copy.92
  112.1 1.9 %collective-permute-start.1 = (bf16[1,2,256]{2,1,0:T(2,128)(2,1)S(1)}, bf16[1,2,256]{2,1,0:T(2,128)(2,1)S(1)}, u32[]{:S(2)}, u32[]{:S(2)}) collective-permute-start(bf16[1,2,256]{2,1,0:T(2,128)(2,1)S(1)} %slice.132), channel_id=1, source_target_pairs={{0,16},{16,32},{32,48},{48,64},{64,80},{80,96},{96,112},{112,128},... | collective-permute-start | bytes 3080 | tf_op jit(solution)/shard_map/ppermute | solution.py:14
  114.1 1.1 collective-permute-done.1
  115.2 1.5 pad_maximum_fusion.1
  116.6 38.1 %all-gather = f32[512,256]{1,0:T(8,128)S(1)} all-gather(f32[16,256]{1,0:T(8,128)S(1)} %bitcast_add_fusion.1), channel_id=2, replica_groups=mesh['seq'=32,'chan'=16] {'seq'}, dimensions={0}, use_global_device_ids=true | all-gather | bytes 540672 | tf_op jit(solution)/shard_map/all_gather | solution.py:67
  155.0 5.4 %add_bitcast_fusion = f32[128,16,256]{0,1,2:T(8,128)} fusion(f32[256,128,16]{1,2,0:T(8,128)} %fusion.17, f32[16,16,256]{0,1,2:T(8,128)} %copy.94, f32[128,16,256]{0,1,2:T(8,128)S(1)} %multiply_add_fusion, f32[16,256]{0,1:T(8,128)S(1)} %copy.93, f32[128]{0:T(128)S(1)} %copy-done.28, f32[16,256]{0,1:T(8,128)S(1)} %copy.89), kind=kOutput, calls=%fused_computation.7 | convolution fusion | flops 102760448 | bytes 6586880 | tf_op jit(solution)/shard_map/nic,knc->kic/dot_general | solution.py:77
  160.4 3.3 %copy.95 = f32[128,16,256]{2,1,0:T(8,128)} copy(f32[128,16,256]{0,1,2:T(8,128)} %add_bitcast_fusion) | data formatting | bytes 4194304 | tf_op jit(solution)/shard_map/add | solution.py:78
  163.8 1.8 fusion.1
  165.6 0.9 fusion
  166.5 22.9 %all_to_all.53 = bf16[16,128,256]{2,1,0:T(8,128)(2,1)S(1)} all-to-all(bf16[16,128,256]{2,1,0:T(8,128)(2,1)S(1)} %bitcast.77), channel_id=1, replica_groups=mesh['seq'=32,'chan'=16] {'chan'}, dimensions={0} | all-to-all | bytes 2097152 | tf_op jit(solution)/shard_map/all_to_all | solution.py:113
  190.1 1.3 copy.97
  (87 shorter events, 8.3 us)
Async XLA Ops:
  0.0 1.6 slice-start
  5.4 12.3 %copy-start.19 = (f32[16,256]{1,0:T(8,128)S(1)}, f32[16,256]{1,0:T(8,128)}, u32[]{:S(2)}) copy-start(f32[16,256]{1,0:T(8,128)} %param.7) | copy-start | bytes 49156
  5.4 12.3 %copy-start.21 = (f32[16,256]{1,0:T(8,128)S(1)}, f32[16,256]{1,0:T(8,128)}, u32[]{:S(2)}) copy-start(f32[16,256]{1,0:T(8,128)} %param.8) | copy-start | bytes 49156
  5.4 33.0 %all-to-all-start = ((bf16[2,128,4096]{1,0,2:T(2,128)(2,1)}), bf16[2,128,4096]{1,0,2:T(2,128)(2,1)S(1)}, u32[]{:S(2)}, u32[]{:S(2)}) async-start(bf16[2,128,4096]{1,0,2:T(2,128)(2,1)} %copy.104), calls=%async_computation | async-start | bytes 4194304 | tf_op jit(solution)/shard_map/all_to_all | solution.py:90
  42.9 12.1 %slice-start.1 = ((bf16[3,128,4096]{2,1,0:T(8,128)(2,1)}), bf16[1,128,4096]{2,1,0:T(8,128)(2,1)S(1)}, s32[]{:S(2)}) async-start(bf16[3,128,4096]{2,1,0:T(8,128)(2,1)} %param.5), calls=%async_computation.4 | async-start | bytes 2097152 | tf_op jit(solution)/shard_map/slice | solution.py:98
  43.5 24.8 %collective-permute-start = (bf16[2,2,256]{2,1,0:T(2,128)(2,1)}, bf16[2,2,256]{2,1,0:T(2,128)(2,1)}, u32[]{:S(2)}, u32[]{:S(2)}) collective-permute-start(bf16[2,2,256]{2,1,0:T(2,128)(2,1)} %slice.120), channel_id=1, source_target_pairs={{0,16},{16,32},{32,48},{48,64},{64,80},{80,96},{96,112},{112,128},... | collective-permute-start | bytes 6152 | tf_op jit(solution)/shard_map/ppermute | solution.py:14
  56.3 4.2 %copy-start.18 = (f32[16,256]{1,0:T(8,128)S(1)}, f32[16,256]{1,0:T(8,128)}, u32[]{:S(2)}) copy-start(f32[16,256]{1,0:T(8,128)} %get-tuple-element.28) | copy-start | bytes 49156
  56.3 5.0 %copy-start.17 = (f32[16,256]{1,0:T(8,128)S(1)}, f32[16,256]{1,0:T(8,128)}, u32[]{:S(2)}) copy-start(f32[16,256]{1,0:T(8,128)} %get-tuple-element.29) | copy-start | bytes 49156
  56.3 5.7 %copy-start.16 = (f32[16,256]{1,0:T(8,128)S(1)}, f32[16,256]{1,0:T(8,128)}, u32[]{:S(2)}) copy-start(f32[16,256]{1,0:T(8,128)} %get-tuple-element.30) | copy-start | bytes 49156
  56.3 6.5 %copy-start.15 = (f32[16,256]{1,0:T(8,128)S(1)}, f32[16,256]{1,0:T(8,128)}, u32[]{:S(2)}) copy-start(f32[16,256]{1,0:T(8,128)} %get-tuple-element.31) | copy-start | bytes 49156
  56.3 7.2 %copy-start.14 = (f32[16,256]{1,0:T(8,128)S(1)}, f32[16,256]{1,0:T(8,128)}, u32[]{:S(2)}) copy-start(f32[16,256]{1,0:T(8,128)} %get-tuple-element.32) | copy-start | bytes 49156
  56.3 8.0 %copy-start.13 = (f32[16,256]{1,0:T(8,128)S(1)}, f32[16,256]{1,0:T(8,128)}, u32[]{:S(2)}) copy-start(f32[16,256]{1,0:T(8,128)} %get-tuple-element.33) | copy-start | bytes 49156
  56.3 8.7 %copy-start.12 = (f32[16,256]{1,0:T(8,128)S(1)}, f32[16,256]{1,0:T(8,128)}, u32[]{:S(2)}) copy-start(f32[16,256]{1,0:T(8,128)} %get-tuple-element.27) | copy-start | bytes 49156
  56.3 9.5 %copy-start.3 = (f32[16,16,256]{2,1,0:T(8,128)S(1)}, f32[16,16,256]{2,1,0:T(8,128)}, u32[]{:S(2)}) copy-start(f32[16,16,256]{2,1,0:T(8,128)} %get-tuple-element.25) | copy-start | bytes 786436
  68.3 1.2 copy-start.22
  68.3 1.2 copy-start.23
  71.3 1.0 copy-start
  80.5 30.0 %all-to-all-start.1 = ((bf16[128,16,256]{0,2,1:T(8,128)(2,1)}), bf16[128,16,256]{0,2,1:T(8,128)(2,1)}, u32[]{:S(2)}, u32[]{:S(2)}) async-start(bf16[128,16,256]{0,2,1:T(8,128)(2,1)} %bitcast.74), calls=%async_computation.1 | async-start | bytes 2097152 | tf_op jit(solution)/shard_map/all_to_all | solution.py:99
  85.0 3.1 %copy-start.9 = (f32[16,256]{0,1:T(8,128)S(1)}, f32[16,256]{0,1:T(8,128)}, u32[]{:S(2)}) copy-start(f32[16,256]{0,1:T(8,128)} %copy.83) | copy-start | bytes 49156
  88.1 1.3 copy-start.8
  89.4 1.3 copy-start.7
  90.7 1.3 copy-start.6
  92.0 1.3 copy-start.4
  93.3 1.3 copy-start.5
  110.5 3.5 %copy-start.10 = (f32[1,16,256]{2,1,0:T(8,128)S(1)}, f32[1,16,256]{2,1,0:T(8,128)}, u32[]{:S(2)}) copy-start(f32[1,16,256]{2,1,0:T(8,128)} %copy.90) | copy-start | bytes 49156
  110.5 3.5 %copy-start.11 = (f32[1,16,256]{2,1,0:T(8,128)S(1)}, f32[1,16,256]{2,1,0:T(8,128)}, u32[]{:S(2)}) copy-start(f32[1,16,256]{2,1,0:T(8,128)} %copy.91) | copy-start | bytes 49156
  110.5 3.5 %copy-start.20 = (f32[16,256]{1,0:T(8,128)S(1)}, f32[16,256]{1,0:T(8,128)}, u32[]{:S(2)}) copy-start(f32[16,256]{1,0:T(8,128)} %param.7) | copy-start | bytes 49156
  110.5 44.2 %copy-start.29 = (pred[32]{0:T(512)(128)(4,1)S(1)}, pred[32]{0:T(512)(128)(4,1)}, u32[]{:S(2)}) copy-start(pred[32]{0:T(512)(128)(4,1)} %iota_compare_fusion.2) | copy-start | bytes 100
  110.6 44.1 %copy-start.30 = (f32[32]{0:T(128)S(1)}, f32[32]{0:T(128)}, u32[]{:S(2)}) copy-start(f32[32]{0:T(128)} %convert_multiply_fusion.1) | copy-start | bytes 388
  112.1 2.0 %copy-start.2 = (bf16[16,128,256]{2,1,0:T(8,128)(2,1)}, bf16[16,128,256]{2,1,0:T(8,128)(2,1)S(1)}, u32[]{:S(2)}) copy-start(bf16[16,128,256]{2,1,0:T(8,128)(2,1)S(1)} %copy.92) | copy-start | bytes 3145732
  112.1 42.9 %copy-start.28 = (f32[128]{0:T(128)S(1)}, f32[128]{0:T(128)}, u32[]{:S(2)}) copy-start(f32[128]{0:T(128)} %convert_multiply_fusion.2) | copy-start | bytes 1540
  112.1 3.1 %collective-permute-start.1 = (bf16[1,2,256]{2,1,0:T(2,128)(2,1)S(1)}, bf16[1,2,256]{2,1,0:T(2,128)(2,1)S(1)}, u32[]{:S(2)}, u32[]{:S(2)}) collective-permute-start(bf16[1,2,256]{2,1,0:T(2,128)(2,1)S(1)} %slice.132), channel_id=1, source_target_pairs={{0,16},{16,32},{32,48},{48,64},{64,80},{80,96},{96,112},{112,128},... | collective-permute-start | bytes 3080 | tf_op jit(solution)/shard_map/ppermute | solution.py:14
  160.4 3.3 %copy-start.1 = (bf16[2048,256]{1,0:T(8,128)(2,1)S(1)}, bf16[2048,256]{1,0:T(8,128)(2,1)}, u32[]{:S(2)}) copy-start(bf16[2048,256]{1,0:T(8,128)(2,1)} %copy-done) | copy-start | bytes 3145732
  160.4 3.3 %copy-start.27 = (f32[256]{0:T(256)S(1)}, f32[256]{0:T(256)}, u32[]{:S(2)}) copy-start(f32[256]{0:T(256)} %param.9) | copy-start | bytes 3076
  163.7 1.9 copy-start.24
  163.7 1.9 copy-start.25
  163.8 1.9 copy-start.26

commit v13 on v12

--- a/solution.py
+++ b/solution.py
@@ -59,8 +59,13 @@
     starts = shifted(local_end, 1)
     step = 1
     while step < count:
-        starts = starts + jnp.exp(-decay_rate * float(block * step)) * shifted(starts, step)
-        step *= 2
+        total = starts
+        for multiple in range(1, 4):
+            if step * multiple < count:
+                weight = jnp.exp(-decay_rate * float(block * step * multiple))
+                total = total + weight * shifted(starts, step * multiple)
+        starts = total
+        step *= 4
     end_state = jnp.exp(-decay_rate * float(block)) * starts[count - 1] + local_end[count - 1]
     end_state, passenger = lax.optimization_barrier((end_state, passenger))
     sections = lax.axis_size("seq")

time: 192 us -> 202 us (1.052)
  local copies, waits for them, and re-layouts: 51.5 us -> 57.6 us
  other arithmetic: 21.2 us -> 25 us
    slice x1 -> x3, local copies, waits for them, and re-layouts: 1.99 us -> 5.93 us  [shifted(): values[:values.shape[0] - distance]]
    add x7 -> x4, other arithmetic: 10.6 us -> 14.3 us  [long_part(): total = total + weight * shifted(starts, step * multiple)]
    exp x7 -> x10, local copies, waits for them, and re-layouts: 5.26 us -> 7.44 us  [long_part(): weight = jnp.exp(-decay_rate * float(block * step * multiple))]
    unnamed x66 -> x74, local copies, waits for them, and re-layouts: 7.51 us -> 7.55 us
  transfers between devices with their start and end apart: 4 -> 4, of which waited for: 2 -> 2; matrix products, arithmetic and copies ran while one was open for 24% -> 26% of each run, Pallas kernels for 0% -> 0%
where the time goes in v13:
time: 202 us; the launch traced here: 201 us
  blocking collectives  60.8 us (30%)
  local copies, waits for them, and re-layouts  57.6 us (29%)
  starting transfers between devices  25 us (12%)
  other arithmetic  25 us (12%)
  waiting for transfers between devices  19.8 us (10%)
  matrix products  12.5 us (6%)
    all_gather x1, blocking collectives, long_part(): gathered = lax.all_gather(end_state, 'seq')  37.8 us
    all_to_all x1, blocking collectives, local(): lax.all_to_all(gated, 'chan', split_axis=0, concat_axis=1, tiled=True)  22.9 us
    all_to_all x1, waiting for transfers between devices, arrive(): lax.all_to_all(streams, 'chan', split_axis=2, concat_axis=1, tiled=True)  18.7 us
    add x4, other arithmetic, long_part(): total = total + weight * shifted(starts, step * multiple)  14.3 us
    ppermute x2, starting transfers between devices, from_behind(): return lax.ppermute(block, axis, route)  12.8 us
    all_to_all x1, starting transfers between devices, arrive(): lax.all_to_all(streams, 'chan', split_axis=2, concat_axis=1, tiled=True)  7.7 us
    unnamed x74, local copies, waits for them, and re-layouts  7.55 us
    exp x10, local copies, waits for them, and re-layouts, long_part(): weight = jnp.exp(-decay_rate * float(block * step * multiple))  7.44 us
  transfers between devices with their start and end apart: 4, of which 2 were waited for; matrix products, arithmetic and copies ran while one was open for 26% of the time, Pallas kernels for 0%

profile of v13, /device:TPU:1, one launch (start us, length us, event | category | flops | bytes accessed | tf_op | source)
XLA Modules:
  0.0 201.1 jit_solution(6442244589734006608)
XLA Ops:
  0.0 1.6 slice-done
  1.6 3.8 %copy.113 = bf16[2,128,4096]{1,0,2:T(2,128)(2,1)} copy(bf16[2,128,4096]{2,1,0:T(8,128)(2,1)S(1)} %slice-done) | data formatting | bytes 4194304
  5.4 7.7 %all-to-all-start = ((bf16[2,128,4096]{1,0,2:T(2,128)(2,1)}), bf16[2,128,4096]{1,0,2:T(2,128)(2,1)S(1)}, u32[]{:S(2)}, u32[]{:S(2)}) async-start(bf16[2,128,4096]{1,0,2:T(2,128)(2,1)} %copy.113), calls=%async_computation | async-start | bytes 4194304 | tf_op jit(solution)/shard_map/all_to_all | solution.py:95
  14.2 1.4 constant_dynamic-slice_fusion.2
  15.7 1.4 constant_dynamic-slice_fusion.1
  18.4 1.0 exponential_multiply_fusion
  19.7 18.7 %all-to-all-done = bf16[2,128,4096]{1,0,2:T(2,128)(2,1)S(1)} async-done(((bf16[2,128,4096]{1,0,2:T(2,128)(2,1)}), bf16[2,128,4096]{1,0,2:T(2,128)(2,1)S(1)}, u32[]{:S(2)}, u32[]{:S(2)}) %all-to-all-start) | async-done | bytes 2097184 | tf_op jit(solution)/shard_map/all_to_all | solution.py:95
  38.4 1.6 copy.79
  40.0 2.9 %copy.80 = bf16[2,16,128,256]{3,2,1,0:T(8,128)(2,1)S(1)} copy(bf16[2,16,128,256]{2,3,1,0:T(8,128)(2,1)} %bitcast.75) | data formatting | bytes 4194304 | tf_op jit(solution)/shard_map/all_to_all | solution.py:95
  43.4 10.9 %collective-permute-start = (bf16[2,2,256]{2,1,0:T(2,128)(2,1)}, bf16[2,2,256]{2,1,0:T(2,128)(2,1)}, u32[]{:S(2)}, u32[]{:S(2)}) collective-permute-start(bf16[2,2,256]{2,1,0:T(2,128)(2,1)} %slice.132), channel_id=1, source_target_pairs={{0,16},{16,32},{32,48},{48,64},{64,80},{80,96},{96,112},{112,128},... | collective-permute-start | bytes 6152 | tf_op jit(solution)/shard_map/ppermute | solution.py:14
  55.0 1.3 copy.114
  56.4 0.8 copy.118
  57.2 3.4 %copy.87 = f32[16,16,256]{1,0,2:T(8,128)} copy(f32[16,16,256]{2,1,0:T(8,128)} %get-tuple-element.39) | data formatting | bytes 524288 | tf_op jit(solution)/shard_map/exp | solution.py:39
  60.6 0.8 copy.88
  62.1 0.7 copy.90
  63.6 0.7 copy.92
  67.3 0.7 copy.97
  68.1 2.5 %copy.103 = f32[16,16,256]{0,1,2:T(8,128)} copy(f32[16,16,256]{2,1,0:T(8,128)S(1)} %copy-done.3) | data formatting | bytes 524288 | tf_op jit(solution)/shard_map/mul | solution.py:40
  70.6 1.1 pad_maximum_fusion
  71.8 1.4 add_convert_fusion
  73.5 1.0 copy-done
  74.5 1.6 copy.84
  76.1 2.7 %convolution_bitcast_fusion = f32[128,16,256]{0,1,2:T(8,128)S(1)} fusion(bf16[128,16,256]{0,1,2:T(8,128)(2,1)S(1)} %copy.84, f32[16,16,256]{1,0,2:T(8,128)} %copy.87), kind=kOutput, calls=%fused_computation.21 | convolution fusion | flops 100663296 | bytes 3407872 | tf_op jit(solution)/shard_map/njc,kjc->knc/dot_general | solution.py:58
  78.8 2.0 pad_slice_fusion
  80.8 2.0 pad_slice_fusion.1
  82.8 1.9 pad_slice_fusion.2
  84.7 1.9 slice.144
  86.7 4.5 %all-to-all-start.1 = ((bf16[128,16,256]{0,2,1:T(8,128)(2,1)}), bf16[128,16,256]{0,2,1:T(8,128)(2,1)}, u32[]{:S(2)}, u32[]{:S(2)}) async-start(bf16[128,16,256]{0,2,1:T(8,128)(2,1)} %bitcast.78), calls=%async_computation.1 | async-start | bytes 2097152 | tf_op jit(solution)/shard_map/all_to_all | solution.py:104
  91.2 6.0 %multiply_add_fusion.3 = f32[128,16,256]{0,1,2:T(8,128)S(1)} fusion(f32[125,16,256]{0,1,2:T(8,128)} %pad_slice_fusion, f32[126,16,256]{0,1,2:T(8,128)} %pad_slice_fusion.1, f32[127,16,256]{0,1,2:T(8,128)} %pad_slice_fusion.2, f32[127,16,256]{0,1,2:T(8,128)S(1)} %bitcast.64, f32[16,256]{0,1:T(8,128)} %copy.90, f32[16,256]{0,1:T(8,128)} %copy.89, ...), kind=kLoop, calls=%fused_computation.16 | loop fusion | flops 3145728 | bytes 10420224 | tf_op jit(solution)/shard_map/add | solution.py:66
  97.3 3.6 %multiply_add_fusion.2 = f32[128,16,256]{0,1,2:T(8,128)S(1)} fusion(f32[116,16,256]{0,1,2:T(8,128)S(1)} %bitcast.65, f32[120,16,256]{0,1,2:T(8,128)S(1)} %bitcast.66, f32[128,16,256]{0,1,2:T(8,128)S(1)} %multiply_add_fusion.3, f32[124,16,256]{0,1,2:T(8,128)S(1)} %bitcast.67, f32[16,256]{0,1:T(8,128)S(1)} %copy-done.7, f32[16,256]{0,1:T(8,128)S(1)} %copy-done.5, ...), kind=kLoop, calls=%fused_computation.15 | loop fusion | flops 3145728 | bytes 10141696 | tf_op jit(solution)/shard_map/add | solution.py:66
  100.9 3.6 %multiply_add_fusion.1 = f32[128,16,256]{0,1,2:T(8,128)S(1)} fusion(f32[80,16,256]{0,1,2:T(8,128)S(1)} %bitcast.68, f32[96,16,256]{0,1,2:T(8,128)S(1)} %bitcast.69, f32[128,16,256]{0,1,2:T(8,128)S(1)} %multiply_add_fusion.2, f32[112,16,256]{0,1,2:T(8,128)S(1)} %bitcast.70, f32[16,256]{0,1:T(8,128)S(1)} %copy-done.9, f32[16,256]{0,1:T(8,128)S(1)} %copy-done.8, ...), kind=kLoop, calls=%fused_computation.14 | loop fusion | flops 3145728 | bytes 8962048 | tf_op jit(solution)/shard_map/add | solution.py:66
  104.5 1.3 multiply_add_fusion
  105.7 2.0 slice.143
  107.7 3.1 %copy.99 = f32[1,16,256]{2,1,0:T(8,128)} copy(f32[1,16,256]{0,1,2:T(8,128)} %slice.143) | data formatting | bytes 32768 | tf_op jit(solution)/shard_map/slice | solution.py:69
  110.8 3.1 %copy.100 = f32[1,16,256]{2,1,0:T(8,128)} copy(f32[1,16,256]{0,1,2:T(8,128)} %slice.144) | data formatting | bytes 32768 | tf_op jit(solution)/shard_map/slice | solution.py:69
  113.9 2.5 %copy.85 = f32[16,16,256]{1,0,2:T(8,128)} copy(f32[16,16,256]{2,1,0:T(8,128)S(1)} %fusion.14) | data formatting | bytes 524288 | tf_op jit(solution)/shard_map/optimization_barrier | solution.py:103
  116.4 4.0 %fusion.17 = f32[256,128,16]{1,2,0:T(8,128)} fusion(bf16[128,16,256]{0,1,2:T(8,128)(2,1)S(1)} %copy.84, f32[16,16,256]{1,0,2:T(8,128)} %copy.85), kind=kOutput, calls=%fused_computation.63 | convolution fusion | flops 100663296 | bytes 3407872 | tf_op jit(solution)/shard_map/ijc,kjc->kic/dot_general | solution.py:79
  120.5 1.5 copy.101
  122.0 1.9 collective-permute-start.1
  124.0 1.1 collective-permute-done.1
  125.1 1.5 pad_maximum_fusion.1
  126.6 37.8 %all-gather = f32[512,256]{1,0:T(8,128)S(1)} all-gather(f32[16,256]{1,0:T(8,128)S(1)} %bitcast_add_fusion.1), channel_id=2, replica_groups=mesh['seq'=32,'chan'=16] {'seq'}, dimensions={0}, use_global_device_ids=true | all-gather | bytes 540672 | tf_op jit(solution)/shard_map/all_gather | solution.py:72
  164.7 5.4 %add_bitcast_fusion = f32[128,16,256]{0,1,2:T(8,128)} fusion(f32[256,128,16]{1,2,0:T(8,128)} %fusion.17, f32[16,16,256]{0,1,2:T(8,128)} %copy.103, f32[128,16,256]{0,1,2:T(8,128)S(1)} %multiply_add_fusion, f32[16,256]{0,1:T(8,128)S(1)} %copy.102, f32[128]{0:T(128)S(1)} %copy-done.32, f32[16,256]{0,1:T(8,128)S(1)} %copy.98), kind=kOutput, calls=%fused_computation.7 | convolution fusion | flops 102760448 | bytes 6586880 | tf_op jit(solution)/shard_map/nic,knc->kic/dot_general | solution.py:82
  170.1 3.3 %copy.104 = f32[128,16,256]{2,1,0:T(8,128)} copy(f32[128,16,256]{0,1,2:T(8,128)} %add_bitcast_fusion) | data formatting | bytes 4194304 | tf_op jit(solution)/shard_map/add | solution.py:83
  173.5 1.8 fusion.1
  175.3 0.9 fusion
  176.2 22.9 %all_to_all.53 = bf16[16,128,256]{2,1,0:T(8,128)(2,1)S(1)} all-to-all(bf16[16,128,256]{2,1,0:T(8,128)(2,1)S(1)} %bitcast.81), channel_id=1, replica_groups=mesh['seq'=32,'chan'=16] {'chan'}, dimensions={0} | all-to-all | bytes 2097152 | tf_op jit(solution)/shard_map/all_to_all | solution.py:118
  199.8 1.3 copy.106
  (97 shorter events, 9.8 us)
Async XLA Ops:
  0.0 1.6 slice-start
  5.4 12.3 %copy-start.23 = (f32[16,256]{1,0:T(8,128)S(1)}, f32[16,256]{1,0:T(8,128)}, u32[]{:S(2)}) copy-start(f32[16,256]{1,0:T(8,128)} %param.7) | copy-start | bytes 49156
  5.4 12.3 %copy-start.25 = (f32[16,256]{1,0:T(8,128)S(1)}, f32[16,256]{1,0:T(8,128)}, u32[]{:S(2)}) copy-start(f32[16,256]{1,0:T(8,128)} %param.8) | copy-start | bytes 49156
  5.4 33.0 %all-to-all-start = ((bf16[2,128,4096]{1,0,2:T(2,128)(2,1)}), bf16[2,128,4096]{1,0,2:T(2,128)(2,1)S(1)}, u32[]{:S(2)}, u32[]{:S(2)}) async-start(bf16[2,128,4096]{1,0,2:T(2,128)(2,1)} %copy.113), calls=%async_computation | async-start | bytes 4194304 | tf_op jit(solution)/shard_map/all_to_all | solution.py:95
  42.9 12.1 %slice-start.1 = ((bf16[3,128,4096]{2,1,0:T(8,128)(2,1)}), bf16[1,128,4096]{2,1,0:T(8,128)(2,1)S(1)}, s32[]{:S(2)}) async-start(bf16[3,128,4096]{2,1,0:T(8,128)(2,1)} %param.5), calls=%async_computation.4 | async-start | bytes 2097152 | tf_op jit(solution)/shard_map/slice | solution.py:103
  43.4 27.1 %collective-permute-start = (bf16[2,2,256]{2,1,0:T(2,128)(2,1)}, bf16[2,2,256]{2,1,0:T(2,128)(2,1)}, u32[]{:S(2)}, u32[]{:S(2)}) collective-permute-start(bf16[2,2,256]{2,1,0:T(2,128)(2,1)} %slice.132), channel_id=1, source_target_pairs={{0,16},{16,32},{32,48},{48,64},{64,80},{80,96},{96,112},{112,128},... | collective-permute-start | bytes 6152 | tf_op jit(solution)/shard_map/ppermute | solution.py:14
  56.3 4.2 %copy-start.22 = (f32[16,256]{1,0:T(8,128)S(1)}, f32[16,256]{1,0:T(8,128)}, u32[]{:S(2)}) copy-start(f32[16,256]{1,0:T(8,128)} %get-tuple-element.28) | copy-start | bytes 49156
  56.3 5.0 %copy-start.21 = (f32[16,256]{1,0:T(8,128)S(1)}, f32[16,256]{1,0:T(8,128)}, u32[]{:S(2)}) copy-start(f32[16,256]{1,0:T(8,128)} %get-tuple-element.29) | copy-start | bytes 49156
  56.3 5.7 %copy-start.20 = (f32[16,256]{1,0:T(8,128)S(1)}, f32[16,256]{1,0:T(8,128)}, u32[]{:S(2)}) copy-start(f32[16,256]{1,0:T(8,128)} %get-tuple-element.30) | copy-start | bytes 49156
  56.3 6.5 %copy-start.19 = (f32[16,256]{1,0:T(8,128)S(1)}, f32[16,256]{1,0:T(8,128)}, u32[]{:S(2)}) copy-start(f32[16,256]{1,0:T(8,128)} %get-tuple-element.31) | copy-start | bytes 49156
  56.3 7.2 %copy-start.18 = (f32[16,256]{1,0:T(8,128)S(1)}, f32[16,256]{1,0:T(8,128)}, u32[]{:S(2)}) copy-start(f32[16,256]{1,0:T(8,128)} %get-tuple-element.32) | copy-start | bytes 49156
  56.4 8.0 %copy-start.17 = (f32[16,256]{1,0:T(8,128)S(1)}, f32[16,256]{1,0:T(8,128)}, u32[]{:S(2)}) copy-start(f32[16,256]{1,0:T(8,128)} %get-tuple-element.33) | copy-start | bytes 49156
  56.4 8.7 %copy-start.16 = (f32[16,256]{1,0:T(8,128)S(1)}, f32[16,256]{1,0:T(8,128)}, u32[]{:S(2)}) copy-start(f32[16,256]{1,0:T(8,128)} %get-tuple-element.34) | copy-start | bytes 49156
  56.4 9.4 %copy-start.15 = (f32[16,256]{1,0:T(8,128)S(1)}, f32[16,256]{1,0:T(8,128)}, u32[]{:S(2)}) copy-start(f32[16,256]{1,0:T(8,128)} %get-tuple-element.35) | copy-start | bytes 49156
  56.4 10.2 %copy-start.14 = (f32[16,256]{1,0:T(8,128)S(1)}, f32[16,256]{1,0:T(8,128)}, u32[]{:S(2)}) copy-start(f32[16,256]{1,0:T(8,128)} %get-tuple-element.36) | copy-start | bytes 49156
  56.4 10.9 %copy-start.13 = (f32[16,256]{1,0:T(8,128)S(1)}, f32[16,256]{1,0:T(8,128)}, u32[]{:S(2)}) copy-start(f32[16,256]{1,0:T(8,128)} %get-tuple-element.27) | copy-start | bytes 49156
  56.4 11.7 %copy-start.3 = (f32[16,16,256]{2,1,0:T(8,128)S(1)}, f32[16,16,256]{2,1,0:T(8,128)}, u32[]{:S(2)}) copy-start(f32[16,16,256]{2,1,0:T(8,128)} %get-tuple-element.25) | copy-start | bytes 786436
  70.6 1.2 copy-start.26
  70.6 1.2 copy-start.27
  73.5 1.0 copy-start
  86.7 33.8 %all-to-all-start.1 = ((bf16[128,16,256]{0,2,1:T(8,128)(2,1)}), bf16[128,16,256]{0,2,1:T(8,128)(2,1)}, u32[]{:S(2)}, u32[]{:S(2)}) async-start(bf16[128,16,256]{0,2,1:T(8,128)(2,1)} %bitcast.78), calls=%async_computation.1 | async-start | bytes 2097152 | tf_op jit(solution)/shard_map/all_to_all | solution.py:104
  91.2 6.0 %copy-start.4 = (f32[16,256]{0,1:T(8,128)S(1)}, f32[16,256]{0,1:T(8,128)}, u32[]{:S(2)}) copy-start(f32[16,256]{0,1:T(8,128)} %copy.91) | copy-start | bytes 49156
  91.2 6.0 %copy-start.5 = (f32[16,256]{0,1:T(8,128)S(1)}, f32[16,256]{0,1:T(8,128)}, u32[]{:S(2)}) copy-start(f32[16,256]{0,1:T(8,128)} %copy.92) | copy-start | bytes 49156
  91.2 6.0 %copy-start.7 = (f32[16,256]{0,1:T(8,128)S(1)}, f32[16,256]{0,1:T(8,128)}, u32[]{:S(2)}) copy-start(f32[16,256]{0,1:T(8,128)} %copy.93) | copy-start | bytes 49156
  97.3 3.6 %copy-start.6 = (f32[16,256]{0,1:T(8,128)S(1)}, f32[16,256]{0,1:T(8,128)}, u32[]{:S(2)}) copy-start(f32[16,256]{0,1:T(8,128)} %copy.94) | copy-start | bytes 49156
  97.3 3.6 %copy-start.8 = (f32[16,256]{0,1:T(8,128)S(1)}, f32[16,256]{0,1:T(8,128)}, u32[]{:S(2)}) copy-start(f32[16,256]{0,1:T(8,128)} %copy.95) | copy-start | bytes 49156
  97.3 3.6 %copy-start.9 = (f32[16,256]{0,1:T(8,128)S(1)}, f32[16,256]{0,1:T(8,128)}, u32[]{:S(2)}) copy-start(f32[16,256]{0,1:T(8,128)} %copy.96) | copy-start | bytes 49156
  100.9 3.6 %copy-start.10 = (f32[16,256]{0,1:T(8,128)S(1)}, f32[16,256]{0,1:T(8,128)}, u32[]{:S(2)}) copy-start(f32[16,256]{0,1:T(8,128)} %copy.97) | copy-start | bytes 49156
  120.5 3.5 %copy-start.11 = (f32[1,16,256]{2,1,0:T(8,128)S(1)}, f32[1,16,256]{2,1,0:T(8,128)}, u32[]{:S(2)}) copy-start(f32[1,16,256]{2,1,0:T(8,128)} %copy.99) | copy-start | bytes 49156
  120.5 3.5 %copy-start.12 = (f32[1,16,256]{2,1,0:T(8,128)S(1)}, f32[1,16,256]{2,1,0:T(8,128)}, u32[]{:S(2)}) copy-start(f32[1,16,256]{2,1,0:T(8,128)} %copy.100) | copy-start | bytes 49156
  120.5 3.5 %copy-start.24 = (f32[16,256]{1,0:T(8,128)S(1)}, f32[16,256]{1,0:T(8,128)}, u32[]{:S(2)}) copy-start(f32[16,256]{1,0:T(8,128)} %param.7) | copy-start | bytes 49156
  120.5 43.9 %copy-start.33 = (pred[32]{0:T(512)(128)(4,1)S(1)}, pred[32]{0:T(512)(128)(4,1)}, u32[]{:S(2)}) copy-start(pred[32]{0:T(512)(128)(4,1)} %iota_compare_fusion.2) | copy-start | bytes 100
  120.5 43.9 %copy-start.34 = (f32[32]{0:T(128)S(1)}, f32[32]{0:T(128)}, u32[]{:S(2)}) copy-start(f32[32]{0:T(128)} %convert_multiply_fusion.1) | copy-start | bytes 388
  122.0 2.0 %copy-start.2 = (bf16[16,128,256]{2,1,0:T(8,128)(2,1)}, bf16[16,128,256]{2,1,0:T(8,128)(2,1)S(1)}, u32[]{:S(2)}) copy-start(bf16[16,128,256]{2,1,0:T(8,128)(2,1)S(1)} %copy.101) | copy-start | bytes 3145732
  122.0 42.7 %copy-start.32 = (f32[128]{0:T(128)S(1)}, f32[128]{0:T(128)}, u32[]{:S(2)}) copy-start(f32[128]{0:T(128)} %convert_multiply_fusion.2) | copy-start | bytes 1540
  122.0 3.1 %collective-permute-start.1 = (bf16[1,2,256]{2,1,0:T(2,128)(2,1)S(1)}, bf16[1,2,256]{2,1,0:T(2,128)(2,1)S(1)}, u32[]{:S(2)}, u32[]{:S(2)}) collective-permute-start(bf16[1,2,256]{2,1,0:T(2,128)(2,1)S(1)} %slice.145), channel_id=1, source_target_pairs={{0,16},{16,32},{32,48},{48,64},{64,80},{80,96},{96,112},{112,128},... | collective-permute-start | bytes 3080 | tf_op jit(solution)/shard_map/ppermute | solution.py:14
  170.1 3.3 %copy-start.1 = (bf16[2048,256]{1,0:T(8,128)(2,1)S(1)}, bf16[2048,256]{1,0:T(8,128)(2,1)}, u32[]{:S(2)}) copy-start(bf16[2048,256]{1,0:T(8,128)(2,1)} %copy-done) | copy-start | bytes 3145732
  170.1 3.3 %copy-start.31 = (f32[256]{0:T(256)S(1)}, f32[256]{0:T(256)}, u32[]{:S(2)}) copy-start(f32[256]{0:T(256)} %param.9) | copy-start | bytes 3076
  173.4 1.9 copy-start.28
  173.4 1.9 copy-start.29
  173.4 1.9 copy-start.30

commit v14 on v12

--- a/solution.py
+++ b/solution.py
@@ -101,10 +101,7 @@
     border = from_behind(queries[:, queries.shape[1] - (taps - 1) :, :], "seq", 1)
     queries = jnp.concatenate([border, queries], axis=1)
     gates = short_filter(keys_values, weights[1:], taps).astype(jnp.bfloat16)
-    gates = lax.optimization_barrier(gates)
-    product = lax.optimization_barrier(
-        (gates[0].astype(jnp.float32) * gates[1].astype(jnp.float32)).astype(jnp.bfloat16)
-    )
+    product = (gates[0].astype(jnp.float32) * gates[1].astype(jnp.float32)).astype(jnp.bfloat16)
     conv_out, queries = lax.optimization_barrier(
         long_part(product, decay_rate, scaled, toeplitz, skip_gain, queries)
     )

time: 192 us -> 193 us (level)
  no operation moved by 1% of the time
where the time goes in v14:
time: 193 us; the launch traced here: 192 us
  blocking collectives  61 us (32%)
  local copies, waits for them, and re-layouts  52.2 us (27%)
  starting transfers between devices  25 us (13%)
  other arithmetic  21.3 us (11%)
  waiting for transfers between devices  19.8 us (10%)
  matrix products  12.5 us (6%)
    all_gather x1, blocking collectives, long_part(): gathered = lax.all_gather(end_state, 'seq')  38 us
    all_to_all x1, blocking collectives, local(): lax.all_to_all(gated, 'chan', split_axis=0, concat_axis=1, tiled=True)  22.9 us
    all_to_all x1, waiting for transfers between devices, arrive(): lax.all_to_all(streams, 'chan', split_axis=2, concat_axis=1, tiled=True)  18.8 us
    ppermute x2, starting transfers between devices, from_behind(): return lax.ppermute(block, axis, route)  12.8 us
    add x7, other arithmetic, long_part(): starts + jnp.exp(-decay_rate * float(block * step)) * shifted(starts, step)  10.6 us
    unnamed x66, local copies, waits for them, and re-layouts  7.89 us
    all_to_all x1, starting transfers between devices, arrive(): lax.all_to_all(streams, 'chan', split_axis=2, concat_axis=1, tiled=True)  7.7 us
    dot_general x1, matrix products, long_part(): jnp.einsum('nic,knc->kic', reading, starts, precision=lax.Precision.HIGHEST)  5.44 us
  transfers between devices with their start and end apart: 4, of which 2 were waited for; matrix products, arithmetic and copies ran while one was open for 24% of the time, Pallas kernels for 0%

profile of v14, /device:TPU:1, one launch (start us, length us, event | category | flops | bytes accessed | tf_op | source)
XLA Modules:
  0.0 192.3 jit_solution(392591454232718991)
XLA Ops:
  0.0 1.6 slice-done
  1.6 3.8 %copy.104 = bf16[2,128,4096]{1,0,2:T(2,128)(2,1)} copy(bf16[2,128,4096]{2,1,0:T(8,128)(2,1)S(1)} %slice-done) | data formatting | bytes 4194304
  5.4 7.7 %all-to-all-start = ((bf16[2,128,4096]{1,0,2:T(2,128)(2,1)}), bf16[2,128,4096]{1,0,2:T(2,128)(2,1)S(1)}, u32[]{:S(2)}, u32[]{:S(2)}) async-start(bf16[2,128,4096]{1,0,2:T(2,128)(2,1)} %copy.104), calls=%async_computation | async-start | bytes 4194304 | tf_op jit(solution)/shard_map/all_to_all | solution.py:90
  14.2 1.5 constant_dynamic-slice_fusion.2
  15.6 1.4 constant_dynamic-slice_fusion.1
  18.3 1.0 exponential_multiply_fusion
  19.6 18.8 %all-to-all-done = bf16[2,128,4096]{1,0,2:T(2,128)(2,1)S(1)} async-done(((bf16[2,128,4096]{1,0,2:T(2,128)(2,1)}), bf16[2,128,4096]{1,0,2:T(2,128)(2,1)S(1)}, u32[]{:S(2)}, u32[]{:S(2)}) %all-to-all-start) | async-done | bytes 2097184 | tf_op jit(solution)/shard_map/all_to_all | solution.py:90
  38.4 1.6 copy.73
  40.0 2.9 %copy.74 = bf16[2,16,128,256]{3,2,1,0:T(8,128)(2,1)S(1)} copy(bf16[2,16,128,256]{2,3,1,0:T(8,128)(2,1)} %bitcast.69) | data formatting | bytes 4194304 | tf_op jit(solution)/shard_map/all_to_all | solution.py:90
  43.5 10.9 %collective-permute-start = (bf16[2,2,256]{2,1,0:T(2,128)(2,1)}, bf16[2,2,256]{2,1,0:T(2,128)(2,1)}, u32[]{:S(2)}, u32[]{:S(2)}) collective-permute-start(bf16[2,2,256]{2,1,0:T(2,128)(2,1)} %slice.120), channel_id=1, source_target_pairs={{0,16},{16,32},{32,48},{48,64},{64,80},{80,96},{96,112},{112,128},... | collective-permute-start | bytes 6152 | tf_op jit(solution)/shard_map/ppermute | solution.py:14
  55.0 1.3 copy.105
  56.3 0.8 copy.109
  57.1 3.5 %copy.81 = f32[16,16,256]{1,0,2:T(8,128)} copy(f32[16,16,256]{2,1,0:T(8,128)} %get-tuple-element.36) | data formatting | bytes 524288 | tf_op jit(solution)/shard_map/exp | solution.py:39
  61.3 0.8 copy.83
  64.3 0.8 copy.87
  65.1 0.8 copy.88
  65.9 2.5 %copy.94 = f32[16,16,256]{0,1,2:T(8,128)} copy(f32[16,16,256]{2,1,0:T(8,128)S(1)} %copy-done.3) | data formatting | bytes 524288 | tf_op jit(solution)/shard_map/mul | solution.py:40
  68.4 1.2 pad_maximum_fusion
  69.6 1.4 add_convert_fusion
  71.1 1.3 copy-done
  72.7 1.6 copy.78
  74.3 2.7 %convolution_bitcast_fusion = f32[128,16,256]{0,1,2:T(8,128)S(1)} fusion(bf16[128,16,256]{0,1,2:T(8,128)(2,1)S(1)} %copy.78, f32[16,16,256]{1,0,2:T(8,128)} %copy.81), kind=kOutput, calls=%fused_computation.23 | convolution fusion | flops 100663296 | bytes 3407872 | tf_op jit(solution)/shard_map/njc,kjc->knc/dot_general | solution.py:58
  77.0 2.0 %slice.131 = f32[1,16,256]{0,1,2:T(8,128)} slice(f32[128,16,256]{0,1,2:T(8,128)S(1)} %convolution_bitcast_fusion), slice={[127:128], [0:16], [0:256]} | slice | bytes 32768 | tf_op jit(solution)/shard_map/slice | solution.py:64
  79.0 2.0 %pad_slice_fusion = f32[127,16,256]{0,1,2:T(8,128)} fusion(f32[127,16,256]{0,1,2:T(8,128)S(1)} %bitcast.59), kind=kLoop, calls=%fused_computation.22 | loop fusion | bytes 4161536 | tf_op jit(solution)/shard_map/slice | solution.py:48
  81.1 4.5 %all-to-all-start.1 = ((bf16[128,16,256]{0,2,1:T(8,128)(2,1)}), bf16[128,16,256]{0,2,1:T(8,128)(2,1)}, u32[]{:S(2)}, u32[]{:S(2)}) async-start(bf16[128,16,256]{0,2,1:T(8,128)(2,1)} %bitcast.73), calls=%async_computation.1 | async-start | bytes 2097152 | tf_op jit(solution)/shard_map/all_to_all | solution.py:99
  85.6 3.1 %multiply_add_fusion.6 = f32[128,16,256]{0,1,2:T(8,128)S(1)} fusion(f32[127,16,256]{0,1,2:T(8,128)} %pad_slice_fusion, f32[127,16,256]{0,1,2:T(8,128)S(1)} %bitcast.60, f32[16,256]{0,1:T(8,128)} %copy.82), kind=kLoop, calls=%fused_computation.20 | loop fusion | flops 1048576 | bytes 6275072 | tf_op jit(solution)/shard_map/add | solution.py:62
  88.7 1.3 multiply_add_fusion.5
  90.0 1.3 multiply_add_fusion.4
  91.2 1.3 multiply_add_fusion.3
  92.5 1.3 multiply_add_fusion.2
  93.8 1.3 multiply_add_fusion.1
  95.1 1.3 multiply_add_fusion
  96.3 2.0 %slice.130 = f32[1,16,256]{0,1,2:T(8,128)} slice(f32[128,16,256]{0,1,2:T(8,128)S(1)} %multiply_add_fusion), slice={[127:128], [0:16], [0:256]} | slice | bytes 32768 | tf_op jit(solution)/shard_map/slice | solution.py:64
  98.4 3.1 %copy.90 = f32[1,16,256]{2,1,0:T(8,128)} copy(f32[1,16,256]{0,1,2:T(8,128)} %slice.130) | data formatting | bytes 32768 | tf_op jit(solution)/shard_map/slice | solution.py:64
  101.5 3.1 %copy.91 = f32[1,16,256]{2,1,0:T(8,128)} copy(f32[1,16,256]{0,1,2:T(8,128)} %slice.131) | data formatting | bytes 32768 | tf_op jit(solution)/shard_map/slice | solution.py:64
  104.6 2.5 %copy.79 = f32[16,16,256]{1,0,2:T(8,128)} copy(f32[16,16,256]{2,1,0:T(8,128)S(1)} %fusion.14) | data formatting | bytes 524288 | tf_op jit(solution)/shard_map/optimization_barrier | solution.py:98
  107.1 4.1 %fusion.17 = f32[256,128,16]{1,2,0:T(8,128)} fusion(bf16[128,16,256]{0,1,2:T(8,128)(2,1)S(1)} %copy.78, f32[16,16,256]{1,0,2:T(8,128)} %copy.79), kind=kOutput, calls=%fused_computation.61 | convolution fusion | flops 100663296 | bytes 3407872 | tf_op jit(solution)/shard_map/ijc,kjc->kic/dot_general | solution.py:74
  111.2 1.5 copy.92
  112.8 1.9 collective-permute-start.1
  114.8 1.1 collective-permute-done.1
  115.8 1.5 pad_maximum_fusion.1
  117.3 38.0 %all-gather = f32[512,256]{1,0:T(8,128)S(1)} all-gather(f32[16,256]{1,0:T(8,128)S(1)} %bitcast_add_fusion), channel_id=2, replica_groups=mesh['seq'=32,'chan'=16] {'seq'}, dimensions={0}, use_global_device_ids=true | all-gather | bytes 540672 | tf_op jit(solution)/shard_map/all_gather | solution.py:67
  155.7 5.4 %add_bitcast_fusion = f32[128,16,256]{0,1,2:T(8,128)} fusion(f32[256,128,16]{1,2,0:T(8,128)} %fusion.17, f32[16,16,256]{0,1,2:T(8,128)} %copy.94, f32[128,16,256]{0,1,2:T(8,128)S(1)} %multiply_add_fusion, f32[16,256]{0,1:T(8,128)S(1)} %copy.93, f32[128]{0:T(128)S(1)} %copy-done.28, f32[16,256]{0,1:T(8,128)S(1)} %copy.89), kind=kOutput, calls=%fused_computation.8 | convolution fusion | flops 102760448 | bytes 6586880 | tf_op jit(solution)/shard_map/nic,knc->kic/dot_general | solution.py:77
  161.1 3.4 %copy.95 = f32[128,16,256]{2,1,0:T(8,128)} copy(f32[128,16,256]{0,1,2:T(8,128)} %add_bitcast_fusion) | data formatting | bytes 4194304 | tf_op jit(solution)/shard_map/add | solution.py:78
  164.5 2.0 %fusion.2 = bf16[2048,256]{1,0:T(8,128)(2,1)S(1)} fusion(f32[128,16,256]{2,1,0:T(8,128)} %copy.95, f32[256]{0:T(256)S(1)} %copy-done.27, bf16[2,2048,256]{2,1,0:T(8,128)(2,1)S(1)} %copy-done.1), kind=kLoop, calls=%fused_computation.6 | loop fusion | flops 4194304 | bytes 5243904 | tf_op jit(solution)/shard_map/convert_element_type | solution.py:79
  166.5 0.9 fusion
  167.4 22.9 %all_to_all.53 = bf16[16,128,256]{2,1,0:T(8,128)(2,1)S(1)} all-to-all(bf16[16,128,256]{2,1,0:T(8,128)(2,1)S(1)} %bitcast.76), channel_id=1, replica_groups=mesh['seq'=32,'chan'=16] {'chan'}, dimensions={0} | all-to-all | bytes 2097152 | tf_op jit(solution)/shard_map/all_to_all | solution.py:110
  191.0 1.3 copy.97
  (87 shorter events, 8.3 us)
Async XLA Ops:
  0.0 1.6 slice-start
  5.4 12.3 %copy-start.19 = (f32[16,256]{1,0:T(8,128)S(1)}, f32[16,256]{1,0:T(8,128)}, u32[]{:S(2)}) copy-start(f32[16,256]{1,0:T(8,128)} %param.7) | copy-start | bytes 49156
  5.4 12.3 %copy-start.21 = (f32[16,256]{1,0:T(8,128)S(1)}, f32[16,256]{1,0:T(8,128)}, u32[]{:S(2)}) copy-start(f32[16,256]{1,0:T(8,128)} %param.8) | copy-start | bytes 49156
  5.4 33.0 %all-to-all-start = ((bf16[2,128,4096]{1,0,2:T(2,128)(2,1)}), bf16[2,128,4096]{1,0,2:T(2,128)(2,1)S(1)}, u32[]{:S(2)}, u32[]{:S(2)}) async-start(bf16[2,128,4096]{1,0,2:T(2,128)(2,1)} %copy.104), calls=%async_computation | async-start | bytes 4194304 | tf_op jit(solution)/shard_map/all_to_all | solution.py:90
  42.9 12.1 %slice-start.1 = ((bf16[3,128,4096]{2,1,0:T(8,128)(2,1)}), bf16[1,128,4096]{2,1,0:T(8,128)(2,1)S(1)}, s32[]{:S(2)}) async-start(bf16[3,128,4096]{2,1,0:T(8,128)(2,1)} %param.5), calls=%async_computation.4 | async-start | bytes 2097152 | tf_op jit(solution)/shard_map/slice | solution.py:98
  43.5 24.9 %collective-permute-start = (bf16[2,2,256]{2,1,0:T(2,128)(2,1)}, bf16[2,2,256]{2,1,0:T(2,128)(2,1)}, u32[]{:S(2)}, u32[]{:S(2)}) collective-permute-start(bf16[2,2,256]{2,1,0:T(2,128)(2,1)} %slice.120), channel_id=1, source_target_pairs={{0,16},{16,32},{32,48},{48,64},{64,80},{80,96},{96,112},{112,128},... | collective-permute-start | bytes 6152 | tf_op jit(solution)/shard_map/ppermute | solution.py:14
  56.3 4.3 %copy-start.18 = (f32[16,256]{1,0:T(8,128)S(1)}, f32[16,256]{1,0:T(8,128)}, u32[]{:S(2)}) copy-start(f32[16,256]{1,0:T(8,128)} %get-tuple-element.28) | copy-start | bytes 49156
  56.3 5.0 %copy-start.17 = (f32[16,256]{1,0:T(8,128)S(1)}, f32[16,256]{1,0:T(8,128)}, u32[]{:S(2)}) copy-start(f32[16,256]{1,0:T(8,128)} %get-tuple-element.29) | copy-start | bytes 49156
  56.3 5.8 %copy-start.16 = (f32[16,256]{1,0:T(8,128)S(1)}, f32[16,256]{1,0:T(8,128)}, u32[]{:S(2)}) copy-start(f32[16,256]{1,0:T(8,128)} %get-tuple-element.30) | copy-start | bytes 49156
  56.3 6.5 %copy-start.15 = (f32[16,256]{1,0:T(8,128)S(1)}, f32[16,256]{1,0:T(8,128)}, u32[]{:S(2)}) copy-start(f32[16,256]{1,0:T(8,128)} %get-tuple-element.31) | copy-start | bytes 49156
  56.3 7.3 %copy-start.14 = (f32[16,256]{1,0:T(8,128)S(1)}, f32[16,256]{1,0:T(8,128)}, u32[]{:S(2)}) copy-start(f32[16,256]{1,0:T(8,128)} %get-tuple-element.32) | copy-start | bytes 49156
  56.3 8.0 %copy-start.13 = (f32[16,256]{1,0:T(8,128)S(1)}, f32[16,256]{1,0:T(8,128)}, u32[]{:S(2)}) copy-start(f32[16,256]{1,0:T(8,128)} %get-tuple-element.33) | copy-start | bytes 49156
  56.3 8.8 %copy-start.12 = (f32[16,256]{1,0:T(8,128)S(1)}, f32[16,256]{1,0:T(8,128)}, u32[]{:S(2)}) copy-start(f32[16,256]{1,0:T(8,128)} %get-tuple-element.27) | copy-start | bytes 49156
  56.3 9.5 %copy-start.3 = (f32[16,16,256]{2,1,0:T(8,128)S(1)}, f32[16,16,256]{2,1,0:T(8,128)}, u32[]{:S(2)}) copy-start(f32[16,16,256]{2,1,0:T(8,128)} %get-tuple-element.25) | copy-start | bytes 786436
  68.4 1.2 copy-start.22
  68.4 1.2 copy-start.23
  71.0 1.3 copy-start
  81.1 30.2 %all-to-all-start.1 = ((bf16[128,16,256]{0,2,1:T(8,128)(2,1)}), bf16[128,16,256]{0,2,1:T(8,128)(2,1)}, u32[]{:S(2)}, u32[]{:S(2)}) async-start(bf16[128,16,256]{0,2,1:T(8,128)(2,1)} %bitcast.73), calls=%async_computation.1 | async-start | bytes 2097152 | tf_op jit(solution)/shard_map/all_to_all | solution.py:99
  85.6 3.1 %copy-start.9 = (f32[16,256]{0,1:T(8,128)S(1)}, f32[16,256]{0,1:T(8,128)}, u32[]{:S(2)}) copy-start(f32[16,256]{0,1:T(8,128)} %copy.83) | copy-start | bytes 49156
  88.7 1.3 copy-start.8
  90.0 1.3 copy-start.7
  91.2 1.3 copy-start.6
  92.5 1.3 copy-start.4
  93.8 1.3 copy-start.5
  111.2 3.5 %copy-start.10 = (f32[1,16,256]{2,1,0:T(8,128)S(1)}, f32[1,16,256]{2,1,0:T(8,128)}, u32[]{:S(2)}) copy-start(f32[1,16,256]{2,1,0:T(8,128)} %copy.90) | copy-start | bytes 49156
  111.2 3.5 %copy-start.11 = (f32[1,16,256]{2,1,0:T(8,128)S(1)}, f32[1,16,256]{2,1,0:T(8,128)}, u32[]{:S(2)}) copy-start(f32[1,16,256]{2,1,0:T(8,128)} %copy.91) | copy-start | bytes 49156
  111.2 3.5 %copy-start.20 = (f32[16,256]{1,0:T(8,128)S(1)}, f32[16,256]{1,0:T(8,128)}, u32[]{:S(2)}) copy-start(f32[16,256]{1,0:T(8,128)} %param.7) | copy-start | bytes 49156
  111.2 44.2 %copy-start.29 = (pred[32]{0:T(512)(128)(4,1)S(1)}, pred[32]{0:T(512)(128)(4,1)}, u32[]{:S(2)}) copy-start(pred[32]{0:T(512)(128)(4,1)} %iota_compare_fusion.2) | copy-start | bytes 100
  111.2 44.1 %copy-start.30 = (f32[32]{0:T(128)S(1)}, f32[32]{0:T(128)}, u32[]{:S(2)}) copy-start(f32[32]{0:T(128)} %convert_multiply_fusion.2) | copy-start | bytes 388
  112.7 2.0 %copy-start.2 = (bf16[16,128,256]{2,1,0:T(8,128)(2,1)}, bf16[16,128,256]{2,1,0:T(8,128)(2,1)S(1)}, u32[]{:S(2)}) copy-start(bf16[16,128,256]{2,1,0:T(8,128)(2,1)S(1)} %copy.92) | copy-start | bytes 3145732
  112.8 42.9 %copy-start.28 = (f32[128]{0:T(128)S(1)}, f32[128]{0:T(128)}, u32[]{:S(2)}) copy-start(f32[128]{0:T(128)} %convert_multiply_fusion.3) | copy-start | bytes 1540
  112.8 3.1 %collective-permute-start.1 = (bf16[1,2,256]{2,1,0:T(2,128)(2,1)S(1)}, bf16[1,2,256]{2,1,0:T(2,128)(2,1)S(1)}, u32[]{:S(2)}, u32[]{:S(2)}) collective-permute-start(bf16[1,2,256]{2,1,0:T(2,128)(2,1)S(1)} %slice.132), channel_id=1, source_target_pairs={{0,16},{16,32},{32,48},{48,64},{64,80},{80,96},{96,112},{112,128},... | collective-permute-start | bytes 3080 | tf_op jit(solution)/shard_map/ppermute | solution.py:14
  161.1 3.4 %copy-start.1 = (bf16[2,2048,256]{2,1,0:T(8,128)(2,1)S(1)}, bf16[2,2048,256]{2,1,0:T(8,128)(2,1)}, u32[]{:S(2)}) copy-start(bf16[2,2048,256]{2,1,0:T(8,128)(2,1)} %copy-done) | copy-start | bytes 6291460
  161.1 3.4 %copy-start.27 = (f32[256]{0:T(256)S(1)}, f32[256]{0:T(256)}, u32[]{:S(2)}) copy-start(f32[256]{0:T(256)} %param.9) | copy-start | bytes 3076
  164.5 2.0 %copy-start.24 = (f32[1,1,256]{2,1,0:T(1,128)S(1)}, f32[1,1,256]{2,1,0:T(1,128)}, u32[]{:S(2)}) copy-start(f32[1,1,256]{2,1,0:T(1,128)} %get-tuple-element.19) | copy-start | bytes 3076
  164.5 2.0 %copy-start.25 = (f32[1,1,256]{2,1,0:T(1,128)S(1)}, f32[1,1,256]{2,1,0:T(1,128)}, u32[]{:S(2)}) copy-start(f32[1,1,256]{2,1,0:T(1,128)} %get-tuple-element.20) | copy-start | bytes 3076
  164.5 2.0 %copy-start.26 = (f32[1,1,256]{2,1,0:T(1,128)S(1)}, f32[1,1,256]{2,1,0:T(1,128)}, u32[]{:S(2)}) copy-start(f32[1,1,256]{2,1,0:T(1,128)} %get-tuple-element.21) | copy-start | bytes 3076
